TPU v7x, 256 devices: a whole 4x4x8 slice. The times are simulated.
256 devices in a mesh: band: 16 (over y, x), slab: 16 (over z, core).
Axes of the slice: x: 4, y: 4, z: 8, core: 2. Of those that a mesh axis runs over, the one named last changes fastest.
Arguments:
- orbitals: bfloat16 [32, 16777216], P('band', 'slab'), may hold values from -6 to 6
- projectors: bfloat16 [16, 16, 512, 18, 128], P('slab', 'band'), may hold values from -0.5 to 0.5
- piece_block: int32 [16, 16, 512], P('slab', 'band'), may hold values from 0 to 511
- piece_atom: int32 [16, 16, 512], P('slab', 'band'), may hold values from -1 to 1151, as said below
- coupling: float32 [6144, 324], P('slab'), may hold values from -0.6 to 0.6
Outputs:
- applied: bfloat16 [32, 16777216], P('band', 'slab')
Inputs may be any that keep to these rules, and one draw needn't show every extreme that they name: `piece_atom`: each entry is -1 (no atom) or side * 384 + slot with side in 0, 1, 2 and slot < 384: the atom in that slot of the slab side - 1 places away along the slab axis, cyclically. Slabs hold different numbers of atoms and of pieces with an atom.
All inputs are finite; a program needn't handle non-finite values.
Results may differ from a plain program's by a relative error of at most 0.0049.
Values may be sent and summed in bfloat16 or wider, within the bound.
No kernel may reach another device: no remote copies, remote signals or barrier semaphores. Data moves between devices by JAX's collectives and lax.ppermute only.
A program may use at most 128 MiB of HBM per device.

v0:
```python
import jax
import jax.numpy as jnp
from jax import lax
from jax.sharding import PartitionSpec as P

PROJ = 18
BLOCK = 128


def extended(cells, sides, width):
    for axis, dim in sides:
        count = lax.axis_size(axis)
        head = lax.slice_in_dim(cells, 0, width, axis=dim)
        tail = lax.slice_in_dim(cells, cells.shape[dim] - width, cells.shape[dim], axis=dim)
        cells = jnp.concatenate(
            [
                lax.ppermute(tail, axis, [(i, (i + 1) % count) for i in range(count)]),
                cells,
                lax.ppermute(head, axis, [((i + 1) % count, i) for i in range(count)]),
            ],
            axis=dim,
        )
    return cells


def fold_rim(padded):
    return padded[0] + padded[2] + padded[4]


def body(orbitals, projectors, piece_block, piece_atom, coupling):
    slab_waves = lax.all_to_all(orbitals, "band", split_axis=1, concat_axis=0, tiled=True)
    band_count = slab_waves.shape[0]
    blocks = slab_waves.reshape(band_count, -1, BLOCK)
    block_count = blocks.shape[1]
    proj_local = projectors[0, 0]
    index_block = piece_block[0, 0]
    index_atom = piece_atom[0, 0]
    pieces = index_block.shape[0]
    slot_count = coupling.shape[0]
    is_live = index_atom >= 0
    picked = jnp.take(blocks, index_block, axis=1)
    projected = jnp.einsum("pjk,npk->pjn", proj_local, picked, preferred_element_type=jnp.float32)
    target = jnp.where(is_live, index_atom, 3 * slot_count)
    partial_value = jax.ops.segment_sum(
        projected.reshape(pieces, -1), target, num_segments=3 * slot_count + 1
    )
    partial_value = partial_value[: 3 * slot_count].reshape(3, slot_count, -1)
    summed = lax.psum(partial_value, "band")
    summed = fold_rim(extended(summed, (("slab", 0),), 1))[None]
    own_total = summed[0]
    share_rows = own_total.shape[0]
    matrices = coupling.reshape(share_rows, PROJ, PROJ)
    dressed = jnp.einsum(
        "aij,ajn->ain",
        matrices,
        own_total.reshape(share_rows, PROJ, band_count),
        precision=lax.Precision.HIGHEST,
    ).astype(jnp.bfloat16)
    beside_all = extended(dressed[None], (("slab", 0),), 1)
    flat_rows = beside_all.reshape(-1, PROJ, band_count)
    chosen = jnp.take(flat_rows, jnp.where(is_live, index_atom, 0), axis=0)
    chosen = jnp.where(is_live[:, None, None], chosen, jnp.zeros((), jnp.bfloat16))
    spread = jnp.einsum("pjk,pjn->npk", proj_local, chosen, preferred_element_type=jnp.float32)
    result = jnp.zeros((band_count, block_count, BLOCK), jnp.float32).at[:, index_block].add(spread)
    result = result.reshape(band_count, -1).astype(jnp.bfloat16)
    return lax.all_to_all(result, "band", split_axis=0, concat_axis=1, tiled=True)


def solution(mesh):
    placed = (
        P("band", "slab"),
        P("slab", "band", None, None, None),
        P("slab", "band", None),
        P("slab", "band", None),
        P("slab", None),
    )
    return jax.shard_map(
        body, mesh=mesh, in_specs=placed, out_specs=P("band", "slab"), check_vma=False
    )
```

profile of v0, /device:TPU:96, one launch (start us, length us, event | category | flops | bytes accessed | tf_op | source)
XLA Modules:
  0.0 465.9 jit_solution(6507110387990564066)
XLA Ops:
  6.5 0.0 copy-start
  6.5 0.0 copy-start.3
  6.5 0.0 copy-start.2
  6.5 7.2 %all-to-all-start = ((bf16[2,16,65536]{2,0,1:T(2,128)(2,1)}), bf16[2,16,65536]{2,0,1:T(2,128)(2,1)}, u32[]{:S(2)}, u32[]{:S(2)}) async-start(bf16[2,16,65536]{2,0,1:T(2,128)(2,1)} %bitcast.41), calls=%async_computation | async-start | bytes 8388608 | tf_op jit(solution)/shard_map/all_to_all | solution.py:31
  13.8 0.0 all-reduce.2.cloned.1.call-start
  13.8 0.0 copy-done.3
  13.9 0.0 copy-done.2
  13.9 63.2 %all-to-all-done = bf16[2,16,65536]{2,0,1:T(2,128)(2,1)} async-done(((bf16[2,16,65536]{2,0,1:T(2,128)(2,1)}), bf16[2,16,65536]{2,0,1:T(2,128)(2,1)}, u32[]{:S(2)}, u32[]{:S(2)}) %all-to-all-start) | async-done | bytes 4194336 | tf_op jit(solution)/shard_map/all_to_all | solution.py:31
  77.0 11.4 %reshape.116 = bf16[32,512,128]{2,1,0:T(8,128)(2,1)} reshape(bf16[16,2,65536]{2,1,0:T(2,128)(2,1)} %bitcast.7) | data formatting | bytes 8388608 | tf_op jit(solution)/shard_map/reshape | solution.py:33
  88.5 6.8 %copy.103 = bf16[32,512,128]{2,0,1:T(8,128)(2,1)} copy(bf16[32,512,128]{2,1,0:T(8,128)(2,1)} %reshape.116) | data formatting | bytes 8388608 | tf_op jit(solution)/shard_map/reshape | solution.py:33
  95.3 5.4 %gather_fusion = bf16[512,32,128]{2,1,0:T(8,128)(2,1)} fusion(bf16[32,512,128]{2,0,1:T(8,128)(2,1)} %copy.103, s32[1024]{0:T(1024)S(1)} %pad_clamp_fusion.1), kind=kCustom, calls=%fused_computation | custom fusion | bytes 8390656 | tf_op jit(solution)/shard_map/jit(_take)/gather | solution.py:41
  100.7 0.0 copy-done
  100.7 10.9 %fusion.11 = f32[512,18,32]{2,1,0:T(8,128)} fusion(bf16[512,18,128]{2,0,1:T(8,128)(2,1)S(1)} %bitcast.35, bf16[512,32,128]{2,1,0:T(8,128)(2,1)} %gather_fusion, pred[512]{0:T(512)(128)(4,1)S(1)} %compare_and_fusion), kind=kOutput, calls=%fused_computation.16 | convolution fusion | flops 77594624 | bytes 7733760 | tf_op jit(solution)/shard_map/pjk,npk->pjn/dot_general | solution.py:42
  111.6 4.5 copy.105
  116.1 1.5 copy.106
  117.6 6.4 %scatter_custom_fusion = f32[1153,576]{1,0:T(8,128)} fusion(s32[512]{0:T(512)S(1)} %bitcast.48, f32[512,576]{1,0:T(8,128)} %copy.106, f32[]{:T(128)} %constant.12.clone.1), kind=kCustom, calls=%fused_computation.21 | custom fusion | flops 294912 | bytes 2657024 | tf_op jit(solution)/shard_map/scatter-add | solution.py:44
  123.9 3.6 slice.20
  127.6 4.6 copy.107
  132.1 0.0 copy-start.1
  132.1 0.0 all-reduce.2.cloned.1.call-update
  132.2 102.6 %all-reduce.2.cloned.1.call-done = f32[3,384,576]{1,2,0:T(8,128)} async-done(((f32[3,384,576]{1,2,0:T(8,128)}), f32[3,384,576]{1,2,0:T(8,128)}) %all-reduce.2.cloned.1.call-update) | async-done | bytes 2654224 | tf_op jit(solution)/shard_map/psum | solution.py:48
  234.7 2.8 fusion.25
  237.5 0.0 collective-permute-start
  237.5 1.7 collective-permute-start.1
  239.2 0.0 copy-done.1
  239.3 0.1 reshape.119
  239.3 3.3 copy.109
  242.7 7.6 %collective-permute-done = f32[1,384,576]{1,2,0:T(8,128)} collective-permute-done((f32[1,384,576]{1,2,0:T(8,128)}, f32[1,384,576]{1,2,0:T(8,128)}, u32[]{:S(2)}, u32[]{:S(2)}) %collective-permute-start) | collective-permute-done | bytes 884768 | tf_op jit(solution)/shard_map/ppermute | solution.py:17
  250.3 0.0 collective-permute-done.1
  250.3 1.8 fusion.21
  252.1 3.4 copy.108
  255.5 11.2 %convert_bitcast_fusion = bf16[1,384,18,32]{3,2,1,0:T(8,128)(2,1)} fusion(f32[384,18,32]{2,1,0:T(8,128)} %copy.108, f32[384,18,18]{2,1,0:T(8,128)} %copy.109), kind=kOutput, calls=%fused_computation.17 | convolution fusion | flops 47996928 | bytes 1824768 | tf_op jit(solution)/shard_map/aij,ajn->ain/dot_general | solution.py:53
  266.7 2.9 copy.110
  269.6 4.1 collective-permute-start.2
  273.7 0.0 collective-permute-start.3
  273.8 3.7 collective-permute-done.2
  277.5 3.6 copy.112
  281.1 0.0 collective-permute-done.3
  281.1 2.6 copy.113
  283.7 6.9 %pad_maximum_fusion = bf16[3,384,18,32]{3,2,1,0:T(8,128)(2,1)} fusion(bf16[1,384,18,32]{3,2,1,0:T(8,128)(2,1)} %copy.113, bf16[1,384,18,32]{3,2,1,0:T(8,128)(2,1)} %convert_bitcast_fusion, bf16[1,384,18,32]{3,2,1,0:T(8,128)(2,1)} %copy.112), kind=kLoop, calls=%fused_computation.4 | loop fusion | flops 1327104 | bytes 2654208 | tf_op jit(solution)/shard_map/concatenate | solution.py:15
  290.5 6.0 %gather_fusion.1 = bf16[512,18,32]{2,1,0:T(8,128)(2,1)} fusion(bf16[1152,18,32]{2,1,0:T(8,128)(2,1)} %bitcast.38, s32[1024]{0:T(1024)S(1)} %pad_clamp_fusion), kind=kCustom, calls=%fused_computation.1 | custom fusion | bytes 1181696 | tf_op jit(solution)/shard_map/jit(_take)/gather | solution.py:61
  296.5 13.1 %fusion.4 = f32[512,32,128]{2,1,0:T(8,128)} fusion(bf16[512,18,128]{2,0,1:T(8,128)(2,1)S(1)} %bitcast.36, bf16[512,18,32]{2,1,0:T(8,128)(2,1)} %gather_fusion.1, pred[512]{0:T(512)(128)(4,1)S(1)} %get-tuple-element.8, pred[512]{0:T(512)(128)(4,1)S(1)} %get-tuple-element.7), kind=kOutput, calls=%fused_computation.9 | convolution fusion | flops 76087296 | bytes 11338752 | tf_op jit(solution)/shard_map/pjk,pjn->npk/dot_general | solution.py:63
  309.6 4.3 broadcast_in_dim.47
  313.9 67.4 %scatter_fusion = f32[32,512,128]{2,0,1:T(8,128)} fusion(f32[32,512,128]{2,0,1:T(8,128)} %broadcast_in_dim.47, s32[512]{0:T(512)S(1)} %bitcast.44, f32[512,32,128]{2,1,0:T(8,128)} %fusion.4), kind=kCustom, calls=%fused_computation.3 | custom fusion | flops 2097152 | bytes 25167872 | tf_op jit(solution)/shard_map/scatter-add | solution.py:64
  381.3 4.4 convert_element_type.15
  385.7 3.6 copy.117
  389.3 10.4 %convert_element_type.16 = bf16[16,2,65536]{2,1,0:T(2,128)(2,1)} reshape(bf16[32,512,128]{2,1,0:T(8,128)(2,1)} %copy.117) | data formatting | bytes 8388608 | tf_op jit(solution)/shard_map/convert_element_type | solution.py:65
  399.7 57.3 %all_to_all.32 = bf16[16,2,65536]{2,1,0:T(2,128)(2,1)S(1)} all-to-all(bf16[16,2,65536]{2,1,0:T(2,128)(2,1)} %convert_element_type.16), channel_id=1, replica_groups=mesh['band'=16,'slab'=16] {'band'}, dimensions={0} | all-to-all | bytes 8388608 | tf_op jit(solution)/shard_map/all_to_all | solution.py:66
  457.0 2.0 copy.128
  (6 shorter events, 0.0 us)
Async XLA Ops:
  6.5 94.2 %copy-start = (bf16[1,1,512,18,128]{4,2,3,1,0:T(8,128)(2,1)S(1)}, bf16[1,1,512,18,128]{4,2,3,1,0:T(8,128)(2,1)}, u32[]{:S(2)}) copy-start(bf16[1,1,512,18,128]{4,2,3,1,0:T(8,128)(2,1)} %param.6) | copy-start | bytes 7077892
  6.5 7.3 %copy-start.3 = (s32[1,1,512]{2,1,0:T(1,128)S(1)}, s32[1,1,512]{2,1,0:T(1,128)}, u32[]{:S(2)}) copy-start(s32[1,1,512]{2,1,0:T(1,128)} %param.7) | copy-start | bytes 6148
  6.5 7.3 %copy-start.2 = (s32[1,1,512]{2,1,0:T(1,128)S(1)}, s32[1,1,512]{2,1,0:T(1,128)}, u32[]{:S(2)}) copy-start(s32[1,1,512]{2,1,0:T(1,128)} %param.8) | copy-start | bytes 6148
  6.5 70.5 %all-to-all-start = ((bf16[2,16,65536]{2,0,1:T(2,128)(2,1)}), bf16[2,16,65536]{2,0,1:T(2,128)(2,1)}, u32[]{:S(2)}, u32[]{:S(2)}) async-start(bf16[2,16,65536]{2,0,1:T(2,128)(2,1)} %bitcast.41), calls=%async_computation | async-start | bytes 8388608 | tf_op jit(solution)/shard_map/all_to_all | solution.py:31
  13.8 221.0 %all-reduce.2.cloned.1.call-start = ((), (), s32[]{:S(2)}) async-start(), calls=%async_computation.2 | async-start | bytes 5308416 | tf_op jit(solution)/shard_map/psum | solution.py:48
  132.1 107.1 %copy-start.1 = (f32[384,324]{0,1:T(8,128)S(1)}, f32[384,324]{0,1:T(8,128)}, u32[]{:S(2)}) copy-start(f32[384,324]{0,1:T(8,128)} %param.9) | copy-start | bytes 1492996
  237.5 12.8 %collective-permute-start = (f32[1,384,576]{1,2,0:T(8,128)}, f32[1,384,576]{1,2,0:T(8,128)}, u32[]{:S(2)}, u32[]{:S(2)}) collective-permute-start(f32[1,384,576]{1,2,0:T(8,128)} %get-tuple-element.5), channel_id=1, source_target_pairs={{0,1},{1,2},{2,3},{3,4},{4,5},{5,6},{6,7},{7,8},{8,9},{9,10},{10,1... | collective-permute-start | bytes 2654216 | tf_op jit(solution)/shard_map/ppermute | solution.py:17
  237.5 12.8 %collective-permute-start.1 = (f32[1,384,576]{1,2,0:T(8,128)}, f32[1,384,576]{1,2,0:T(8,128)}, u32[]{:S(2)}, u32[]{:S(2)}) collective-permute-start(f32[1,384,576]{1,2,0:T(8,128)} %get-tuple-element.6), channel_id=1, source_target_pairs={{1,0},{2,1},{3,2},{4,3},{5,4},{6,5},{7,6},{8,7},{9,8},{10,9},{11,1... | collective-permute-start | bytes 2654216 | tf_op jit(solution)/shard_map/ppermute | solution.py:19
  269.6 7.8 %collective-permute-start.2 = (bf16[1,384,18,32]{1,3,2,0:T(8,128)(2,1)S(1)}, bf16[1,384,18,32]{1,3,2,0:T(8,128)(2,1)}, u32[]{:S(2)}, u32[]{:S(2)}) collective-permute-start(bf16[1,384,18,32]{1,3,2,0:T(8,128)(2,1)S(1)} %copy.110), channel_id=1, source_target_pairs={{0,1},{1,2},{2,3},{3,4},{4,5},{5,6},{6,7},{7,8},{8,9},{9,10},{10,1... | collective-permute-start | bytes 1327112 | tf_op jit(solution)/shard_map/ppermute | solution.py:17
  273.7 7.4 %collective-permute-start.3 = (bf16[1,384,18,32]{1,3,2,0:T(8,128)(2,1)S(1)}, bf16[1,384,18,32]{1,3,2,0:T(8,128)(2,1)S(1)}, u32[]{:S(2)}, u32[]{:S(2)}) collective-permute-start(bf16[1,384,18,32]{1,3,2,0:T(8,128)(2,1)S(1)} %copy.110), channel_id=1, source_target_pairs={{1,0},{2,1},{3,2},{4,3},{5,4},{6,5},{7,6},{8,7},{9,8},{10,9},{11,1... | collective-permute-start | bytes 1327112 | tf_op jit(solution)/shard_map/ppermute | solution.py:19
Sparse Core Ops, SparseCore 0:
  132.3 102.4 all-reduce.1
where the time goes:
time: 468 us; the launch traced here: 466 us
  waiting for transfers between devices  177 us (38%)
  other arithmetic  86.9 us (19%)
  local copies, waits for them, and re-layouts  82.8 us (18%)
  blocking collectives  57.3 us (12%)
  matrix products  35.1 us (8%)
  between operations  13.5 us (3%)
  starting transfers between devices  13.1 us (3%)
    psum x1, waiting for transfers between devices, body(): summed = lax.psum(partial_value, 'band')  103 us
    scatter-add x1, other arithmetic, body(): jnp.zeros((band_count, block_count, BLOCK), jnp.float32).at[:, index_block]  67.4 us
    all_to_all x1, waiting for transfers between devices, body(): lax.all_to_all(orbitals, 'band', split_axis=1, concat_axis=0, tiled=True)  63.2 us
    all_to_all x1, blocking collectives, body(): lax.all_to_all(result, 'band', split_axis=0, concat_axis=1, tiled=True)  57.3 us
    reshape x2, local copies, waits for them, and re-layouts, body(): blocks = slab_waves.reshape(band_count, -1, BLOCK)  18.2 us
    convert_element_type x2, local copies, waits for them, and re-layouts, body(): result = result.reshape(band_count, -1).astype(jnp.bfloat16)  14 us
    dot_general x1, matrix products, body(): jnp.einsum('pjk,pjn->npk', proj_local, chosen, preferred_element_type=jnp...  13.1 us
    ppermute x2, waiting for transfers between devices, extended(): lax.ppermute(tail, axis, [(i, (i + 1) % count) for i in range(count)])  11.3 us
  transfers between devices with their start and end apart: 6, of which 4 were waited for; matrix products, arithmetic and copies ran while one was open for 2% of the time, Pallas kernels for 0%

commit v1 on v0

v1 whole, which is shorter than its diff:
```python
import jax
import jax.numpy as jnp
from jax import lax
from jax.experimental import pallas as pl
from jax.experimental.pallas import tpu as pltpu
from jax.sharding import PartitionSpec as P

PROJ = 18
BLOCK = 128


def shift(cells, axis, step):
    count = lax.axis_size(axis)
    return lax.ppermute(cells, axis, [(i, (i + step) % count) for i in range(count)])


def _scatter_body(blk_ref, spread_ref, out_ref, acc_ref):
    bands = out_ref.shape[0]
    blocks = out_ref.shape[1]
    acc_ref[...] = jnp.zeros(acc_ref.shape, jnp.float32)

    def step(p, carry):
        row = pl.multiple_of(blk_ref[p] * bands, bands)
        acc_ref[pl.ds(row, bands), :] += spread_ref[p]
        return carry

    lax.fori_loop(0, spread_ref.shape[0], step, 0, unroll=2)
    def emit(n, carry):
        out_ref[n] = acc_ref[pl.ds(n, blocks, stride=bands), :].astype(out_ref.dtype)
        return carry

    lax.fori_loop(0, bands, emit, 0)


def scatter_blocks(index_block, spread, block_count):
    pieces, bands, width = spread.shape
    return pl.pallas_call(
        _scatter_body,
        out_shape=jax.ShapeDtypeStruct((bands, block_count, width), jnp.bfloat16),
        in_specs=[
            pl.BlockSpec(memory_space=pltpu.SMEM),
            pl.BlockSpec(memory_space=pltpu.VMEM),
        ],
        out_specs=pl.BlockSpec(memory_space=pltpu.VMEM),
        scratch_shapes=[pltpu.VMEM((block_count * bands, width), jnp.float32)],
        compiler_params=pltpu.CompilerParams(vmem_limit_bytes=48 * 1024 * 1024),
    )(index_block, spread)


def body(orbitals, projectors, piece_block, piece_atom, coupling):
    slab_waves = lax.all_to_all(orbitals, "band", split_axis=1, concat_axis=0, tiled=True)
    band_count = slab_waves.shape[0]
    blocks = slab_waves.reshape(band_count, -1, BLOCK)
    block_count = blocks.shape[1]
    proj_local = projectors[0, 0]
    index_block = piece_block[0, 0]
    index_atom = piece_atom[0, 0]
    pieces = index_block.shape[0]
    slot_count = coupling.shape[0]
    is_live = index_atom >= 0
    picked = jnp.take(blocks, index_block, axis=1)
    projected = jnp.einsum("pjk,npk->pjn", proj_local, picked, preferred_element_type=jnp.float32)
    target = jnp.where(is_live, index_atom, 3 * slot_count)
    partial_value = jax.ops.segment_sum(
        projected.reshape(pieces, -1), target, num_segments=3 * slot_count + 1
    )
    partial_value = partial_value[: 3 * slot_count].reshape(3, slot_count, -1)
    own_total = (
        partial_value[1]
        + shift(partial_value[0], "slab", -1)
        + shift(partial_value[2], "slab", 1)
    )
    own_total = lax.psum(own_total, "band")
    matrices = coupling.reshape(slot_count, PROJ, PROJ)
    dressed = jnp.einsum(
        "aij,ajn->ain",
        matrices,
        own_total.reshape(slot_count, PROJ, band_count),
        precision=lax.Precision.HIGHEST,
    ).astype(jnp.bfloat16)
    flat_rows = jnp.concatenate(
        [shift(dressed, "slab", 1), dressed, shift(dressed, "slab", -1)], axis=0
    )
    chosen = jnp.take(flat_rows, jnp.where(is_live, index_atom, 0), axis=0)
    chosen = jnp.where(is_live[:, None, None], chosen, jnp.zeros((), jnp.bfloat16))
    spread = jnp.einsum("pjk,pjn->pnk", proj_local, chosen, preferred_element_type=jnp.float32)
    result = scatter_blocks(index_block, spread, block_count)
    result = result.reshape(band_count, -1)
    return lax.all_to_all(result, "band", split_axis=0, concat_axis=1, tiled=True)


def solution(mesh):
    placed = (
        P("band", "slab"),
        P("slab", "band", None, None, None),
        P("slab", "band", None),
        P("slab", "band", None),
        P("slab", None),
    )
    return jax.shard_map(
        body, mesh=mesh, in_specs=placed, out_specs=P("band", "slab"), check_vma=False
    )
```

time: 468 us -> 421 us (0.90)
  other arithmetic: 86.9 us -> 18.2 us
  waiting for transfers between devices: 177 us -> 195 us
  Pallas kernels: 0 us -> 15.4 us
  local copies, waits for them, and re-layouts: 82.8 us -> 76.4 us
    scatter-add x1 -> x0, other arithmetic: 67.4 us -> none  [body(): jnp.zeros((band_count, block_count, BLOCK), jnp.float32).at[:, index_block]]
    pallas_call x0 -> x1, Pallas kernels: none -> 15.4 us  [scatter_blocks(): pl.pallas_call(_scatter_body, out_shape=jax.ShapeDtypeStruct((bands, bloc...]
    psum x1, waiting for transfers between devices: 103 us -> 115 us  [body(): own_total = lax.psum(own_total, 'band')]
    convert_element_type x2 -> x1, local copies, waits for them, and re-layouts: 14 us -> 2.94 us  [body(): dressed = jnp.einsum('aij,ajn->ain', matrices, own_total.reshape(slot_cou...]
    all_to_all x0 -> x1, local copies, waits for them, and re-layouts: none -> 10.4 us  [body(): lax.all_to_all(result, 'band', split_axis=0, concat_axis=1, tiled=True)]
    broadcast_in_dim x2 -> x0, local copies, waits for them, and re-layouts: 7.24 us -> none  [the longest x1 4.31 us: body(): jnp.zeros((band_count, block_count, BLOCK), jnp.float32).at[:, index_block]]
    ppermute x4, waiting for transfers between devices: 11.4 us -> 17.1 us  [shift(): lax.ppermute(cells, axis, [(i, (i + step) % count) for i in range(count)])]
  transfers between devices with their start and end apart: 6 -> 6, of which waited for: 4 -> 5; matrix products, arithmetic and copies ran while one was open for 2% -> 3% of each run, Pallas kernels for 0% -> 0%
where the time goes in v1:
time: 421 us; the launch traced here: 420 us
  waiting for transfers between devices  195 us (46%)
  local copies, waits for them, and re-layouts  76.4 us (18%)
  blocking collectives  56.7 us (13%)
  matrix products  35.2 us (8%)
  other arithmetic  18.2 us (4%)
  Pallas kernels  15.4 us (4%)
  between operations  13.5 us (3%)
  starting transfers between devices  9.52 us (2%)
    psum x1, waiting for transfers between devices, body(): own_total = lax.psum(own_total, 'band')  115 us
    all_to_all x1, waiting for transfers between devices, body(): lax.all_to_all(orbitals, 'band', split_axis=1, concat_axis=0, tiled=True)  63.2 us
    all_to_all x1, blocking collectives, body(): lax.all_to_all(result, 'band', split_axis=0, concat_axis=1, tiled=True)  56.7 us
    reshape x2, local copies, waits for them, and re-layouts, body(): blocks = slab_waves.reshape(band_count, -1, BLOCK)  18.2 us
    ppermute x4, waiting for transfers between devices, shift(): lax.ppermute(cells, axis, [(i, (i + step) % count) for i in range(count)])  17.1 us
    pallas_call x1, Pallas kernels, scatter_blocks(): pl.pallas_call(_scatter_body, out_shape=jax.ShapeDtypeStruct((bands, bloc...  15.4 us
    dot_general x1, matrix products, body(): jnp.einsum('pjk,pjn->pnk', proj_local, chosen, preferred_element_type=jnp...  13.1 us
    dot_general x1, matrix products, body(): jnp.einsum('aij,ajn->ain', matrices, own_total.reshape(slot_count, PROJ,...  11.2 us
  transfers between devices with their start and end apart: 6, of which 5 were waited for; matrix products, arithmetic and copies ran while one was open for 3% of the time, Pallas kernels for 0%

profile of v1, /device:TPU:96, one launch (start us, length us, event | category | flops | bytes accessed | tf_op | source)
XLA Modules:
  0.0 419.7 jit_solution(8229614688754706125)
XLA Ops:
  6.5 0.0 copy-start
  6.5 0.0 copy-start.2
  6.5 0.0 copy-start.4
  6.5 7.2 %all-to-all-start = ((bf16[2,16,65536]{2,0,1:T(2,128)(2,1)}), bf16[2,16,65536]{2,0,1:T(2,128)(2,1)}, u32[]{:S(2)}, u32[]{:S(2)}) async-start(bf16[2,16,65536]{2,0,1:T(2,128)(2,1)} %bitcast.37), calls=%async_computation | async-start | bytes 8388608 | tf_op jit(solution)/shard_map/all_to_all | solution.py:51
  13.8 0.0 all-reduce.2.cloned.1.call-start
  13.8 0.0 copy-done.2
  13.9 0.0 copy-done.4
  13.9 63.2 %all-to-all-done = bf16[2,16,65536]{2,0,1:T(2,128)(2,1)} async-done(((bf16[2,16,65536]{2,0,1:T(2,128)(2,1)}), bf16[2,16,65536]{2,0,1:T(2,128)(2,1)}, u32[]{:S(2)}, u32[]{:S(2)}) %all-to-all-start) | async-done | bytes 4194336 | tf_op jit(solution)/shard_map/all_to_all | solution.py:51
  77.0 11.4 %reshape.114 = bf16[32,512,128]{2,1,0:T(8,128)(2,1)} reshape(bf16[16,2,65536]{2,1,0:T(2,128)(2,1)} %bitcast.5) | data formatting | bytes 8388608 | tf_op jit(solution)/shard_map/reshape | solution.py:53
  88.5 6.8 %copy.83 = bf16[32,512,128]{2,0,1:T(8,128)(2,1)} copy(bf16[32,512,128]{2,1,0:T(8,128)(2,1)} %reshape.114) | data formatting | bytes 8388608 | tf_op jit(solution)/shard_map/reshape | solution.py:53
  95.3 5.4 %gather_fusion = bf16[512,32,128]{2,1,0:T(8,128)(2,1)} fusion(bf16[32,512,128]{2,0,1:T(8,128)(2,1)} %copy.83, s32[1024]{0:T(1024)S(1)} %pad_clamp_fusion.1), kind=kCustom, calls=%fused_computation | custom fusion | bytes 8390656 | tf_op jit(solution)/shard_map/jit(_take)/gather | solution.py:61
  100.7 0.0 copy-done
  100.7 10.9 %fusion.11 = f32[512,18,32]{2,1,0:T(8,128)} fusion(bf16[512,18,128]{2,0,1:T(8,128)(2,1)S(1)} %bitcast.31, bf16[512,32,128]{2,1,0:T(8,128)(2,1)} %gather_fusion, pred[512]{0:T(512)(128)(4,1)S(1)} %compare_and_fusion), kind=kOutput, calls=%fused_computation.15 | convolution fusion | flops 77594624 | bytes 7733760 | tf_op jit(solution)/shard_map/pjk,npk->pjn/dot_general | solution.py:62
  111.7 4.5 %copy.85 = f32[512,18,32]{0,2,1:T(8,128)S(1)} copy(f32[512,18,32]{2,1,0:T(8,128)} %fusion.11) | data formatting | bytes 2359296 | tf_op jit(solution)/shard_map/pjk,npk->pjn/dot_general | solution.py:62
  116.1 1.5 copy.86
  117.6 6.4 %scatter_custom_fusion = f32[1153,576]{1,0:T(8,128)} fusion(s32[512]{0:T(512)S(1)} %bitcast.42, f32[512,576]{1,0:T(8,128)} %copy.86, f32[]{:T(128)} %constant.21.clone.1), kind=kCustom, calls=%fused_computation.20 | custom fusion | flops 294912 | bytes 2657024 | tf_op jit(solution)/shard_map/scatter-add | solution.py:64
  124.0 3.3 fusion.24
  127.2 2.4 copy.88
  129.7 0.0 collective-permute-start
  129.7 2.4 copy.89
  132.1 0.5 collective-permute-start.1
  132.6 1.2 copy.98
  133.8 6.7 %collective-permute-done = f32[384,576]{0,1:T(8,128)} collective-permute-done((f32[384,576]{0,1:T(8,128)}, f32[384,576]{0,1:T(8,128)}, u32[]{:S(2)}, u32[]{:S(2)}) %collective-permute-start) | collective-permute-done | bytes 884768 | tf_op jit(solution)/shard_map/ppermute | solution.py:14
  140.6 4.3 %collective-permute-done.1 = f32[384,576]{0,1:T(8,128)} collective-permute-done((f32[384,576]{0,1:T(8,128)}, f32[384,576]{0,1:T(8,128)}, u32[]{:S(2)}, u32[]{:S(2)}) %collective-permute-start.1) | collective-permute-done | bytes 884768 | tf_op jit(solution)/shard_map/ppermute | solution.py:14
  144.9 1.8 add_add_fusion
  146.7 3.4 copy.90
  150.2 0.0 copy-start.3
  150.2 0.0 all-reduce.2.cloned.1.call-update
  150.2 1.0 copy-done.3
  151.2 0.1 reshape.117
  151.3 3.4 copy.91
  154.6 114.6 %all-reduce.2.cloned.1.call-done = f32[384,18,32]{2,1,0:T(8,128)} async-done(((f32[384,18,32]{2,1,0:T(8,128)}), f32[384,18,32]{2,1,0:T(8,128)}) %all-reduce.2.cloned.1.call-update) | async-done | bytes 884752 | tf_op jit(solution)/shard_map/psum | solution.py:73
  269.2 11.2 %convert_bitcast_fusion = bf16[384,18,32]{2,1,0:T(8,128)(2,1)} fusion(f32[384,18,32]{2,1,0:T(8,128)} %all-reduce.2.cloned.1.call-done, f32[384,18,18]{2,1,0:T(8,128)} %copy.91), kind=kOutput, calls=%fused_computation.16 | convolution fusion | flops 47996928 | bytes 1824768 | tf_op jit(solution)/shard_map/aij,ajn->ain/dot_general | solution.py:75
  280.3 2.9 copy.92
  283.3 0.0 collective-permute-start.2
  283.3 1.7 collective-permute-start.3
  285.0 6.1 %collective-permute-done.2 = bf16[384,18,32]{0,2,1:T(8,128)(2,1)} collective-permute-done((bf16[384,18,32]{0,2,1:T(8,128)(2,1)S(1)}, bf16[384,18,32]{0,2,1:T(8,128)(2,1)}, u32[]{:S(2)}, u32[]{:S(2)}) %collective-permute-start.2) | collective-permute-done | bytes 442400 | tf_op jit(solution)/shard_map/ppermute | solution.py:14
  291.1 3.7 copy.94
  294.8 0.0 collective-permute-done.3
  294.8 2.5 copy.95
  297.3 9.9 %pad_maximum_fusion = bf16[1152,18,32]{2,1,0:T(8,128)(2,1)} fusion(bf16[384,18,32]{2,1,0:T(8,128)(2,1)} %copy.95, bf16[384,18,32]{2,1,0:T(8,128)(2,1)} %convert_bitcast_fusion, bf16[384,18,32]{2,1,0:T(8,128)(2,1)} %copy.94), kind=kLoop, calls=%fused_computation.3 | loop fusion | flops 1327104 | bytes 2654208 | tf_op jit(solution)/shard_map/concatenate | solution.py:81
  307.3 6.0 %gather_fusion.1 = bf16[512,18,32]{2,1,0:T(8,128)(2,1)} fusion(bf16[1152,18,32]{2,1,0:T(8,128)(2,1)} %pad_maximum_fusion, s32[1024]{0:T(1024)S(1)} %pad_clamp_fusion), kind=kCustom, calls=%fused_computation.1 | custom fusion | bytes 1181696 | tf_op jit(solution)/shard_map/jit(_take)/gather | solution.py:84
  313.2 13.1 %fusion.4.spread_ref = f32[512,32,128]{2,1,0:T(8,128)} fusion(bf16[512,18,128]{2,0,1:T(8,128)(2,1)S(1)} %bitcast.32, bf16[512,18,32]{2,1,0:T(8,128)(2,1)} %gather_fusion.1, pred[512]{0:T(512)(128)(4,1)S(1)} %get-tuple-element.9, pred[512]{0:T(512)(128)(4,1)S(1)} %get-tuple-element.8), kind=kOutput, calls=%fused_computation.8 | convolution fusion | flops 76087296 | bytes 11338752 | tf_op jit(solution)/shard_map/pjk,pjn->pnk/dot_general | solution.py:86
  326.3 15.4 %shard_map.55 = bf16[32,512,128]{2,1,0:T(8,128)(2,1)S(1)} custom-call(s32[512]{0:T(512)S(1)} %bitcast.34, f32[512,32,128]{2,1,0:T(8,128)} %fusion.4.spread_ref), custom_call_target="tpu_custom_call" | custom-call | tf_op jit(solution)/shard_map/pallas_call | solution.py:37
  341.7 0.0 copy-start.1
  341.7 2.0 copy-done.1
  343.8 10.4 %all_to_all.29 = bf16[16,2,65536]{2,1,0:T(2,128)(2,1)} reshape(bf16[32,512,128]{2,1,0:T(8,128)(2,1)} %copy-done.1) | data formatting | bytes 8388608 | tf_op jit(solution)/shard_map/all_to_all | solution.py:89
  354.2 56.7 %all_to_all.35 = bf16[16,2,65536]{2,1,0:T(2,128)(2,1)S(1)} all-to-all(bf16[16,2,65536]{2,1,0:T(2,128)(2,1)} %all_to_all.29), channel_id=1, replica_groups=mesh['band'=16,'slab'=16] {'band'}, dimensions={0} | all-to-all | bytes 8388608 | tf_op jit(solution)/shard_map/all_to_all | solution.py:89
  410.9 2.0 copy.107
  (6 shorter events, 0.0 us)
Async XLA Ops:
  6.5 94.2 %copy-start = (bf16[1,1,512,18,128]{4,2,3,1,0:T(8,128)(2,1)S(1)}, bf16[1,1,512,18,128]{4,2,3,1,0:T(8,128)(2,1)}, u32[]{:S(2)}) copy-start(bf16[1,1,512,18,128]{4,2,3,1,0:T(8,128)(2,1)} %param.6) | copy-start | bytes 7077892
  6.5 7.3 %copy-start.2 = (s32[1,1,512]{2,1,0:T(1,128)S(1)}, s32[1,1,512]{2,1,0:T(1,128)}, u32[]{:S(2)}) copy-start(s32[1,1,512]{2,1,0:T(1,128)} %param.7) | copy-start | bytes 6148
  6.5 7.3 %copy-start.4 = (s32[1,1,512]{2,1,0:T(1,128)S(1)}, s32[1,1,512]{2,1,0:T(1,128)}, u32[]{:S(2)}) copy-start(s32[1,1,512]{2,1,0:T(1,128)} %param.8) | copy-start | bytes 6148
  6.5 70.5 %all-to-all-start = ((bf16[2,16,65536]{2,0,1:T(2,128)(2,1)}), bf16[2,16,65536]{2,0,1:T(2,128)(2,1)}, u32[]{:S(2)}, u32[]{:S(2)}) async-start(bf16[2,16,65536]{2,0,1:T(2,128)(2,1)} %bitcast.37), calls=%async_computation | async-start | bytes 8388608 | tf_op jit(solution)/shard_map/all_to_all | solution.py:51
  13.8 255.4 %all-reduce.2.cloned.1.call-start = ((), (), s32[]{:S(2)}) async-start(), calls=%async_computation.2 | async-start | bytes 9437184 | tf_op jit(solution)/shard_map/psum | solution.py:73
  129.7 10.9 %collective-permute-start = (f32[384,576]{0,1:T(8,128)}, f32[384,576]{0,1:T(8,128)}, u32[]{:S(2)}, u32[]{:S(2)}) collective-permute-start(f32[384,576]{0,1:T(8,128)} %copy.88), channel_id=1, source_target_pairs={{0,15},{1,0},{2,1},{3,2},{4,3},{5,4},{6,5},{7,6},{8,7},{9,8},{10,9... | collective-permute-start | bytes 2654216 | tf_op jit(solution)/shard_map/ppermute | solution.py:14
  132.1 12.8 %collective-permute-start.1 = (f32[384,576]{0,1:T(8,128)}, f32[384,576]{0,1:T(8,128)}, u32[]{:S(2)}, u32[]{:S(2)}) collective-permute-start(f32[384,576]{0,1:T(8,128)} %copy.89), channel_id=1, source_target_pairs={{0,1},{1,2},{2,3},{3,4},{4,5},{5,6},{6,7},{7,8},{8,9},{9,10},{10,1... | collective-permute-start | bytes 2654216 | tf_op jit(solution)/shard_map/ppermute | solution.py:14
  150.2 1.0 copy-start.3
  283.3 7.8 %collective-permute-start.2 = (bf16[384,18,32]{0,2,1:T(8,128)(2,1)S(1)}, bf16[384,18,32]{0,2,1:T(8,128)(2,1)}, u32[]{:S(2)}, u32[]{:S(2)}) collective-permute-start(bf16[384,18,32]{0,2,1:T(8,128)(2,1)S(1)} %copy.92), channel_id=1, source_target_pairs={{0,1},{1,2},{2,3},{3,4},{4,5},{5,6},{6,7},{7,8},{8,9},{9,10},{10,1... | collective-permute-start | bytes 1327112 | tf_op jit(solution)/shard_map/ppermute | solution.py:14
  283.3 11.5 %collective-permute-start.3 = (bf16[384,18,32]{0,2,1:T(8,128)(2,1)S(1)}, bf16[384,18,32]{0,2,1:T(8,128)(2,1)S(1)}, u32[]{:S(2)}, u32[]{:S(2)}) collective-permute-start(bf16[384,18,32]{0,2,1:T(8,128)(2,1)S(1)} %copy.92), channel_id=1, source_target_pairs={{0,15},{1,0},{2,1},{3,2},{4,3},{5,4},{6,5},{7,6},{8,7},{9,8},{10,9... | collective-permute-start | bytes 1327112 | tf_op jit(solution)/shard_map/ppermute | solution.py:14
  341.7 2.0 copy-start.1
Sparse Core Ops, SparseCore 0:
  150.3 118.8 all-reduce.1

commit v2 on v1

--- a/solution.py
+++ b/solution.py
@@ -70,17 +70,24 @@
         + shift(partial_value[0], "slab", -1)
         + shift(partial_value[2], "slab", 1)
     )
-    own_total = lax.psum(own_total, "band")
-    matrices = coupling.reshape(slot_count, PROJ, PROJ)
+    band_size = lax.axis_size("band")
+    share = slot_count // band_size
+    arrived = lax.all_to_all(
+        own_total.reshape(band_size, share, -1), "band", split_axis=0, concat_axis=0, tiled=True
+    )
+    mine = arrived.sum(axis=0)
+    first = lax.axis_index("band") * share
+    matrices = lax.dynamic_slice_in_dim(coupling, first, share, axis=0).reshape(share, PROJ, PROJ)
     dressed = jnp.einsum(
         "aij,ajn->ain",
         matrices,
-        own_total.reshape(slot_count, PROJ, band_count),
+        mine.reshape(share, PROJ, band_count),
         precision=lax.Precision.HIGHEST,
     ).astype(jnp.bfloat16)
-    flat_rows = jnp.concatenate(
-        [shift(dressed, "slab", 1), dressed, shift(dressed, "slab", -1)], axis=0
-    )
+    sides = jnp.stack([shift(dressed, "slab", 1), dressed, shift(dressed, "slab", -1)])
+    spread_out = jnp.broadcast_to(sides[None], (band_size,) + sides.shape)
+    every = lax.all_to_all(spread_out, "band", split_axis=0, concat_axis=0, tiled=True)
+    flat_rows = jnp.swapaxes(every, 0, 1).reshape(3 * slot_count, PROJ, band_count)
     chosen = jnp.take(flat_rows, jnp.where(is_live, index_atom, 0), axis=0)
     chosen = jnp.where(is_live[:, None, None], chosen, jnp.zeros((), jnp.bfloat16))
     spread = jnp.einsum("pjk,pjn->pnk", proj_local, chosen, preferred_element_type=jnp.float32)

time: 421 us -> 334 us (0.79)
  waiting for transfers between devices: 195 us -> 115 us
  between operations: 13.5 us -> 0.2 us
  local copies, waits for them, and re-layouts: 76.4 us -> 89.3 us
  starting transfers between devices: 9.52 us -> 21.3 us
  matrix products: 35.2 us -> 25.6 us
  other arithmetic: 18.2 us -> 9.44 us
    psum x1 -> x0, waiting for transfers between devices: 115 us -> none  [body(): own_total = lax.psum(own_total, 'band')]
    all_to_all x0 -> x2, waiting for transfers between devices: none -> 37.8 us  [the longest x1 24.4 us: body(): lax.all_to_all(spread_out, 'band', split_axis=0, concat_axis=0, tiled=True)]
    unnamed x12 -> x14, local copies, waits for them, and re-layouts: 6.27 us -> 22.6 us
    concatenate x1 -> x0, other arithmetic: 9.94 us -> none  [body(): jnp.concatenate([shift(dressed, 'slab', 1), dressed, shift(dressed, 'slab...]
    dot_general x1, matrix products: 11.2 us -> 1.57 us  [body(): jnp.einsum('aij,ajn->ain', matrices, mine.reshape(share, PROJ, band_count...]
    all_to_all x0 -> x2, starting transfers between devices: none -> 9.3 us  [the longest x1 4.67 us: body(): lax.all_to_all(own_total.reshape(band_size, share, -1), 'band', split_axi...]
  transfers between devices with their start and end apart: 6 -> 7, of which waited for: 5 -> 6; matrix products, arithmetic and copies ran while one was open for 3% -> 1% of each run, Pallas kernels for 0% -> 0%
where the time goes in v2:
time: 334 us; the launch traced here: 332 us
  waiting for transfers between devices  115 us (34%)
  local copies, waits for them, and re-layouts  89.3 us (27%)
  blocking collectives  55.1 us (16%)
  matrix products  25.6 us (8%)
  starting transfers between devices  21.3 us (6%)
  Pallas kernels  15.4 us (5%)
  other arithmetic  9.44 us (3%)
    all_to_all x1, waiting for transfers between devices, body(): lax.all_to_all(orbitals, 'band', split_axis=1, concat_axis=0, tiled=True)  63.2 us
    all_to_all x1, blocking collectives, body(): lax.all_to_all(result, 'band', split_axis=0, concat_axis=1, tiled=True)  55.1 us
    all_to_all x1, waiting for transfers between devices, body(): lax.all_to_all(spread_out, 'band', split_axis=0, concat_axis=0, tiled=True)  24.4 us
    unnamed x14, local copies, waits for them, and re-layouts  22.6 us
    reshape x2, local copies, waits for them, and re-layouts, body(): blocks = slab_waves.reshape(band_count, -1, BLOCK)  18.2 us
    pallas_call x1, Pallas kernels, scatter_blocks(): pl.pallas_call(_scatter_body, out_shape=jax.ShapeDtypeStruct((bands, bloc...  15.4 us
    ppermute x4, waiting for transfers between devices, shift(): lax.ppermute(cells, axis, [(i, (i + step) % count) for i in range(count)])  14.4 us
    all_to_all x1, waiting for transfers between devices, body(): lax.all_to_all(own_total.reshape(band_size, share, -1), 'band', split_axi...  13.4 us
  transfers between devices with their start and end apart: 7, of which 6 were waited for; matrix products, arithmetic and copies ran while one was open for 1% of the time, Pallas kernels for 0%

profile of v2, /device:TPU:96, one launch (start us, length us, event | category | flops | bytes accessed | tf_op | source)
XLA Modules:
  0.0 331.7 jit_solution(18297733236083760706)
XLA Ops:
  0.0 0.0 copy-start
  0.0 0.0 copy-start.2
  0.0 0.0 copy-start.3
  0.0 7.2 %all-to-all-start = ((bf16[2,16,65536]{2,0,1:T(2,128)(2,1)}), bf16[2,16,65536]{2,0,1:T(2,128)(2,1)}, u32[]{:S(2)}, u32[]{:S(2)}) async-start(bf16[2,16,65536]{2,0,1:T(2,128)(2,1)} %bitcast.44), calls=%async_computation | async-start | bytes 8388608 | tf_op jit(solution)/shard_map/all_to_all | solution.py:51
  7.2 0.0 copy-done.2
  7.3 0.0 copy-done.3
  7.3 63.2 %all-to-all-done = bf16[2,16,65536]{2,0,1:T(2,128)(2,1)} async-done(((bf16[2,16,65536]{2,0,1:T(2,128)(2,1)}), bf16[2,16,65536]{2,0,1:T(2,128)(2,1)}, u32[]{:S(2)}, u32[]{:S(2)}) %all-to-all-start) | async-done | bytes 4194336 | tf_op jit(solution)/shard_map/all_to_all | solution.py:51
  70.5 11.4 %reshape.122 = bf16[32,512,128]{2,1,0:T(8,128)(2,1)} reshape(bf16[16,2,65536]{2,1,0:T(2,128)(2,1)} %bitcast.5) | data formatting | bytes 8388608 | tf_op jit(solution)/shard_map/reshape | solution.py:53
  81.9 6.8 %copy.31 = bf16[32,512,128]{2,0,1:T(8,128)(2,1)} copy(bf16[32,512,128]{2,1,0:T(8,128)(2,1)} %reshape.122) | data formatting | bytes 8388608 | tf_op jit(solution)/shard_map/reshape | solution.py:53
  88.8 5.4 %gather_fusion = bf16[512,32,128]{2,1,0:T(8,128)(2,1)} fusion(bf16[32,512,128]{2,0,1:T(8,128)(2,1)} %copy.31, s32[1024]{0:T(1024)S(1)} %pad_clamp_fusion.1), kind=kCustom, calls=%fused_computation | custom fusion | bytes 8390656 | tf_op jit(solution)/shard_map/jit(_take)/gather | solution.py:61
  94.2 0.0 copy-done
  94.2 10.9 %fusion.11 = f32[512,18,32]{2,1,0:T(8,128)} fusion(bf16[512,18,128]{2,0,1:T(8,128)(2,1)S(1)} %bitcast.37, bf16[512,32,128]{2,1,0:T(8,128)(2,1)} %gather_fusion, pred[512]{0:T(512)(128)(4,1)S(1)} %compare_and_fusion), kind=kOutput, calls=%fused_computation.14 | convolution fusion | flops 77594624 | bytes 7733760 | tf_op jit(solution)/shard_map/pjk,npk->pjn/dot_general | solution.py:62
  105.1 4.5 %copy.33 = f32[512,18,32]{0,2,1:T(8,128)S(1)} copy(f32[512,18,32]{2,1,0:T(8,128)} %fusion.11) | data formatting | bytes 2359296 | tf_op jit(solution)/shard_map/pjk,npk->pjn/dot_general | solution.py:62
  109.6 1.5 copy.34
  111.1 6.5 %scatter_custom_fusion = f32[1153,576]{1,0:T(8,128)} fusion(s32[512]{0:T(512)S(1)} %bitcast.52, f32[512,576]{1,0:T(8,128)} %copy.34, f32[]{:T(128)} %constant.42.clone.1), kind=kCustom, calls=%fused_computation.18 | custom fusion | flops 294912 | bytes 2657024 | tf_op jit(solution)/shard_map/scatter-add | solution.py:64
  117.6 2.6 fusion.25
  120.2 2.5 copy.37
  122.7 0.0 collective-permute-start.1
  122.7 1.2 copy.35
  124.0 1.7 collective-permute-start
  125.7 9.8 %collective-permute-done.1 = f32[384,576]{0,1:T(8,128)} collective-permute-done((f32[384,576]{0,1:T(8,128)}, f32[384,576]{0,1:T(8,128)}, u32[]{:S(2)}, u32[]{:S(2)}) %collective-permute-start.1) | collective-permute-done | bytes 884768 | tf_op jit(solution)/shard_map/ppermute | solution.py:14
  135.5 1.5 copy.38
  137.0 0.0 collective-permute-done
  137.0 2.5 copy.36
  139.5 2.7 fusion.21
  142.1 4.7 %all-to-all-start.1 = ((f32[16,24,576]{2,1,0:T(8,128)}), f32[16,24,576]{2,1,0:T(8,128)S(1)}, u32[]{:S(2)}, u32[]{:S(2)}) async-start(f32[16,24,576]{2,1,0:T(8,128)} %bitcast.45), calls=%async_computation.1 | async-start | bytes 1966080 | tf_op jit(solution)/shard_map/all_to_all | solution.py:75
  146.8 1.1 constant_dynamic-slice_fusion
  147.9 0.1 copy.29
  148.0 0.9 reshape.121
  148.9 13.4 %all-to-all-done.1 = f32[16,24,576]{2,1,0:T(8,128)S(1)} async-done(((f32[16,24,576]{2,1,0:T(8,128)}), f32[16,24,576]{2,1,0:T(8,128)S(1)}, u32[]{:S(2)}, u32[]{:S(2)}) %all-to-all-start.1) | async-done | bytes 884768 | tf_op jit(solution)/shard_map/all_to_all | solution.py:75
  162.3 0.1 reduce_sum.9
  162.3 0.1 reshape.125
  162.4 1.6 convolution_convert_fusion
  164.0 3.0 collective-permute-start.3
  167.1 0.0 collective-permute-start.2
  167.1 2.7 collective-permute-done.3
  169.7 1.9 collective-permute-done.2
  171.6 0.1 pad_maximum_fusion
  171.8 3.0 broadcast_bitcast_fusion
  174.8 0.0 copy-start.4
  174.8 8.1 %reshape.153 = bf16[16,2,20736]{2,1,0:T(2,128)(2,1)} reshape(bf16[16,3,18,24,32]{4,3,2,1,0:T(8,128)(2,1)} %broadcast_bitcast_fusion) | data formatting | bytes 2654208
  182.9 4.6 %all-to-all-start.2 = ((bf16[16,2,20736]{2,1,0:T(2,128)(2,1)}), bf16[16,2,20736]{2,1,0:T(2,128)(2,1)}, u32[]{:S(2)}, u32[]{:S(2)}) async-start(bf16[16,2,20736]{2,1,0:T(2,128)(2,1)} %reshape.153), calls=%async_computation.2 | async-start | bytes 2654208 | tf_op jit(solution)/shard_map/all_to_all | solution.py:89
  187.6 0.0 copy-done.4
  187.6 24.4 %all-to-all-done.2 = bf16[16,2,20736]{2,1,0:T(2,128)(2,1)} async-done(((bf16[16,2,20736]{2,1,0:T(2,128)(2,1)}), bf16[16,2,20736]{2,1,0:T(2,128)(2,1)}, u32[]{:S(2)}, u32[]{:S(2)}) %all-to-all-start.2) | async-done | bytes 1327136 | tf_op jit(solution)/shard_map/all_to_all | solution.py:89
  212.0 7.4 %reshape.154 = bf16[16,3,18,24,32]{4,3,2,1,0:T(8,128)(2,1)} reshape(bf16[16,2,20736]{2,1,0:T(2,128)(2,1)} %all-to-all-done.2) | data formatting | bytes 2654208
  219.4 3.4 %bitcast_bitcast_fusion = bf16[3,16,24,18,32]{4,2,3,0,1:T(8,128)(2,1)S(1)} fusion(bf16[16,3,18,24,32]{4,3,2,1,0:T(8,128)(2,1)} %reshape.154), kind=kLoop, calls=%fused_computation.40 | loop fusion | bytes 2654208 | tf_op jit(solution)/shard_map/transpose | solution.py:90
  222.9 4.8 %copy.44 = bf16[3,16,24,18,32]{4,3,2,1,0:T(8,128)(2,1)} copy(bf16[3,16,24,18,32]{4,2,3,0,1:T(8,128)(2,1)S(1)} %bitcast_bitcast_fusion) | data formatting | bytes 2654208 | tf_op jit(solution)/shard_map/reshape | solution.py:90
  227.7 6.0 %gather_fusion.1 = bf16[512,18,32]{2,1,0:T(8,128)(2,1)} fusion(bf16[1152,18,32]{2,1,0:T(8,128)(2,1)} %bitcast.42, s32[1024]{0:T(1024)S(1)} %pad_clamp_fusion), kind=kCustom, calls=%fused_computation.1 | custom fusion | bytes 1181696 | tf_op jit(solution)/shard_map/jit(_take)/gather | solution.py:91
  233.6 13.1 %fusion.4.spread_ref = f32[512,32,128]{2,1,0:T(8,128)} fusion(bf16[512,18,128]{2,0,1:T(8,128)(2,1)S(1)} %bitcast.38, bf16[512,18,32]{2,1,0:T(8,128)(2,1)} %gather_fusion.1, pred[512]{0:T(512)(128)(4,1)S(1)} %get-tuple-element.8, pred[512]{0:T(512)(128)(4,1)S(1)} %get-tuple-element.7), kind=kOutput, calls=%fused_computation.7 | convolution fusion | flops 76087296 | bytes 11338752 | tf_op jit(solution)/shard_map/pjk,pjn->pnk/dot_general | solution.py:93
  246.7 15.4 %shard_map.55 = bf16[32,512,128]{2,1,0:T(8,128)(2,1)S(1)} custom-call(s32[512]{0:T(512)S(1)} %bitcast.40, f32[512,32,128]{2,1,0:T(8,128)} %fusion.4.spread_ref), custom_call_target="tpu_custom_call" | custom-call | tf_op jit(solution)/shard_map/pallas_call | solution.py:37
  262.1 0.0 copy-start.1
  262.1 2.0 copy-done.1
  264.1 10.5 %all_to_all.37 = bf16[16,2,65536]{2,1,0:T(2,128)(2,1)} reshape(bf16[32,512,128]{2,1,0:T(8,128)(2,1)} %copy-done.1) | data formatting | bytes 8388608 | tf_op jit(solution)/shard_map/all_to_all | solution.py:96
  274.6 55.1 %all_to_all.45 = bf16[16,2,65536]{2,1,0:T(2,128)(2,1)S(1)} all-to-all(bf16[16,2,65536]{2,1,0:T(2,128)(2,1)} %all_to_all.37), channel_id=1, replica_groups=mesh['band'=16,'slab'=16] {'band'}, dimensions={0} | all-to-all | bytes 8388608 | tf_op jit(solution)/shard_map/all_to_all | solution.py:96
  329.7 2.0 copy.53
  (7 shorter events, 0.1 us)
Async XLA Ops:
  0.0 94.2 %copy-start = (bf16[1,1,512,18,128]{4,2,3,1,0:T(8,128)(2,1)S(1)}, bf16[1,1,512,18,128]{4,2,3,1,0:T(8,128)(2,1)}, u32[]{:S(2)}) copy-start(bf16[1,1,512,18,128]{4,2,3,1,0:T(8,128)(2,1)} %param.6) | copy-start | bytes 7077892
  0.0 7.2 %copy-start.2 = (s32[1,1,512]{2,1,0:T(1,128)S(1)}, s32[1,1,512]{2,1,0:T(1,128)}, u32[]{:S(2)}) copy-start(s32[1,1,512]{2,1,0:T(1,128)} %param.7) | copy-start | bytes 6148
  0.0 7.3 %copy-start.3 = (s32[1,1,512]{2,1,0:T(1,128)S(1)}, s32[1,1,512]{2,1,0:T(1,128)}, u32[]{:S(2)}) copy-start(s32[1,1,512]{2,1,0:T(1,128)} %param.8) | copy-start | bytes 6148
  0.0 70.5 %all-to-all-start = ((bf16[2,16,65536]{2,0,1:T(2,128)(2,1)}), bf16[2,16,65536]{2,0,1:T(2,128)(2,1)}, u32[]{:S(2)}, u32[]{:S(2)}) async-start(bf16[2,16,65536]{2,0,1:T(2,128)(2,1)} %bitcast.44), calls=%async_computation | async-start | bytes 8388608 | tf_op jit(solution)/shard_map/all_to_all | solution.py:51
  122.7 12.8 %collective-permute-start.1 = (f32[384,576]{0,1:T(8,128)}, f32[384,576]{0,1:T(8,128)}, u32[]{:S(2)}, u32[]{:S(2)}) collective-permute-start(f32[384,576]{0,1:T(8,128)} %copy.37), channel_id=1, source_target_pairs={{0,1},{1,2},{2,3},{3,4},{4,5},{5,6},{6,7},{7,8},{8,9},{9,10},{10,1... | collective-permute-start | bytes 2654216 | tf_op jit(solution)/shard_map/ppermute | solution.py:14
  124.0 13.0 %collective-permute-start = (f32[384,576]{0,1:T(8,128)}, f32[384,576]{0,1:T(8,128)}, u32[]{:S(2)}, u32[]{:S(2)}) collective-permute-start(f32[384,576]{0,1:T(8,128)} %copy.35), channel_id=1, source_target_pairs={{0,15},{1,0},{2,1},{3,2},{4,3},{5,4},{6,5},{7,6},{8,7},{9,8},{10,9... | collective-permute-start | bytes 2654216 | tf_op jit(solution)/shard_map/ppermute | solution.py:14
  142.1 20.1 %all-to-all-start.1 = ((f32[16,24,576]{2,1,0:T(8,128)}), f32[16,24,576]{2,1,0:T(8,128)S(1)}, u32[]{:S(2)}, u32[]{:S(2)}) async-start(f32[16,24,576]{2,1,0:T(8,128)} %bitcast.45), calls=%async_computation.1 | async-start | bytes 1966080 | tf_op jit(solution)/shard_map/all_to_all | solution.py:75
  164.0 5.7 %collective-permute-start.3 = (bf16[24,18,32]{2,1,0:T(8,128)(2,1)S(1)}, bf16[24,18,32]{2,1,0:T(8,128)(2,1)S(1)}, u32[]{:S(2)}, u32[]{:S(2)}) collective-permute-start(bf16[24,18,32]{2,1,0:T(8,128)(2,1)S(1)} %convolution_convert_fusion), channel_id=1, source_target_pairs={{0,15},{1,0},{2,1},{3,2},{4,3},{5,4},{6,5},{7,6},{8,7},{9,8},{10,9... | collective-permute-start | bytes 82952 | tf_op jit(solution)/shard_map/ppermute | solution.py:14
  167.1 4.6 %collective-permute-start.2 = (bf16[24,18,32]{2,1,0:T(8,128)(2,1)S(1)}, bf16[24,18,32]{2,1,0:T(8,128)(2,1)S(1)}, u32[]{:S(2)}, u32[]{:S(2)}) collective-permute-start(bf16[24,18,32]{2,1,0:T(8,128)(2,1)S(1)} %convolution_convert_fusion), channel_id=1, source_target_pairs={{0,1},{1,2},{2,3},{3,4},{4,5},{5,6},{6,7},{7,8},{8,9},{9,10},{10,1... | collective-permute-start | bytes 82952 | tf_op jit(solution)/shard_map/ppermute | solution.py:14
  174.8 12.7 %copy-start.4 = (s32[1,1,512]{2,1,0:T(1,128)S(1)}, s32[1,1,512]{2,1,0:T(1,128)}, u32[]{:S(2)}) copy-start(s32[1,1,512]{2,1,0:T(1,128)} %param.8) | copy-start | bytes 6148
  182.9 29.1 %all-to-all-start.2 = ((bf16[16,2,20736]{2,1,0:T(2,128)(2,1)}), bf16[16,2,20736]{2,1,0:T(2,128)(2,1)}, u32[]{:S(2)}, u32[]{:S(2)}) async-start(bf16[16,2,20736]{2,1,0:T(2,128)(2,1)} %reshape.153), calls=%async_computation.2 | async-start | bytes 2654208 | tf_op jit(solution)/shard_map/all_to_all | solution.py:89
  262.1 2.0 copy-start.1

commit v3 on v2

--- a/solution.py
+++ b/solution.py
@@ -48,29 +48,37 @@
 
 
 def body(orbitals, projectors, piece_block, piece_atom, coupling):
-    slab_waves = lax.all_to_all(orbitals, "band", split_axis=1, concat_axis=0, tiled=True)
-    band_count = slab_waves.shape[0]
-    blocks = slab_waves.reshape(band_count, -1, BLOCK)
-    block_count = blocks.shape[1]
+    band_size = lax.axis_size("band")
+    local_bands = orbitals.shape[0]
+    band_count = band_size * local_bands
     proj_local = projectors[0, 0]
     index_block = piece_block[0, 0]
     index_atom = piece_atom[0, 0]
     pieces = index_block.shape[0]
     slot_count = coupling.shape[0]
     is_live = index_atom >= 0
-    picked = jnp.take(blocks, index_block, axis=1)
-    projected = jnp.einsum("pjk,npk->pjn", proj_local, picked, preferred_element_type=jnp.float32)
     target = jnp.where(is_live, index_atom, 3 * slot_count)
-    partial_value = jax.ops.segment_sum(
-        projected.reshape(pieces, -1), target, num_segments=3 * slot_count + 1
-    )
-    partial_value = partial_value[: 3 * slot_count].reshape(3, slot_count, -1)
+    halves = []
+    for c in range(local_bands):
+        got = lax.all_to_all(
+            orbitals[c].reshape(band_size, -1), "band", split_axis=0, concat_axis=0, tiled=True
+        )
+        blocks = got.reshape(band_size, -1, BLOCK)
+        block_count = blocks.shape[1]
+        picked = jnp.take(blocks, index_block, axis=1)
+        projected = jnp.einsum(
+            "pjk,npk->pjn", proj_local, picked, preferred_element_type=jnp.float32
+        )
+        summed = jax.ops.segment_sum(
+            projected.reshape(pieces, -1), target, num_segments=3 * slot_count + 1
+        )
+        halves.append(summed[: 3 * slot_count].reshape(3 * slot_count, PROJ, band_size))
+    partial_value = jnp.concatenate(halves, axis=-1).reshape(3, slot_count, -1)
     own_total = (
         partial_value[1]
         + shift(partial_value[0], "slab", -1)
         + shift(partial_value[2], "slab", 1)
     )
-    band_size = lax.axis_size("band")
     share = slot_count // band_size
     arrived = lax.all_to_all(
         own_total.reshape(band_size, share, -1), "band", split_axis=0, concat_axis=0, tiled=True
@@ -90,10 +98,20 @@
     flat_rows = jnp.swapaxes(every, 0, 1).reshape(3 * slot_count, PROJ, band_count)
     chosen = jnp.take(flat_rows, jnp.where(is_live, index_atom, 0), axis=0)
     chosen = jnp.where(is_live[:, None, None], chosen, jnp.zeros((), jnp.bfloat16))
-    spread = jnp.einsum("pjk,pjn->pnk", proj_local, chosen, preferred_element_type=jnp.float32)
-    result = scatter_blocks(index_block, spread, block_count)
-    result = result.reshape(band_count, -1)
-    return lax.all_to_all(result, "band", split_axis=0, concat_axis=1, tiled=True)
+    outs = []
+    for c in range(local_bands):
+        spread = jnp.einsum(
+            "pjk,pjn->pnk",
+            proj_local,
+            chosen[:, :, c * band_size : (c + 1) * band_size],
+            preferred_element_type=jnp.float32,
+        )
+        result = scatter_blocks(index_block, spread, block_count)
+        sent = lax.all_to_all(
+            result.reshape(band_size, -1), "band", split_axis=0, concat_axis=0, tiled=True
+        )
+        outs.append(sent.reshape(-1))
+    return jnp.stack(outs)
 
 
 def solution(mesh):

time: 334 us -> 472 us (1.41); the launches traced: 332 us -> 463 us
  other arithmetic: 9.44 us -> 119 us
  local copies, waits for them, and re-layouts: 89.3 us -> 171 us
  blocking collectives: 55.1 us -> 0 us
  waiting for transfers between devices: 115 us -> 86.7 us
  starting transfers between devices: 21.3 us -> 40.1 us
  matrix products: 25.6 us -> 32.5 us
    all_to_all x0 -> x6, other arithmetic: none -> 89.1 us  [the longest x4 59 us: body(): lax.all_to_all(orbitals[c].reshape(band_size, -1), 'band', split_axis=0,...]
    unnamed x14 -> x25, local copies, waits for them, and re-layouts: 22.6 us -> 81 us
    all_to_all x1 -> x0, blocking collectives: 55.1 us -> none  [body(): lax.all_to_all(result, 'band', split_axis=0, concat_axis=1, tiled=True)]
    all_to_all x1 -> x4, waiting for transfers between devices: 63.2 us -> 36.7 us  [the longest x2 24 us: body(): lax.all_to_all(result.reshape(band_size, -1), 'band', split_axis=0, conca...]
    all_to_all x1 -> x4, starting transfers between devices: 7.23 us -> 23.7 us  [the longest x2 12 us: body(): lax.all_to_all(result.reshape(band_size, -1), 'band', split_axis=0, conca...]
    slice x3 -> x5, local copies, waits for them, and re-layouts: 6.33 us -> 21.7 us  [the longest x4 11.8 us: body(): summed[:3 * slot_count].reshape(3 * slot_count, PROJ, band_size)]
    reshape x2, local copies, waits for them, and re-layouts: 18.2 us -> 6.54 us  [body(): blocks = got.reshape(band_size, -1, BLOCK)]
    another operation x0 -> x1, other arithmetic: none -> 10.8 us  [body(): return jnp.stack(outs)]
  transfers between devices with their start and end apart: 7 -> 10, of which waited for: 6 -> 7; matrix products, arithmetic and copies ran while one was open for 1% -> 25% of each run, Pallas kernels for 0% -> 2%
where the time goes in v3:
time: 472 us; the launch traced here: 463 us
  local copies, waits for them, and re-layouts  171 us (36%)
  other arithmetic  119 us (25%)
  waiting for transfers between devices  86.7 us (18%)
  starting transfers between devices  40.1 us (8%)
  matrix products  32.5 us (7%)
  Pallas kernels  14.3 us (3%)
    unnamed x25, local copies, waits for them, and re-layouts  81 us
    all_to_all x4, other arithmetic, body(): lax.all_to_all(orbitals[c].reshape(band_size, -1), 'band', split_axis=0,...  59 us
    all_to_all x2, other arithmetic, body(): lax.all_to_all(result.reshape(band_size, -1), 'band', split_axis=0, conca...  30.1 us
    all_to_all x2, waiting for transfers between devices, body(): lax.all_to_all(result.reshape(band_size, -1), 'band', split_axis=0, conca...  24 us
    all_to_all x1, waiting for transfers between devices, body(): lax.all_to_all(spread_out, 'band', split_axis=0, concat_axis=0, tiled=True)  22 us
    dot_general x2, matrix products, body(): jnp.einsum('pjk,npk->pjn', proj_local, picked, preferred_element_type=jnp...  20.9 us
    all_to_all x2, local copies, waits for them, and re-layouts, body(): lax.all_to_all(result.reshape(band_size, -1), 'band', split_axis=0, conca...  20 us
    ppermute x4, waiting for transfers between devices, shift(): lax.ppermute(cells, axis, [(i, (i + step) % count) for i in range(count)])  15 us
  transfers between devices with their start and end apart: 10, of which 7 were waited for; matrix products, arithmetic and copies ran while one was open for 25% of the time, Pallas kernels for 2%

profile of v3, /device:TPU:96, one launch (start us, length us, event | category | flops | bytes accessed | tf_op | source)
XLA Modules:
  0.0 463.4 jit_solution(14066729745636023718)
XLA Ops:
  0.0 10.0 %fusion.33 = (bf16[1,1048576]{1,0:T(2,128)(2,1)}, bf16[1,1048576]{1,0:T(2,128)(2,1)}) fusion(bf16[2,1048576]{1,0:T(2,128)(2,1)} %param.7), kind=kLoop, calls=%fused_computation.57 | loop fusion | bytes 8388608 | tf_op jit(solution)/shard_map/slice | solution.py:64
  10.5 15.0 %reduce.2 = bf16[16,65536]{1,0:T(8,128)(2,1)} reduce(bf16[16,1,65536]{2,1,0:T(2,128)(2,1)} %bitcast.66, bf16[]{:T(256)} %broadcast.107), dimensions={1}, to_apply=%bitcast.4.reduce_sub_computation | reduce | bytes 4194306 | tf_op jit(solution)/shard_map/all_to_all | solution.py:63
  25.5 4.0 reshape.177
  29.5 7.1 %all-to-all-start = ((bf16[16,2,32768]{2,1,0:T(2,128)(2,1)}), bf16[16,2,32768]{2,1,0:T(2,128)(2,1)}, u32[]{:S(2)}, u32[]{:S(2)}) async-start(bf16[16,2,32768]{2,1,0:T(2,128)(2,1)} %reshape.177), calls=%async_computation | async-start | bytes 4194304 | tf_op jit(solution)/shard_map/all_to_all | solution.py:63
  36.6 15.1 %reduce.3 = bf16[16,65536]{1,0:T(8,128)(2,1)} reduce(bf16[16,1,65536]{2,1,0:T(2,128)(2,1)} %bitcast.65, bf16[]{:T(256)} %broadcast.107), dimensions={1}, to_apply=%bitcast.10.reduce_sub_computation | reduce | bytes 4194306 | tf_op jit(solution)/shard_map/all_to_all | solution.py:63
  51.7 4.0 reshape.175
  55.7 12.7 %all-to-all-done = bf16[16,2,32768]{2,1,0:T(2,128)(2,1)} async-done(((bf16[16,2,32768]{2,1,0:T(2,128)(2,1)}), bf16[16,2,32768]{2,1,0:T(2,128)(2,1)}, u32[]{:S(2)}, u32[]{:S(2)}) %all-to-all-start) | async-done | bytes 2097184 | tf_op jit(solution)/shard_map/all_to_all | solution.py:63
  68.4 4.6 all-to-all-start.1
  73.2 10.4 %reshape.178 = bf16[16,1,65536]{2,1,0:T(2,128)(2,1)} reshape(bf16[16,2,32768]{2,1,0:T(2,128)(2,1)} %all-to-all-done) | data formatting | bytes 4194304
  83.6 14.4 %reduce = bf16[16,65536]{1,0:T(8,128)(2,1)} reduce(bf16[16,1,65536]{2,1,0:T(2,128)(2,1)} %reshape.178, bf16[]{:T(256)} %constant.47), dimensions={1}, to_apply=%all_to_all.31.reduce_sub_computation | reduce | bytes 4194306 | tf_op jit(solution)/shard_map/all_to_all | solution.py:63
  98.0 3.3 copy_bitcast_fusion.1
  101.3 4.0 gather_fusion.1
  105.2 10.5 %fusion.8 = f32[512,18,16]{1,2,0:T(8,128)} fusion(bf16[512,18,128]{2,0,1:T(8,128)(2,1)S(1)} %bitcast.55, bf16[512,16,128]{2,1,0:T(8,128)(2,1)} %gather_fusion.1, pred[512]{0:T(512)(128)(4,1)S(1)} %compare_and_fusion), kind=kOutput, calls=%fused_computation.19 | convolution fusion | flops 38797312 | bytes 5046784 | tf_op jit(solution)/shard_map/pjk,npk->pjn/dot_general | solution.py:69
  115.7 3.0 copy.41
  119.9 5.8 %scatter_custom_fusion = f32[1153,288]{1,0:T(8,128)} fusion(s32[512]{0:T(512)S(1)} %bitcast.79, f32[512,288]{1,0:T(8,128)} %copy.42, f32[]{:T(128)} %constant.25.clone.1), kind=kCustom, calls=%fused_computation.36 | custom fusion | flops 147456 | bytes 1328768 | tf_op jit(solution)/shard_map/scatter-add | solution.py:72
  125.7 2.8 slice.45
  128.5 3.1 copy.43
  131.6 10.4 %reshape.176 = bf16[16,1,65536]{2,1,0:T(2,128)(2,1)} reshape(bf16[16,2,32768]{2,1,0:T(2,128)(2,1)} %all-to-all-done.1) | data formatting | bytes 4194304
  142.1 14.4 %reduce.1 = bf16[16,65536]{1,0:T(8,128)(2,1)} reduce(bf16[16,1,65536]{2,1,0:T(2,128)(2,1)} %reshape.176, bf16[]{:T(256)} %constant.47), dimensions={1}, to_apply=%all_to_all.33.reduce_sub_computation | reduce | bytes 4194306 | tf_op jit(solution)/shard_map/all_to_all | solution.py:63
  156.5 3.3 copy_bitcast_fusion
  159.8 4.0 gather_fusion.2
  163.8 10.5 %fusion.11 = f32[512,18,16]{1,2,0:T(8,128)} fusion(bf16[512,18,128]{2,0,1:T(8,128)(2,1)S(1)} %bitcast.58, bf16[512,16,128]{2,1,0:T(8,128)(2,1)} %gather_fusion.2, pred[512]{0:T(512)(128)(4,1)S(1)} %compare_and_fusion), kind=kOutput, calls=%fused_computation.20 | convolution fusion | flops 38797312 | bytes 5046784 | tf_op jit(solution)/shard_map/pjk,npk->pjn/dot_general | solution.py:69
  174.2 3.0 copy.46
  178.4 5.6 %scatter_custom_fusion.1 = f32[1153,288]{1,0:T(8,128)} fusion(s32[512]{0:T(512)S(1)} %bitcast.80, f32[512,288]{1,0:T(8,128)} %copy.47, f32[]{:T(128)} %constant.25.clone.1), kind=kCustom, calls=%fused_computation.34 | custom fusion | flops 147456 | bytes 1328768 | tf_op jit(solution)/shard_map/scatter-add | solution.py:72
  184.0 2.8 slice.46
  186.8 3.0 copy.48
  189.9 1.9 fusion.29
  191.8 1.7 collective-permute-start
  193.6 10.7 %collective-permute-done.1 = f32[384,576]{0,1:T(8,128)S(1)} collective-permute-done((f32[384,576]{0,1:T(8,128)S(1)}, f32[384,576]{0,1:T(8,128)S(1)}, u32[]{:S(2)}, u32[]{:S(2)}) %collective-permute-start.1) | collective-permute-done | bytes 884768 | tf_op jit(solution)/shard_map/ppermute | solution.py:14
  205.8 7.2 %all-to-all-start.2 = ((f32[16,24,576]{2,1,0:T(8,128)}), f32[16,24,576]{2,1,0:T(8,128)S(1)}, u32[]{:S(2)}, u32[]{:S(2)}) async-start(f32[16,24,576]{2,1,0:T(8,128)} %bitcast.18), calls=%async_computation.2 | async-start | bytes 1966080 | tf_op jit(solution)/shard_map/all_to_all | solution.py:83
  215.1 13.1 %all-to-all-done.2 = f32[16,24,576]{2,1,0:T(8,128)S(1)} async-done(((f32[16,24,576]{2,1,0:T(8,128)}), f32[16,24,576]{2,1,0:T(8,128)S(1)}, u32[]{:S(2)}, u32[]{:S(2)}) %all-to-all-start.2) | async-done | bytes 884768 | tf_op jit(solution)/shard_map/all_to_all | solution.py:83
  228.3 1.6 convolution_convert_fusion
  229.9 2.6 collective-permute-start.3
  232.8 2.4 collective-permute-done.3
  235.2 1.9 collective-permute-done.2
  237.3 3.0 broadcast_bitcast_fusion
  240.3 8.1 %reshape.179 = bf16[16,2,20736]{2,1,0:T(2,128)(2,1)} reshape(bf16[16,3,18,24,32]{4,3,2,1,0:T(8,128)(2,1)} %broadcast_bitcast_fusion) | data formatting | bytes 2654208
  248.4 4.5 all-to-all-start.3
  252.9 22.0 %all-to-all-done.3 = bf16[16,2,20736]{2,1,0:T(2,128)(2,1)} async-done(((bf16[16,2,20736]{2,1,0:T(2,128)(2,1)}), bf16[16,2,20736]{2,1,0:T(2,128)(2,1)}, u32[]{:S(2)}, u32[]{:S(2)}) %all-to-all-start.3) | async-done | bytes 1327136 | tf_op jit(solution)/shard_map/all_to_all | solution.py:97
  274.9 7.4 %reshape.180 = bf16[16,3,18,24,32]{4,3,2,1,0:T(8,128)(2,1)} reshape(bf16[16,2,20736]{2,1,0:T(2,128)(2,1)} %all-to-all-done.3) | data formatting | bytes 2654208
  282.3 3.4 bitcast_bitcast_fusion
  285.7 4.8 %copy.58 = bf16[3,16,24,18,32]{4,3,2,1,0:T(8,128)(2,1)} copy(bf16[3,16,24,18,32]{4,2,3,0,1:T(8,128)(2,1)S(1)} %bitcast_bitcast_fusion) | data formatting | bytes 2654208 | tf_op jit(solution)/shard_map/reshape | solution.py:98
  290.5 6.0 %gather_fusion = bf16[512,18,32]{2,1,0:T(8,128)(2,1)} fusion(bf16[1152,18,32]{2,1,0:T(8,128)(2,1)} %bitcast.67, s32[1024]{0:T(1024)S(1)} %pad_clamp_fusion), kind=kCustom, calls=%fused_computation.2 | custom fusion | bytes 1181696 | tf_op jit(solution)/shard_map/jit(_take)/gather | solution.py:99
  296.5 6.8 %copy.53 = bf16[512,18,32]{1,2,0:T(8,128)(2,1)} copy(bf16[512,18,32]{2,1,0:T(8,128)(2,1)} %gather_fusion) | data formatting | bytes 1179648 | tf_op jit(solution)/shard_map/jit(_take)/gather | solution.py:99
  303.3 5.0 %select_select_fusion = bf16[512,18,32]{1,2,0:T(8,128)(2,1)S(1)} fusion(bf16[512,18,32]{1,2,0:T(8,128)(2,1)} %copy.53, pred[512]{0:T(512)(128)(4,1)S(1)} %get-tuple-element.12, pred[512]{0:T(512)(128)(4,1)S(1)} %get-tuple-element.11), kind=kLoop, calls=%fused_computation.6 | loop fusion | flops 589824 | bytes 1180672 | tf_op jit(solution)/shard_map/jit(_where)/select_n | solution.py:100
  308.4 2.0 copy-done.4
  310.4 4.2 fusion.2.spread_ref
  314.6 7.1 %shard_map.55 = bf16[16,512,128]{2,1,0:T(8,128)(2,1)S(1)} custom-call(s32[512]{0:T(512)S(1)} %bitcast.61, f32[512,16,128]{2,1,0:T(8,128)} %fusion.2.spread_ref), custom_call_target="tpu_custom_call" | custom-call | tf_op jit(solution)/shard_map/pallas_call | solution.py:37
  321.7 1.3 copy-done.1
  323.1 10.0 %all_to_all.40 = bf16[16,1,65536]{2,1,0:T(2,128)(2,1)} reshape(bf16[16,512,128]{2,1,0:T(8,128)(2,1)} %copy-done.1) | data formatting | bytes 4194304 | tf_op jit(solution)/shard_map/all_to_all | solution.py:110
  333.1 15.0 %reduce.5 = bf16[16,65536]{1,0:T(8,128)(2,1)} reduce(bf16[16,1,65536]{2,1,0:T(2,128)(2,1)} %all_to_all.40, bf16[]{:T(256)} %broadcast.107), dimensions={1}, to_apply=%all_to_all.40.reduce_sub_computation | reduce | bytes 4194306 | tf_op jit(solution)/shard_map/all_to_all | solution.py:110
  348.1 4.0 reshape.183
  352.1 4.7 %all-to-all-start.4 = ((bf16[16,2,32768]{2,1,0:T(2,128)(2,1)}), bf16[16,2,32768]{2,1,0:T(2,128)(2,1)}, u32[]{:S(2)}, u32[]{:S(2)}) async-start(bf16[16,2,32768]{2,1,0:T(2,128)(2,1)} %reshape.183), calls=%async_computation.4 | async-start | bytes 4194304 | tf_op jit(solution)/shard_map/all_to_all | solution.py:110
  356.8 5.8 %fusion.spread_ref = f32[512,16,128]{2,1,0:T(8,128)} fusion(bf16[512,18,128]{2,0,1:T(8,128)(2,1)S(1)} %bitcast.56, bf16[512,18,32]{1,2,0:T(8,128)(2,1)} %copy-done.4), kind=kOutput, calls=%fused_computation.7 | convolution fusion | flops 37748736 | bytes 8650752 | tf_op jit(solution)/shard_map/pjk,pjn->pnk/dot_general | solution.py:103
  362.6 7.1 %shard_map.56 = bf16[16,512,128]{2,1,0:T(8,128)(2,1)S(1)} custom-call(s32[512]{0:T(512)S(1)} %bitcast.62, f32[512,16,128]{2,1,0:T(8,128)} %fusion.spread_ref), custom_call_target="tpu_custom_call" | custom-call | tf_op jit(solution)/shard_map/pallas_call | solution.py:37
  369.7 1.3 copy-done.2
  371.1 10.0 %all_to_all.41 = bf16[16,1,65536]{2,1,0:T(2,128)(2,1)} reshape(bf16[16,512,128]{2,1,0:T(8,128)(2,1)} %copy-done.2) | data formatting | bytes 4194304 | tf_op jit(solution)/shard_map/all_to_all | solution.py:110
  381.1 15.1 %reduce.4 = bf16[16,65536]{1,0:T(8,128)(2,1)} reduce(bf16[16,1,65536]{2,1,0:T(2,128)(2,1)} %all_to_all.41, bf16[]{:T(256)} %broadcast.107), dimensions={1}, to_apply=%all_to_all.41.reduce_sub_computation | reduce | bytes 4194306 | tf_op jit(solution)/shard_map/all_to_all | solution.py:110
  396.1 4.0 reshape.181
  400.1 7.3 %all-to-all-start.5 = ((bf16[16,2,32768]{2,1,0:T(2,128)(2,1)}), bf16[16,2,32768]{2,1,0:T(2,128)(2,1)}, u32[]{:S(2)}, u32[]{:S(2)}) async-start(bf16[16,2,32768]{2,1,0:T(2,128)(2,1)} %reshape.181), calls=%async_computation.5 | async-start | bytes 4194304 | tf_op jit(solution)/shard_map/all_to_all | solution.py:110
  407.4 10.5 %reshape.184 = bf16[16,1,65536]{2,1,0:T(2,128)(2,1)} reshape(bf16[16,2,32768]{2,1,0:T(2,128)(2,1)} %all-to-all-done.4) | data formatting | bytes 4194304
  417.9 24.0 %all-to-all-done.5 = bf16[16,2,32768]{2,1,0:T(2,128)(2,1)} async-done(((bf16[16,2,32768]{2,1,0:T(2,128)(2,1)}), bf16[16,2,32768]{2,1,0:T(2,128)(2,1)}, u32[]{:S(2)}, u32[]{:S(2)}) %all-to-all-start.5) | async-done | bytes 2097184 | tf_op jit(solution)/shard_map/all_to_all | solution.py:110
  441.8 10.5 %reshape.182 = bf16[16,1,65536]{2,1,0:T(2,128)(2,1)} reshape(bf16[16,2,32768]{2,1,0:T(2,128)(2,1)} %all-to-all-done.5) | data formatting | bytes 4194304
  452.3 10.8 %pad_maximum_fusion = bf16[2,1048576]{1,0:T(2,128)(2,1)} fusion(bf16[1,1048576]{1,0:T(2,128)(2,1)} %bitcast.64, bf16[1,1048576]{1,0:T(2,128)(2,1)} %bitcast.63), kind=kLoop, calls=%fused_computation.5 | loop fusion | flops 8388608 | bytes 8388608 | tf_op jit(solution)/shard_map/stack | solution.py:114
  (34 shorter events, 7.1 us)
Async XLA Ops:
  0.0 105.2 %copy-start = (bf16[1,1,512,18,128]{4,2,3,1,0:T(8,128)(2,1)S(1)}, bf16[1,1,512,18,128]{4,2,3,1,0:T(8,128)(2,1)}, u32[]{:S(2)}) copy-start(bf16[1,1,512,18,128]{4,2,3,1,0:T(8,128)(2,1)} %param.8) | copy-start | bytes 7077892
  29.5 38.9 %all-to-all-start = ((bf16[16,2,32768]{2,1,0:T(2,128)(2,1)}), bf16[16,2,32768]{2,1,0:T(2,128)(2,1)}, u32[]{:S(2)}, u32[]{:S(2)}) async-start(bf16[16,2,32768]{2,1,0:T(2,128)(2,1)} %reshape.177), calls=%async_computation | async-start | bytes 4194304 | tf_op jit(solution)/shard_map/all_to_all | solution.py:63
  55.7 17.4 %copy-start.3 = (s32[1,1,512]{2,1,0:T(1,128)S(1)}, s32[1,1,512]{2,1,0:T(1,128)}, u32[]{:S(2)}) copy-start(s32[1,1,512]{2,1,0:T(1,128)} %param.9) | copy-start | bytes 6148
  55.7 17.4 %copy-start.5 = (s32[1,1,512]{2,1,0:T(1,128)S(1)}, s32[1,1,512]{2,1,0:T(1,128)}, u32[]{:S(2)}) copy-start(s32[1,1,512]{2,1,0:T(1,128)} %param.10) | copy-start | bytes 6148
  68.4 63.2 %all-to-all-start.1 = ((bf16[16,2,32768]{2,1,0:T(2,128)(2,1)}), bf16[16,2,32768]{2,1,0:T(2,128)(2,1)}, u32[]{:S(2)}, u32[]{:S(2)}) async-start(bf16[16,2,32768]{2,1,0:T(2,128)(2,1)} %reshape.175), calls=%async_computation.1 | async-start | bytes 4194304 | tf_op jit(solution)/shard_map/all_to_all | solution.py:63
  191.8 12.5 %collective-permute-start.1 = (f32[384,576]{0,1:T(8,128)S(1)}, f32[384,576]{0,1:T(8,128)S(1)}, u32[]{:S(2)}, u32[]{:S(2)}) collective-permute-start(f32[384,576]{0,1:T(8,128)S(1)} %bitcast.73), channel_id=1, source_target_pairs={{0,1},{1,2},{2,3},{3,4},{4,5},{5,6},{6,7},{7,8},{8,9},{9,10},{10,1... | collective-permute-start | bytes 2654216 | tf_op jit(solution)/shard_map/ppermute | solution.py:14
  191.8 12.5 %collective-permute-start = (f32[384,576]{0,1:T(8,128)S(1)}, f32[384,576]{0,1:T(8,128)S(1)}, u32[]{:S(2)}, u32[]{:S(2)}) collective-permute-start(f32[384,576]{0,1:T(8,128)S(1)} %bitcast.72), channel_id=1, source_target_pairs={{0,15},{1,0},{2,1},{3,2},{4,3},{5,4},{6,5},{7,6},{8,7},{9,8},{10,9... | collective-permute-start | bytes 2654216 | tf_op jit(solution)/shard_map/ppermute | solution.py:14
  205.8 22.4 %all-to-all-start.2 = ((f32[16,24,576]{2,1,0:T(8,128)}), f32[16,24,576]{2,1,0:T(8,128)S(1)}, u32[]{:S(2)}, u32[]{:S(2)}) async-start(f32[16,24,576]{2,1,0:T(8,128)} %bitcast.18), calls=%async_computation.2 | async-start | bytes 1966080 | tf_op jit(solution)/shard_map/all_to_all | solution.py:83
  229.9 5.3 %collective-permute-start.3 = (bf16[24,18,32]{2,1,0:T(8,128)(2,1)S(1)}, bf16[24,18,32]{2,1,0:T(8,128)(2,1)S(1)}, u32[]{:S(2)}, u32[]{:S(2)}) collective-permute-start(bf16[24,18,32]{2,1,0:T(8,128)(2,1)S(1)} %convolution_convert_fusion), channel_id=1, source_target_pairs={{0,15},{1,0},{2,1},{3,2},{4,3},{5,4},{6,5},{7,6},{8,7},{9,8},{10,9... | collective-permute-start | bytes 82952 | tf_op jit(solution)/shard_map/ppermute | solution.py:14
  232.5 4.6 collective-permute-start.2
  248.4 4.6 copy-start.6
  248.4 26.5 %all-to-all-start.3 = ((bf16[16,2,20736]{2,1,0:T(2,128)(2,1)}), bf16[16,2,20736]{2,1,0:T(2,128)(2,1)}, u32[]{:S(2)}, u32[]{:S(2)}) async-start(bf16[16,2,20736]{2,1,0:T(2,128)(2,1)} %reshape.179), calls=%async_computation.3 | async-start | bytes 2654208 | tf_op jit(solution)/shard_map/all_to_all | solution.py:97
  308.4 2.0 copy-start.4
  321.7 1.3 copy-start.1
  352.1 48.0 %all-to-all-start.4 = ((bf16[16,2,32768]{2,1,0:T(2,128)(2,1)}), bf16[16,2,32768]{2,1,0:T(2,128)(2,1)}, u32[]{:S(2)}, u32[]{:S(2)}) async-start(bf16[16,2,32768]{2,1,0:T(2,128)(2,1)} %reshape.183), calls=%async_computation.4 | async-start | bytes 4194304 | tf_op jit(solution)/shard_map/all_to_all | solution.py:110
  369.7 1.3 copy-start.2
  400.1 41.7 %all-to-all-start.5 = ((bf16[16,2,32768]{2,1,0:T(2,128)(2,1)}), bf16[16,2,32768]{2,1,0:T(2,128)(2,1)}, u32[]{:S(2)}, u32[]{:S(2)}) async-start(bf16[16,2,32768]{2,1,0:T(2,128)(2,1)} %reshape.181), calls=%async_computation.5 | async-start | bytes 4194304 | tf_op jit(solution)/shard_map/all_to_all | solution.py:110

commit v4 on v2

--- a/solution.py
+++ b/solution.py
@@ -83,13 +83,17 @@
         matrices,
         mine.reshape(share, PROJ, band_count),
         precision=lax.Precision.HIGHEST,
-    ).astype(jnp.bfloat16)
+    ).astype(jnp.bfloat16).reshape(share, PROJ * band_count)
     sides = jnp.stack([shift(dressed, "slab", 1), dressed, shift(dressed, "slab", -1)])
-    spread_out = jnp.broadcast_to(sides[None], (band_size,) + sides.shape)
+    spread_out = jnp.broadcast_to(sides.reshape(1, -1), (band_size, sides.size))
     every = lax.all_to_all(spread_out, "band", split_axis=0, concat_axis=0, tiled=True)
-    flat_rows = jnp.swapaxes(every, 0, 1).reshape(3 * slot_count, PROJ, band_count)
-    chosen = jnp.take(flat_rows, jnp.where(is_live, index_atom, 0), axis=0)
-    chosen = jnp.where(is_live[:, None, None], chosen, jnp.zeros((), jnp.bfloat16))
+    rows = every.reshape(band_size * 3 * share, PROJ * band_count)
+    side_of = index_atom // slot_count
+    slot_of = index_atom % slot_count
+    row_of = (slot_of // share) * (3 * share) + side_of * share + slot_of % share
+    chosen = jnp.take(rows, jnp.where(is_live, row_of, 0), axis=0)
+    chosen = jnp.where(is_live[:, None], chosen, jnp.zeros((), jnp.bfloat16))
+    chosen = chosen.reshape(pieces, PROJ, band_count)
     spread = jnp.einsum("pjk,pjn->pnk", proj_local, chosen, preferred_element_type=jnp.float32)
     result = scatter_blocks(index_block, spread, block_count)
     result = result.reshape(band_count, -1)

time: 334 us -> 353 us (1.057)
  other arithmetic: 9.44 us -> 43 us
  local copies, waits for them, and re-layouts: 89.3 us -> 80.1 us
  matrix products: 25.6 us -> 20.3 us
    scatter-add x1, other arithmetic: 6.54 us -> 17.5 us  [body(): jax.ops.segment_sum(projected.reshape(pieces, -1), target, num_segments=3...]
    broadcast_in_dim x0 -> x1, other arithmetic: none -> 10.7 us  [body(): spread_out = jnp.broadcast_to(sides.reshape(1, -1), (band_size, sides.size))]
    unnamed x14 -> x13, local copies, waits for them, and re-layouts: 22.6 us -> 12.3 us
    all_to_all x0 -> x1, other arithmetic: none -> 10.2 us  [body(): lax.all_to_all(spread_out, 'band', split_axis=0, concat_axis=0, tiled=True)]
    dot_general x1, matrix products: 13.1 us -> 7.79 us  [body(): jnp.einsum('pjk,pjn->pnk', proj_local, chosen, preferred_element_type=jnp...]
    select_n x0 -> x1, local copies, waits for them, and re-layouts: none -> 3.67 us  [body(): chosen = jnp.where(is_live[:, None], chosen, jnp.zeros((), jnp.bfloat16))]
    broadcast_in_dim x0 -> x3, local copies, waits for them, and re-layouts: none -> 3.54 us  [body(): spread_out = jnp.broadcast_to(sides.reshape(1, -1), (band_size, sides.size))]
  transfers between devices with their start and end apart: 7 -> 7, of which waited for: 6 -> 6; matrix products, arithmetic and copies ran while one was open for 1% -> 2% of each run, Pallas kernels for 0% -> 0%
where the time goes in v4:
time: 353 us; the launch traced here: 350 us
  waiting for transfers between devices  113 us (32%)
  local copies, waits for them, and re-layouts  80.1 us (23%)
  blocking collectives  55.4 us (16%)
  other arithmetic  43 us (12%)
  starting transfers between devices  21.2 us (6%)
  matrix products  20.3 us (6%)
  Pallas kernels  15.4 us (4%)
    all_to_all x1, waiting for transfers between devices, body(): lax.all_to_all(orbitals, 'band', split_axis=1, concat_axis=0, tiled=True)  62.6 us
    all_to_all x1, blocking collectives, body(): lax.all_to_all(result, 'band', split_axis=0, concat_axis=1, tiled=True)  55.4 us
    all_to_all x1, waiting for transfers between devices, body(): lax.all_to_all(spread_out, 'band', split_axis=0, concat_axis=0, tiled=True)  24.4 us
    reshape x2, local copies, waits for them, and re-layouts, body(): blocks = slab_waves.reshape(band_count, -1, BLOCK)  18.2 us
    scatter-add x1, other arithmetic, body(): jax.ops.segment_sum(projected.reshape(pieces, -1), target, num_segments=3...  17.5 us
    pallas_call x1, Pallas kernels, scatter_blocks(): pl.pallas_call(_scatter_body, out_shape=jax.ShapeDtypeStruct((bands, bloc...  15.4 us
    all_to_all x1, waiting for transfers between devices, body(): lax.all_to_all(own_total.reshape(band_size, share, -1), 'band', split_axi...  13.4 us
    ppermute x4, waiting for transfers between devices, shift(): lax.ppermute(cells, axis, [(i, (i + step) % count) for i in range(count)])  13 us
  transfers between devices with their start and end apart: 7, of which 6 were waited for; matrix products, arithmetic and copies ran while one was open for 2% of the time, Pallas kernels for 0%

profile of v4, /device:TPU:96, one launch (start us, length us, event | category | flops | bytes accessed | tf_op | source)
XLA Modules:
  0.0 349.5 jit_solution(10232175073230912191)
XLA Ops:
  0.0 0.0 copy-start
  0.0 0.0 copy-start.2
  0.0 0.0 copy-start.3
  0.0 7.2 %all-to-all-start = ((bf16[2,16,65536]{2,0,1:T(2,128)(2,1)}), bf16[2,16,65536]{2,0,1:T(2,128)(2,1)}, u32[]{:S(2)}, u32[]{:S(2)}) async-start(bf16[2,16,65536]{2,0,1:T(2,128)(2,1)} %bitcast.57), calls=%async_computation | async-start | bytes 8388608 | tf_op jit(solution)/shard_map/all_to_all | solution.py:51
  7.2 0.0 copy-done.2
  7.3 0.0 copy-done.3
  7.3 0.6 compare_select_fusion
  7.9 62.6 %all-to-all-done = bf16[2,16,65536]{2,0,1:T(2,128)(2,1)} async-done(((bf16[2,16,65536]{2,0,1:T(2,128)(2,1)}), bf16[2,16,65536]{2,0,1:T(2,128)(2,1)}, u32[]{:S(2)}, u32[]{:S(2)}) %all-to-all-start) | async-done | bytes 4194336 | tf_op jit(solution)/shard_map/all_to_all | solution.py:51
  70.5 11.4 %reshape.248 = bf16[32,512,128]{2,1,0:T(8,128)(2,1)} reshape(bf16[16,2,65536]{2,1,0:T(2,128)(2,1)} %bitcast.6) | data formatting | bytes 8388608 | tf_op jit(solution)/shard_map/reshape | solution.py:53
  81.9 6.8 %copy.31 = bf16[32,512,128]{2,0,1:T(8,128)(2,1)} copy(bf16[32,512,128]{2,1,0:T(8,128)(2,1)} %reshape.248) | data formatting | bytes 8388608 | tf_op jit(solution)/shard_map/reshape | solution.py:53
  88.8 5.4 %gather_fusion = bf16[512,32,128]{2,1,0:T(8,128)(2,1)} fusion(bf16[32,512,128]{2,0,1:T(8,128)(2,1)} %copy.31, s32[1024]{0:T(1024)S(1)} %pad_clamp_fusion.1), kind=kCustom, calls=%fused_computation | custom fusion | bytes 8390656 | tf_op jit(solution)/shard_map/jit(_take)/gather | solution.py:61
  94.2 0.0 copy-done
  94.2 11.0 %fusion.7 = f32[512,18,32]{2,1,0:T(8,128)} fusion(bf16[512,18,128]{2,0,1:T(8,128)(2,1)S(1)} %bitcast.51, bf16[512,32,128]{2,1,0:T(8,128)(2,1)} %gather_fusion, pred[512]{0:T(512)(128)(4,1)S(1)} %compare_and_fusion), kind=kOutput, calls=%fused_computation.10 | convolution fusion | flops 77594624 | bytes 7733760 | tf_op jit(solution)/shard_map/pjk,npk->pjn/dot_general | solution.py:62
  105.1 4.5 %copy.33 = f32[512,18,32]{0,2,1:T(8,128)S(1)} copy(f32[512,18,32]{2,1,0:T(8,128)} %fusion.7) | data formatting | bytes 2359296 | tf_op jit(solution)/shard_map/pjk,npk->pjn/dot_general | solution.py:62
  109.6 1.5 copy.34
  111.1 17.5 %scatter_custom_fusion = f32[1153,576]{1,0:T(8,128)} fusion(s32[512]{0:T(512)S(1)} %bitcast.66, f32[512,576]{1,0:T(8,128)} %copy.34, f32[]{:T(128)} %constant.72.clone.1), kind=kCustom, calls=%fused_computation.12 | custom fusion | flops 294912 | bytes 2657024 | tf_op jit(solution)/shard_map/scatter-add | solution.py:64
  128.6 2.6 fusion.25
  131.2 2.5 copy.37
  133.6 0.0 collective-permute-start.1
  133.6 1.3 copy.35
  134.9 1.7 collective-permute-start
  136.6 9.8 %collective-permute-done.1 = f32[384,576]{0,1:T(8,128)} collective-permute-done((f32[384,576]{0,1:T(8,128)}, f32[384,576]{0,1:T(8,128)}, u32[]{:S(2)}, u32[]{:S(2)}) %collective-permute-start.1) | collective-permute-done | bytes 884768 | tf_op jit(solution)/shard_map/ppermute | solution.py:14
  146.4 1.5 copy.38
  147.9 0.0 collective-permute-done
  147.9 2.5 copy.36
  150.4 2.7 fusion.15
  153.1 4.7 %all-to-all-start.1 = ((f32[16,24,576]{2,1,0:T(8,128)}), f32[16,24,576]{2,1,0:T(8,128)S(1)}, u32[]{:S(2)}, u32[]{:S(2)}) async-start(f32[16,24,576]{2,1,0:T(8,128)} %bitcast.58), calls=%async_computation.1 | async-start | bytes 1966080 | tf_op jit(solution)/shard_map/all_to_all | solution.py:75
  157.8 1.1 constant_dynamic-slice_fusion
  158.8 0.1 copy.29
  158.9 0.9 reshape.247
  159.8 13.4 %all-to-all-done.1 = f32[16,24,576]{2,1,0:T(8,128)S(1)} async-done(((f32[16,24,576]{2,1,0:T(8,128)}), f32[16,24,576]{2,1,0:T(8,128)S(1)}, u32[]{:S(2)}, u32[]{:S(2)}) %all-to-all-start.1) | async-done | bytes 884768 | tf_op jit(solution)/shard_map/all_to_all | solution.py:75
  173.2 0.1 reduce_sum.9
  173.3 0.1 reshape.251
  173.4 1.6 convolution_convert_fusion
  175.0 0.1 reshape.252
  175.1 3.0 collective-permute-start.3
  178.1 0.0 collective-permute-start.2
  178.1 0.1 stack_reshape.3
  178.3 1.4 collective-permute-done.3
  179.7 1.7 collective-permute-done.2
  181.4 0.1 broadcast_in_dim.52
  181.6 2.9 broadcast_in_dim.53
  184.5 0.5 broadcast.286
  185.0 10.7 %reduce.5 = bf16[16,41472]{1,0:T(8,128)(2,1)} reduce(bf16[16,1,41472]{2,1,0:T(2,128)(2,1)} %broadcast_in_dim.53, bf16[]{:T(256)} %broadcast.286), dimensions={1}, to_apply=%broadcast_in_dim.53.reduce_sub_computation | reduce | bytes 2654210 | tf_op jit(solution)/shard_map/broadcast_in_dim | solution.py:88
  195.7 0.0 copy-start.4
  195.7 2.3 reshape.283
  198.0 4.6 %all-to-all-start.2 = ((bf16[16,2,20736]{2,1,0:T(2,128)(2,1)}), bf16[16,2,20736]{2,1,0:T(2,128)(2,1)}, u32[]{:S(2)}, u32[]{:S(2)}) async-start(bf16[16,2,20736]{2,1,0:T(2,128)(2,1)} %reshape.283), calls=%async_computation.2 | async-start | bytes 2654208 | tf_op jit(solution)/shard_map/all_to_all | solution.py:89
  202.6 0.0 copy-done.4
  202.7 24.4 %all-to-all-done.2 = bf16[16,2,20736]{2,1,0:T(2,128)(2,1)} async-done(((bf16[16,2,20736]{2,1,0:T(2,128)(2,1)}), bf16[16,2,20736]{2,1,0:T(2,128)(2,1)}, u32[]{:S(2)}, u32[]{:S(2)}) %all-to-all-start.2) | async-done | bytes 1327136 | tf_op jit(solution)/shard_map/all_to_all | solution.py:89
  227.1 5.9 %reshape.284 = bf16[16,1,41472]{2,1,0:T(2,128)(2,1)} reshape(bf16[16,2,20736]{2,1,0:T(2,128)(2,1)} %all-to-all-done.2) | data formatting | bytes 2654208
  233.1 10.2 %reduce.2 = bf16[16,41472]{1,0:T(8,128)(2,1)} reduce(bf16[16,1,41472]{2,1,0:T(2,128)(2,1)} %reshape.284, bf16[]{:T(256)} %constant.83), dimensions={1}, to_apply=%all_to_all.37.reduce_sub_computation | reduce | bytes 2654210 | tf_op jit(solution)/shard_map/all_to_all | solution.py:89
  243.2 3.2 reshape.253
  246.4 3.7 %gather_fusion.1 = bf16[512,576]{1,0:T(8,128)(2,1)S(1)} fusion(bf16[1152,576]{1,0:T(8,128)(2,1)} %reshape.253, s32[1024]{0:T(1024)S(1)} %pad_clamp_fusion), kind=kCustom, calls=%fused_computation.1 | custom fusion | bytes 1181696 | tf_op jit(solution)/shard_map/jit(_take)/gather | solution.py:94
  250.1 1.1 copy.39
  251.1 1.1 select_select_fusion
  252.3 3.7 %copy.40 = bf16[512,18,32]{2,1,0:T(8,128)(2,1)} copy(bf16[512,18,32]{0,2,1:T(8,128)(2,1)S(1)} %select_select_fusion) | data formatting | bytes 1179648 | tf_op jit(solution)/shard_map/jit(_where)/select_n | solution.py:95
  256.0 7.8 %fusion.4.spread_ref = f32[512,32,128]{2,1,0:T(8,128)} fusion(bf16[512,18,32]{2,1,0:T(8,128)(2,1)} %copy.40, bf16[512,18,128]{2,0,1:T(8,128)(2,1)S(1)} %bitcast.52), kind=kOutput, calls=%fused_computation.7 | convolution fusion | flops 75497472 | bytes 11337728 | tf_op jit(solution)/shard_map/pjk,pjn->pnk/dot_general | solution.py:97
  263.8 15.4 %shard_map.55 = bf16[32,512,128]{2,1,0:T(8,128)(2,1)S(1)} custom-call(s32[512]{0:T(512)S(1)} %bitcast.54, f32[512,32,128]{2,1,0:T(8,128)} %fusion.4.spread_ref), custom_call_target="tpu_custom_call" | custom-call | tf_op jit(solution)/shard_map/pallas_call | solution.py:37
  279.2 0.0 copy-start.1
  279.2 2.0 copy-done.1
  281.2 10.5 %all_to_all.38 = bf16[16,2,65536]{2,1,0:T(2,128)(2,1)} reshape(bf16[32,512,128]{2,1,0:T(8,128)(2,1)} %copy-done.1) | data formatting | bytes 8388608 | tf_op jit(solution)/shard_map/all_to_all | solution.py:100
  291.6 55.4 %all_to_all.46 = bf16[16,2,65536]{2,1,0:T(2,128)(2,1)S(1)} all-to-all(bf16[16,2,65536]{2,1,0:T(2,128)(2,1)} %all_to_all.38), channel_id=1, replica_groups=mesh['band'=16,'slab'=16] {'band'}, dimensions={0} | all-to-all | bytes 8388608 | tf_op jit(solution)/shard_map/all_to_all | solution.py:100
  347.1 2.0 copy.50
  (8 shorter events, 0.1 us)
Async XLA Ops:
  0.0 94.2 %copy-start = (bf16[1,1,512,18,128]{4,2,3,1,0:T(8,128)(2,1)S(1)}, bf16[1,1,512,18,128]{4,2,3,1,0:T(8,128)(2,1)}, u32[]{:S(2)}) copy-start(bf16[1,1,512,18,128]{4,2,3,1,0:T(8,128)(2,1)} %param.6) | copy-start | bytes 7077892
  0.0 7.2 %copy-start.2 = (s32[1,1,512]{2,1,0:T(1,128)S(1)}, s32[1,1,512]{2,1,0:T(1,128)}, u32[]{:S(2)}) copy-start(s32[1,1,512]{2,1,0:T(1,128)} %param.7) | copy-start | bytes 6148
  0.0 7.3 %copy-start.3 = (s32[1,1,512]{2,1,0:T(1,128)S(1)}, s32[1,1,512]{2,1,0:T(1,128)}, u32[]{:S(2)}) copy-start(s32[1,1,512]{2,1,0:T(1,128)} %param.8) | copy-start | bytes 6148
  0.0 70.5 %all-to-all-start = ((bf16[2,16,65536]{2,0,1:T(2,128)(2,1)}), bf16[2,16,65536]{2,0,1:T(2,128)(2,1)}, u32[]{:S(2)}, u32[]{:S(2)}) async-start(bf16[2,16,65536]{2,0,1:T(2,128)(2,1)} %bitcast.57), calls=%async_computation | async-start | bytes 8388608 | tf_op jit(solution)/shard_map/all_to_all | solution.py:51
  133.6 12.8 %collective-permute-start.1 = (f32[384,576]{0,1:T(8,128)}, f32[384,576]{0,1:T(8,128)}, u32[]{:S(2)}, u32[]{:S(2)}) collective-permute-start(f32[384,576]{0,1:T(8,128)} %copy.37), channel_id=1, source_target_pairs={{0,1},{1,2},{2,3},{3,4},{4,5},{5,6},{6,7},{7,8},{8,9},{9,10},{10,1... | collective-permute-start | bytes 2654216 | tf_op jit(solution)/shard_map/ppermute | solution.py:14
  134.9 13.0 %collective-permute-start = (f32[384,576]{0,1:T(8,128)}, f32[384,576]{0,1:T(8,128)}, u32[]{:S(2)}, u32[]{:S(2)}) collective-permute-start(f32[384,576]{0,1:T(8,128)} %copy.35), channel_id=1, source_target_pairs={{0,15},{1,0},{2,1},{3,2},{4,3},{5,4},{6,5},{7,6},{8,7},{9,8},{10,9... | collective-permute-start | bytes 2654216 | tf_op jit(solution)/shard_map/ppermute | solution.py:14
  153.1 20.1 %all-to-all-start.1 = ((f32[16,24,576]{2,1,0:T(8,128)}), f32[16,24,576]{2,1,0:T(8,128)S(1)}, u32[]{:S(2)}, u32[]{:S(2)}) async-start(f32[16,24,576]{2,1,0:T(8,128)} %bitcast.58), calls=%async_computation.1 | async-start | bytes 1966080 | tf_op jit(solution)/shard_map/all_to_all | solution.py:75
  175.1 4.6 %collective-permute-start.3 = (bf16[24,576]{1,0:T(8,128)(2,1)S(1)}, bf16[24,576]{1,0:T(8,128)(2,1)S(1)}, u32[]{:S(2)}, u32[]{:S(2)}) collective-permute-start(bf16[24,576]{1,0:T(8,128)(2,1)S(1)} %reshape.252), channel_id=1, source_target_pairs={{0,15},{1,0},{2,1},{3,2},{4,3},{5,4},{6,5},{7,6},{8,7},{9,8},{10,9... | collective-permute-start | bytes 82952 | tf_op jit(solution)/shard_map/ppermute | solution.py:14
  178.1 3.3 collective-permute-start.2
  195.7 6.9 %copy-start.4 = (s32[512,1]{0,1:T(1,128)S(1)}, s32[512,1]{0,1:T(1,128)}, u32[]{:S(2)}) copy-start(s32[512,1]{0,1:T(1,128)} %get-tuple-element.11) | copy-start | bytes 6148
  198.0 29.1 %all-to-all-start.2 = ((bf16[16,2,20736]{2,1,0:T(2,128)(2,1)}), bf16[16,2,20736]{2,1,0:T(2,128)(2,1)}, u32[]{:S(2)}, u32[]{:S(2)}) async-start(bf16[16,2,20736]{2,1,0:T(2,128)(2,1)} %reshape.283), calls=%async_computation.2 | async-start | bytes 2654208 | tf_op jit(solution)/shard_map/all_to_all | solution.py:89
  279.2 2.0 copy-start.1

commit v5 on v4

--- a/solution.py
+++ b/solution.py
@@ -84,14 +84,17 @@
         mine.reshape(share, PROJ, band_count),
         precision=lax.Precision.HIGHEST,
     ).astype(jnp.bfloat16).reshape(share, PROJ * band_count)
-    sides = jnp.stack([shift(dressed, "slab", 1), dressed, shift(dressed, "slab", -1)])
-    spread_out = jnp.broadcast_to(sides.reshape(1, -1), (band_size, sides.size))
-    every = lax.all_to_all(spread_out, "band", split_axis=0, concat_axis=0, tiled=True)
-    rows = every.reshape(band_size * 3 * share, PROJ * band_count)
+    every = jnp.concatenate([shift(dressed, "slab", 1), dressed, shift(dressed, "slab", -1)])
+    mask = 1
+    while mask < band_size:
+        swap = [(i, i ^ mask) for i in range(band_size)]
+        every = jnp.concatenate([every, lax.ppermute(every, "band", swap)])
+        mask *= 2
     side_of = index_atom // slot_count
     slot_of = index_atom % slot_count
-    row_of = (slot_of // share) * (3 * share) + side_of * share + slot_of % share
-    chosen = jnp.take(rows, jnp.where(is_live, row_of, 0), axis=0)
+    place = lax.axis_index("band") ^ (slot_of // share)
+    row_of = place * (3 * share) + side_of * share + slot_of % share
+    chosen = jnp.take(every, jnp.where(is_live, row_of, 0), axis=0)
     chosen = jnp.where(is_live[:, None], chosen, jnp.zeros((), jnp.bfloat16))
     chosen = chosen.reshape(pieces, PROJ, band_count)
     spread = jnp.einsum("pjk,pjn->pnk", proj_local, chosen, preferred_element_type=jnp.float32)

time: 353 us -> 316 us (0.90)
  other arithmetic: 43 us -> 11.2 us
  waiting for transfers between devices: 113 us -> 128 us
  local copies, waits for them, and re-layouts: 80.1 us -> 70 us
  starting transfers between devices: 21.2 us -> 17.4 us
    ppermute x0 -> x4, waiting for transfers between devices: none -> 38.6 us  [body(): every = jnp.concatenate([every, lax.ppermute(every, 'band', swap)])]
    all_to_all x1 -> x0, waiting for transfers between devices: 24.4 us -> none  [body(): lax.all_to_all(spread_out, 'band', split_axis=0, concat_axis=0, tiled=True)]
    scatter-add x1, other arithmetic: 17.5 us -> 6.54 us  [body(): jax.ops.segment_sum(projected.reshape(pieces, -1), target, num_segments=3...]
    broadcast_in_dim x1 -> x0, other arithmetic: 10.7 us -> none  [body(): spread_out = jnp.broadcast_to(sides.reshape(1, -1), (band_size, sides.size))]
    all_to_all x1 -> x0, other arithmetic: 10.2 us -> none  [body(): lax.all_to_all(spread_out, 'band', split_axis=0, concat_axis=0, tiled=True)]
    unnamed x13 -> x16, local copies, waits for them, and re-layouts: 12.3 us -> 7.28 us
    all_to_all x1 -> x0, starting transfers between devices: 4.56 us -> none  [body(): lax.all_to_all(spread_out, 'band', split_axis=0, concat_axis=0, tiled=True)]
    broadcast_in_dim x3 -> x0, local copies, waits for them, and re-layouts: 3.54 us -> none  [body(): spread_out = jnp.broadcast_to(sides.reshape(1, -1), (band_size, sides.size))]
  transfers between devices with their start and end apart: 7 -> 10, of which waited for: 6 -> 9; matrix products, arithmetic and copies ran while one was open for 2% -> 3% of each run, Pallas kernels for 0% -> 0%
where the time goes in v5:
time: 316 us; the launch traced here: 315 us
  waiting for transfers between devices  128 us (41%)
  local copies, waits for them, and re-layouts  70 us (22%)
  blocking collectives  52.9 us (17%)
  matrix products  20.3 us (6%)
  starting transfers between devices  17.4 us (6%)
  Pallas kernels  15.4 us (5%)
  other arithmetic  11.2 us (4%)
    all_to_all x1, waiting for transfers between devices, body(): lax.all_to_all(orbitals, 'band', split_axis=1, concat_axis=0, tiled=True)  62.6 us
    all_to_all x1, blocking collectives, body(): lax.all_to_all(result, 'band', split_axis=0, concat_axis=1, tiled=True)  52.9 us
    ppermute x4, waiting for transfers between devices, body(): every = jnp.concatenate([every, lax.ppermute(every, 'band', swap)])  38.6 us
    reshape x2, local copies, waits for them, and re-layouts, body(): blocks = slab_waves.reshape(band_count, -1, BLOCK)  18.2 us
    pallas_call x1, Pallas kernels, scatter_blocks(): pl.pallas_call(_scatter_body, out_shape=jax.ShapeDtypeStruct((bands, bloc...  15.4 us
    all_to_all x1, waiting for transfers between devices, body(): lax.all_to_all(own_total.reshape(band_size, share, -1), 'band', split_axi...  13.4 us
    ppermute x4, waiting for transfers between devices, shift(): lax.ppermute(cells, axis, [(i, (i + step) % count) for i in range(count)])  13.1 us
    dot_general x1, matrix products, body(): jnp.einsum('pjk,npk->pjn', proj_local, picked, preferred_element_type=jnp...  10.9 us
  transfers between devices with their start and end apart: 10, of which 9 were waited for; matrix products, arithmetic and copies ran while one was open for 3% of the time, Pallas kernels for 0%

profile of v5, /device:TPU:96, one launch (start us, length us, event | category | flops | bytes accessed | tf_op | source)
XLA Modules:
  0.0 315.1 jit_solution(16373116458125915784)
XLA Ops:
  0.0 0.0 copy-start
  0.0 7.2 %all-to-all-start = ((bf16[2,16,65536]{2,0,1:T(2,128)(2,1)}), bf16[2,16,65536]{2,0,1:T(2,128)(2,1)}, u32[]{:S(2)}, u32[]{:S(2)}) async-start(bf16[2,16,65536]{2,0,1:T(2,128)(2,1)} %bitcast.55), calls=%async_computation | async-start | bytes 8388608 | tf_op jit(solution)/shard_map/all_to_all | solution.py:51
  7.3 0.0 copy-done.2
  7.3 0.0 copy-done.3
  7.3 0.6 compare_select_fusion
  7.9 62.6 %all-to-all-done = bf16[2,16,65536]{2,0,1:T(2,128)(2,1)} async-done(((bf16[2,16,65536]{2,0,1:T(2,128)(2,1)}), bf16[2,16,65536]{2,0,1:T(2,128)(2,1)}, u32[]{:S(2)}, u32[]{:S(2)}) %all-to-all-start) | async-done | bytes 4194336 | tf_op jit(solution)/shard_map/all_to_all | solution.py:51
  70.5 11.4 %reshape.238 = bf16[32,512,128]{2,1,0:T(8,128)(2,1)} reshape(bf16[16,2,65536]{2,1,0:T(2,128)(2,1)} %bitcast.6) | data formatting | bytes 8388608 | tf_op jit(solution)/shard_map/reshape | solution.py:53
  81.9 6.8 %copy.31 = bf16[32,512,128]{2,0,1:T(8,128)(2,1)} copy(bf16[32,512,128]{2,1,0:T(8,128)(2,1)} %reshape.238) | data formatting | bytes 8388608 | tf_op jit(solution)/shard_map/reshape | solution.py:53
  88.8 5.4 %gather_fusion = bf16[512,32,128]{2,1,0:T(8,128)(2,1)} fusion(bf16[32,512,128]{2,0,1:T(8,128)(2,1)} %copy.31, s32[1024]{0:T(1024)S(1)} %pad_clamp_fusion.1), kind=kCustom, calls=%fused_computation | custom fusion | bytes 8390656 | tf_op jit(solution)/shard_map/jit(_take)/gather | solution.py:61
  94.2 0.0 copy-done
  94.2 10.9 %fusion.7 = f32[512,18,32]{2,1,0:T(8,128)} fusion(bf16[512,18,128]{2,0,1:T(8,128)(2,1)S(1)} %bitcast.49, bf16[512,32,128]{2,1,0:T(8,128)(2,1)} %gather_fusion, pred[512]{0:T(512)(128)(4,1)S(1)} %compare_and_fusion), kind=kOutput, calls=%fused_computation.10 | convolution fusion | flops 77594624 | bytes 7733760 | tf_op jit(solution)/shard_map/pjk,npk->pjn/dot_general | solution.py:62
  105.1 4.5 %copy.33 = f32[512,18,32]{0,2,1:T(8,128)S(1)} copy(f32[512,18,32]{2,1,0:T(8,128)} %fusion.7) | data formatting | bytes 2359296 | tf_op jit(solution)/shard_map/pjk,npk->pjn/dot_general | solution.py:62
  109.6 1.5 copy.34
  111.1 6.5 %scatter_custom_fusion = f32[1153,576]{1,0:T(8,128)} fusion(s32[512]{0:T(512)S(1)} %bitcast.62, f32[512,576]{1,0:T(8,128)} %copy.34, f32[]{:T(128)} %constant.72.clone.1), kind=kCustom, calls=%fused_computation.12 | custom fusion | flops 294912 | bytes 2657024 | tf_op jit(solution)/shard_map/scatter-add | solution.py:64
  117.6 2.6 fusion.25
  120.2 2.5 copy.37
  122.7 0.0 collective-permute-start.1
  122.7 1.2 copy.35
  123.9 1.7 collective-permute-start
  125.7 9.8 %collective-permute-done.1 = f32[384,576]{0,1:T(8,128)} collective-permute-done((f32[384,576]{0,1:T(8,128)}, f32[384,576]{0,1:T(8,128)}, u32[]{:S(2)}, u32[]{:S(2)}) %collective-permute-start.1) | collective-permute-done | bytes 884768 | tf_op jit(solution)/shard_map/ppermute | solution.py:14
  135.5 1.5 copy.38
  137.0 0.0 collective-permute-done
  137.0 2.4 copy.36
  139.4 2.7 fusion.15
  142.1 4.7 %all-to-all-start.1 = ((f32[16,24,576]{2,1,0:T(8,128)}), f32[16,24,576]{2,1,0:T(8,128)S(1)}, u32[]{:S(2)}, u32[]{:S(2)}) async-start(f32[16,24,576]{2,1,0:T(8,128)} %bitcast.56), calls=%async_computation.1 | async-start | bytes 1966080 | tf_op jit(solution)/shard_map/all_to_all | solution.py:75
  146.8 1.1 constant_dynamic-slice_fusion
  147.9 0.1 copy.29
  148.0 0.9 reshape.237
  148.8 13.4 %all-to-all-done.1 = f32[16,24,576]{2,1,0:T(8,128)S(1)} async-done(((f32[16,24,576]{2,1,0:T(8,128)}), f32[16,24,576]{2,1,0:T(8,128)S(1)}, u32[]{:S(2)}, u32[]{:S(2)}) %all-to-all-start.1) | async-done | bytes 884768 | tf_op jit(solution)/shard_map/all_to_all | solution.py:75
  162.2 0.1 reduce_sum.9
  162.3 0.1 reshape.241
  162.4 1.6 convolution_convert_fusion
  164.0 0.1 reshape.242
  164.1 3.0 collective-permute-start.3
  167.1 0.0 collective-permute-start.2
  167.1 1.6 collective-permute-done.3
  168.7 1.7 collective-permute-done.2
  170.5 0.1 collective-permute-start.4
  170.6 0.6 constant_dynamic-update-slice_fusion.10
  171.2 0.6 constant_dynamic-update-slice_fusion.9
  171.8 4.3 %collective-permute-done.4 = bf16[72,576]{1,0:T(8,128)(2,1)S(1)} collective-permute-done((bf16[72,576]{1,0:T(8,128)(2,1)S(1)}, bf16[72,576]{1,0:T(8,128)(2,1)S(1)}, u32[]{:S(2)}, u32[]{:S(2)}) %collective-permute-start.4) | collective-permute-done | bytes 82976 | tf_op jit(solution)/shard_map/ppermute | solution.py:91
  176.1 0.1 collective-permute-start.5
  176.2 0.6 constant_dynamic-update-slice_fusion.8
  176.8 0.7 constant_dynamic-update-slice_fusion.7
  177.5 6.9 %collective-permute-done.5 = bf16[144,576]{1,0:T(8,128)(2,1)S(1)} collective-permute-done((bf16[144,576]{1,0:T(8,128)(2,1)S(1)}, bf16[144,576]{1,0:T(8,128)(2,1)S(1)}, u32[]{:S(2)}, u32[]{:S(2)}) %collective-permute-start.5) | collective-permute-done | bytes 165920 | tf_op jit(solution)/shard_map/ppermute | solution.py:91
  184.4 0.7 constant_dynamic-update-slice_fusion.6
  185.1 0.0 collective-permute-start.6
  185.1 9.7 %collective-permute-done.6 = bf16[288,576]{1,0:T(8,128)(2,1)S(1)} collective-permute-done((bf16[288,576]{1,0:T(8,128)(2,1)S(1)}, bf16[288,576]{1,0:T(8,128)(2,1)S(1)}, u32[]{:S(2)}, u32[]{:S(2)}) %collective-permute-start.6) | collective-permute-done | bytes 331808 | tf_op jit(solution)/shard_map/ppermute | solution.py:91
  194.8 0.8 constant_dynamic-update-slice_fusion.5
  195.6 0.5 collective-permute-start.7
  196.2 0.0 copy-done.4
  196.3 17.7 %collective-permute-done.7 = bf16[576,576]{1,0:T(8,128)(2,1)S(1)} collective-permute-done((bf16[576,576]{1,0:T(8,128)(2,1)S(1)}, bf16[576,576]{1,0:T(8,128)(2,1)S(1)}, u32[]{:S(2)}, u32[]{:S(2)}) %collective-permute-start.7) | collective-permute-done | bytes 663584 | tf_op jit(solution)/shard_map/ppermute | solution.py:91
  213.9 0.9 constant_dynamic-update-slice_fusion.11
  214.9 3.9 %gather_fusion.1 = bf16[512,576]{1,0:T(8,128)(2,1)S(1)} fusion(bf16[1152,576]{1,0:T(8,128)(2,1)} %constant_dynamic-update-slice_fusion.11, s32[1024]{0:T(1024)S(1)} %pad_clamp_fusion), kind=kCustom, calls=%fused_computation.1 | custom fusion | bytes 1181696 | tf_op jit(solution)/shard_map/jit(_take)/gather | solution.py:97
  218.8 1.1 copy.39
  219.9 1.1 select_select_fusion
  221.0 3.4 %copy.40 = bf16[512,18,32]{2,1,0:T(8,128)(2,1)} copy(bf16[512,18,32]{0,2,1:T(8,128)(2,1)S(1)} %select_select_fusion) | data formatting | bytes 1179648 | tf_op jit(solution)/shard_map/jit(_where)/select_n | solution.py:98
  224.4 7.8 %fusion.4.spread_ref = f32[512,32,128]{2,1,0:T(8,128)} fusion(bf16[512,18,32]{2,1,0:T(8,128)(2,1)} %copy.40, bf16[512,18,128]{2,0,1:T(8,128)(2,1)S(1)} %bitcast.50), kind=kOutput, calls=%fused_computation.7 | convolution fusion | flops 75497472 | bytes 11337728 | tf_op jit(solution)/shard_map/pjk,pjn->pnk/dot_general | solution.py:100
  232.2 15.4 %shard_map.55 = bf16[32,512,128]{2,1,0:T(8,128)(2,1)S(1)} custom-call(s32[512]{0:T(512)S(1)} %bitcast.52, f32[512,32,128]{2,1,0:T(8,128)} %fusion.4.spread_ref), custom_call_target="tpu_custom_call" | custom-call | tf_op jit(solution)/shard_map/pallas_call | solution.py:37
  247.7 0.0 copy-start.1
  247.7 2.0 copy-done.1
  249.7 10.5 %all_to_all.33 = bf16[16,2,65536]{2,1,0:T(2,128)(2,1)} reshape(bf16[32,512,128]{2,1,0:T(8,128)(2,1)} %copy-done.1) | data formatting | bytes 8388608 | tf_op jit(solution)/shard_map/all_to_all | solution.py:103
  260.1 52.9 %all_to_all.40 = bf16[16,2,65536]{2,1,0:T(2,128)(2,1)S(1)} all-to-all(bf16[16,2,65536]{2,1,0:T(2,128)(2,1)} %all_to_all.33), channel_id=1, replica_groups=mesh['band'=16,'slab'=16] {'band'}, dimensions={0} | all-to-all | bytes 8388608 | tf_op jit(solution)/shard_map/all_to_all | solution.py:103
  313.0 2.0 copy.65
  (12 shorter events, 0.1 us)
Async XLA Ops:
  0.0 94.2 %copy-start = (bf16[1,1,512,18,128]{4,2,3,1,0:T(8,128)(2,1)S(1)}, bf16[1,1,512,18,128]{4,2,3,1,0:T(8,128)(2,1)}, u32[]{:S(2)}) copy-start(bf16[1,1,512,18,128]{4,2,3,1,0:T(8,128)(2,1)} %param.6) | copy-start | bytes 7077892
  0.0 7.3 %copy-start.2 = (s32[1,1,512]{2,1,0:T(1,128)S(1)}, s32[1,1,512]{2,1,0:T(1,128)}, u32[]{:S(2)}) copy-start(s32[1,1,512]{2,1,0:T(1,128)} %param.7) | copy-start | bytes 6148
  0.0 7.3 %copy-start.3 = (s32[1,1,512]{2,1,0:T(1,128)S(1)}, s32[1,1,512]{2,1,0:T(1,128)}, u32[]{:S(2)}) copy-start(s32[1,1,512]{2,1,0:T(1,128)} %param.8) | copy-start | bytes 6148
  0.0 70.5 %all-to-all-start = ((bf16[2,16,65536]{2,0,1:T(2,128)(2,1)}), bf16[2,16,65536]{2,0,1:T(2,128)(2,1)}, u32[]{:S(2)}, u32[]{:S(2)}) async-start(bf16[2,16,65536]{2,0,1:T(2,128)(2,1)} %bitcast.55), calls=%async_computation | async-start | bytes 8388608 | tf_op jit(solution)/shard_map/all_to_all | solution.py:51
  122.7 12.8 %collective-permute-start.1 = (f32[384,576]{0,1:T(8,128)}, f32[384,576]{0,1:T(8,128)}, u32[]{:S(2)}, u32[]{:S(2)}) collective-permute-start(f32[384,576]{0,1:T(8,128)} %copy.37), channel_id=1, source_target_pairs={{0,1},{1,2},{2,3},{3,4},{4,5},{5,6},{6,7},{7,8},{8,9},{9,10},{10,1... | collective-permute-start | bytes 2654216 | tf_op jit(solution)/shard_map/ppermute | solution.py:14
  123.9 13.0 %collective-permute-start = (f32[384,576]{0,1:T(8,128)}, f32[384,576]{0,1:T(8,128)}, u32[]{:S(2)}, u32[]{:S(2)}) collective-permute-start(f32[384,576]{0,1:T(8,128)} %copy.35), channel_id=1, source_target_pairs={{0,15},{1,0},{2,1},{3,2},{4,3},{5,4},{6,5},{7,6},{8,7},{9,8},{10,9... | collective-permute-start | bytes 2654216 | tf_op jit(solution)/shard_map/ppermute | solution.py:14
  142.1 20.1 %all-to-all-start.1 = ((f32[16,24,576]{2,1,0:T(8,128)}), f32[16,24,576]{2,1,0:T(8,128)S(1)}, u32[]{:S(2)}, u32[]{:S(2)}) async-start(f32[16,24,576]{2,1,0:T(8,128)} %bitcast.56), calls=%async_computation.1 | async-start | bytes 1966080 | tf_op jit(solution)/shard_map/all_to_all | solution.py:75
  148.0 48.2 %copy-start.4 = (s32[512,1]{0,1:T(1,128)S(1)}, s32[512,1]{0,1:T(1,128)}, u32[]{:S(2)}) copy-start(s32[512,1]{0,1:T(1,128)} %get-tuple-element.28) | copy-start | bytes 6148
  164.1 4.6 %collective-permute-start.3 = (bf16[24,576]{1,0:T(8,128)(2,1)S(1)}, bf16[24,576]{1,0:T(8,128)(2,1)S(1)}, u32[]{:S(2)}, u32[]{:S(2)}) collective-permute-start(bf16[24,576]{1,0:T(8,128)(2,1)S(1)} %reshape.242), channel_id=1, source_target_pairs={{0,15},{1,0},{2,1},{3,2},{4,3},{5,4},{6,5},{7,6},{8,7},{9,8},{10,9... | collective-permute-start | bytes 82952 | tf_op jit(solution)/shard_map/ppermute | solution.py:14
  167.1 3.3 %collective-permute-start.2 = (bf16[24,576]{1,0:T(8,128)(2,1)S(1)}, bf16[24,576]{1,0:T(8,128)(2,1)S(1)}, u32[]{:S(2)}, u32[]{:S(2)}) collective-permute-start(bf16[24,576]{1,0:T(8,128)(2,1)S(1)} %reshape.242), channel_id=1, source_target_pairs={{0,1},{1,2},{2,3},{3,4},{4,5},{5,6},{6,7},{7,8},{8,9},{9,10},{10,1... | collective-permute-start | bytes 82952 | tf_op jit(solution)/shard_map/ppermute | solution.py:14
  170.5 5.6 %collective-permute-start.4 = (bf16[72,576]{1,0:T(8,128)(2,1)S(1)}, bf16[72,576]{1,0:T(8,128)(2,1)S(1)}, u32[]{:S(2)}, u32[]{:S(2)}) collective-permute-start(bf16[72,576]{1,0:T(8,128)(2,1)S(1)} %pad_maximum_fusion.1), channel_id=1, source_target_pairs={{0,16},{16,0},{32,48},{48,32},{64,80},{80,64},{96,112},{112,96},{1... | collective-permute-start | bytes 248840 | tf_op jit(solution)/shard_map/ppermute | solution.py:91
  176.1 8.2 %collective-permute-start.5 = (bf16[144,576]{1,0:T(8,128)(2,1)S(1)}, bf16[144,576]{1,0:T(8,128)(2,1)S(1)}, u32[]{:S(2)}, u32[]{:S(2)}) collective-permute-start(bf16[144,576]{1,0:T(8,128)(2,1)S(1)} %pad_maximum_fusion), channel_id=1, source_target_pairs={{0,32},{16,48},{32,0},{48,16},{64,96},{80,112},{96,64},{112,80},{1... | collective-permute-start | bytes 497672 | tf_op jit(solution)/shard_map/ppermute | solution.py:91
  185.1 9.7 %collective-permute-start.6 = (bf16[288,576]{1,0:T(8,128)(2,1)S(1)}, bf16[288,576]{1,0:T(8,128)(2,1)S(1)}, u32[]{:S(2)}, u32[]{:S(2)}) collective-permute-start(bf16[288,576]{1,0:T(8,128)(2,1)S(1)} %get-tuple-element.13), channel_id=1, source_target_pairs={{0,64},{16,80},{32,96},{48,112},{64,0},{80,16},{96,32},{112,48},{1... | collective-permute-start | bytes 995336 | tf_op jit(solution)/shard_map/ppermute | solution.py:91
  195.6 18.3 %collective-permute-start.7 = (bf16[576,576]{1,0:T(8,128)(2,1)S(1)}, bf16[576,576]{1,0:T(8,128)(2,1)S(1)}, u32[]{:S(2)}, u32[]{:S(2)}) collective-permute-start(bf16[576,576]{1,0:T(8,128)(2,1)S(1)} %get-tuple-element.9), channel_id=1, source_target_pairs={{0,128},{16,144},{32,160},{48,176},{64,192},{80,208},{96,224},{112... | collective-permute-start | bytes 1990664 | tf_op jit(solution)/shard_map/ppermute | solution.py:91
  247.7 2.0 copy-start.1

commit v6 on v5

--- a/solution.py
+++ b/solution.py
@@ -12,6 +12,13 @@
 def shift(cells, axis, step):
     count = lax.axis_size(axis)
     return lax.ppermute(cells, axis, [(i, (i + step) % count) for i in range(count)])
+
+
+def doubling_masks(count):
+    masks = [1 << k for k in range(count.bit_length() - 1)]
+    far = [m for k, m in enumerate(masks) if k % 2 == 1]
+    near = [m for k, m in enumerate(masks) if k % 2 == 0]
+    return far + near
 
 
 def _scatter_body(blk_ref, spread_ref, out_ref, acc_ref):
@@ -85,14 +92,14 @@
         precision=lax.Precision.HIGHEST,
     ).astype(jnp.bfloat16).reshape(share, PROJ * band_count)
     every = jnp.concatenate([shift(dressed, "slab", 1), dressed, shift(dressed, "slab", -1)])
-    mask = 1
-    while mask < band_size:
+    masks = doubling_masks(band_size)
+    for mask in masks:
         swap = [(i, i ^ mask) for i in range(band_size)]
         every = jnp.concatenate([every, lax.ppermute(every, "band", swap)])
-        mask *= 2
     side_of = index_atom // slot_count
     slot_of = index_atom % slot_count
-    place = lax.axis_index("band") ^ (slot_of // share)
+    apart = lax.axis_index("band") ^ (slot_of // share)
+    place = sum(((apart // mask) % 2) << step for step, mask in enumerate(masks))
     row_of = place * (3 * share) + side_of * share + slot_of % share
     chosen = jnp.take(every, jnp.where(is_live, row_of, 0), axis=0)
     chosen = jnp.where(is_live[:, None], chosen, jnp.zeros((), jnp.bfloat16))

time: 316 us -> 316 us (level)
  no operation moved by 1% of the time
where the time goes in v6:
time: 316 us; the launch traced here: 315 us
  waiting for transfers between devices  127 us (40%)
  local copies, waits for them, and re-layouts  70 us (22%)
  blocking collectives  52.9 us (17%)
  matrix products  20.3 us (6%)
  starting transfers between devices  17.7 us (6%)
  Pallas kernels  15.4 us (5%)
  other arithmetic  11.2 us (4%)
    all_to_all x1, waiting for transfers between devices, body(): lax.all_to_all(orbitals, 'band', split_axis=1, concat_axis=0, tiled=True)  62.5 us
    all_to_all x1, blocking collectives, body(): lax.all_to_all(result, 'band', split_axis=0, concat_axis=1, tiled=True)  52.9 us
    ppermute x4, waiting for transfers between devices, body(): every = jnp.concatenate([every, lax.ppermute(every, 'band', swap)])  38.2 us
    reshape x2, local copies, waits for them, and re-layouts, body(): blocks = slab_waves.reshape(band_count, -1, BLOCK)  18.2 us
    pallas_call x1, Pallas kernels, scatter_blocks(): pl.pallas_call(_scatter_body, out_shape=jax.ShapeDtypeStruct((bands, bloc...  15.4 us
    all_to_all x1, waiting for transfers between devices, body(): lax.all_to_all(own_total.reshape(band_size, share, -1), 'band', split_axi...  13.4 us
    ppermute x4, waiting for transfers between devices, shift(): lax.ppermute(cells, axis, [(i, (i + step) % count) for i in range(count)])  13.1 us
    dot_general x1, matrix products, body(): jnp.einsum('pjk,npk->pjn', proj_local, picked, preferred_element_type=jnp...  10.9 us
  transfers between devices with their start and end apart: 10, of which 9 were waited for; matrix products, arithmetic and copies ran while one was open for 3% of the time, Pallas kernels for 0%

profile of v6, /device:TPU:96, one launch (start us, length us, event | category | flops | bytes accessed | tf_op | source)
XLA Modules:
  0.0 315.1 jit_solution(12916835553294877710)
XLA Ops:
  0.0 0.0 copy-start
  0.0 7.2 %all-to-all-start = ((bf16[2,16,65536]{2,0,1:T(2,128)(2,1)}), bf16[2,16,65536]{2,0,1:T(2,128)(2,1)}, u32[]{:S(2)}, u32[]{:S(2)}) async-start(bf16[2,16,65536]{2,0,1:T(2,128)(2,1)} %bitcast.55), calls=%async_computation | async-start | bytes 8388608 | tf_op jit(solution)/shard_map/all_to_all | solution.py:58
  7.3 0.0 copy-done.2
  7.3 0.0 copy-done.3
  7.3 0.7 compare_select_fusion
  8.0 62.5 %all-to-all-done = bf16[2,16,65536]{2,0,1:T(2,128)(2,1)} async-done(((bf16[2,16,65536]{2,0,1:T(2,128)(2,1)}), bf16[2,16,65536]{2,0,1:T(2,128)(2,1)}, u32[]{:S(2)}, u32[]{:S(2)}) %all-to-all-start) | async-done | bytes 4194336 | tf_op jit(solution)/shard_map/all_to_all | solution.py:58
  70.5 11.4 %reshape.482 = bf16[32,512,128]{2,1,0:T(8,128)(2,1)} reshape(bf16[16,2,65536]{2,1,0:T(2,128)(2,1)} %bitcast.6) | data formatting | bytes 8388608 | tf_op jit(solution)/shard_map/reshape | solution.py:60
  81.9 6.8 %copy.31 = bf16[32,512,128]{2,0,1:T(8,128)(2,1)} copy(bf16[32,512,128]{2,1,0:T(8,128)(2,1)} %reshape.482) | data formatting | bytes 8388608 | tf_op jit(solution)/shard_map/reshape | solution.py:60
  88.8 5.4 %gather_fusion = bf16[512,32,128]{2,1,0:T(8,128)(2,1)} fusion(bf16[32,512,128]{2,0,1:T(8,128)(2,1)} %copy.31, s32[1024]{0:T(1024)S(1)} %pad_clamp_fusion.1), kind=kCustom, calls=%fused_computation | custom fusion | bytes 8390656 | tf_op jit(solution)/shard_map/jit(_take)/gather | solution.py:68
  94.2 0.0 copy-done
  94.2 10.9 %fusion.7 = f32[512,18,32]{2,1,0:T(8,128)} fusion(bf16[512,18,128]{2,0,1:T(8,128)(2,1)S(1)} %bitcast.49, bf16[512,32,128]{2,1,0:T(8,128)(2,1)} %gather_fusion, pred[512]{0:T(512)(128)(4,1)S(1)} %compare_and_fusion), kind=kOutput, calls=%fused_computation.10 | convolution fusion | flops 77594624 | bytes 7733760 | tf_op jit(solution)/shard_map/pjk,npk->pjn/dot_general | solution.py:69
  105.1 4.5 %copy.33 = f32[512,18,32]{0,2,1:T(8,128)S(1)} copy(f32[512,18,32]{2,1,0:T(8,128)} %fusion.7) | data formatting | bytes 2359296 | tf_op jit(solution)/shard_map/pjk,npk->pjn/dot_general | solution.py:69
  109.6 1.5 copy.34
  111.1 6.5 %scatter_custom_fusion = f32[1153,576]{1,0:T(8,128)} fusion(s32[512]{0:T(512)S(1)} %bitcast.62, f32[512,576]{1,0:T(8,128)} %copy.34, f32[]{:T(128)} %constant.147.clone.1), kind=kCustom, calls=%fused_computation.12 | custom fusion | flops 294912 | bytes 2657024 | tf_op jit(solution)/shard_map/scatter-add | solution.py:71
  117.6 2.6 fusion.51
  120.2 2.5 copy.37
  122.7 0.0 collective-permute-start.1
  122.7 1.2 copy.35
  123.9 1.7 collective-permute-start
  125.7 9.8 %collective-permute-done.1 = f32[384,576]{0,1:T(8,128)} collective-permute-done((f32[384,576]{0,1:T(8,128)}, f32[384,576]{0,1:T(8,128)}, u32[]{:S(2)}, u32[]{:S(2)}) %collective-permute-start.1) | collective-permute-done | bytes 884768 | tf_op jit(solution)/shard_map/ppermute | solution.py:14
  135.5 1.5 copy.38
  137.0 0.0 collective-permute-done
  137.0 2.4 copy.36
  139.4 2.7 fusion.15
  142.1 4.7 %all-to-all-start.1 = ((f32[16,24,576]{2,1,0:T(8,128)}), f32[16,24,576]{2,1,0:T(8,128)S(1)}, u32[]{:S(2)}, u32[]{:S(2)}) async-start(f32[16,24,576]{2,1,0:T(8,128)} %bitcast.56), calls=%async_computation.1 | async-start | bytes 1966080 | tf_op jit(solution)/shard_map/all_to_all | solution.py:82
  146.8 1.1 constant_dynamic-slice_fusion
  147.9 0.1 copy.29
  148.0 0.9 reshape.481
  148.8 13.4 %all-to-all-done.1 = f32[16,24,576]{2,1,0:T(8,128)S(1)} async-done(((f32[16,24,576]{2,1,0:T(8,128)}), f32[16,24,576]{2,1,0:T(8,128)S(1)}, u32[]{:S(2)}, u32[]{:S(2)}) %all-to-all-start.1) | async-done | bytes 884768 | tf_op jit(solution)/shard_map/all_to_all | solution.py:82
  162.2 0.1 reduce_sum.9
  162.3 0.1 reshape.485
  162.4 1.6 convolution_convert_fusion
  164.0 0.1 reshape.486
  164.1 3.0 collective-permute-start.3
  167.1 0.0 collective-permute-start.2
  167.1 1.6 collective-permute-done.3
  168.7 1.7 collective-permute-done.2
  170.5 0.1 collective-permute-start.4
  170.6 0.6 constant_dynamic-update-slice_fusion.10
  171.2 0.6 constant_dynamic-update-slice_fusion.9
  171.8 5.8 %collective-permute-done.4 = bf16[72,576]{1,0:T(8,128)(2,1)S(1)} collective-permute-done((bf16[72,576]{1,0:T(8,128)(2,1)S(1)}, bf16[72,576]{1,0:T(8,128)(2,1)S(1)}, u32[]{:S(2)}, u32[]{:S(2)}) %collective-permute-start.4) | collective-permute-done | bytes 82976 | tf_op jit(solution)/shard_map/ppermute | solution.py:98
  177.6 0.9 collective-permute-start.5
  178.6 0.6 constant_dynamic-update-slice_fusion.8
  179.2 0.7 constant_dynamic-update-slice_fusion.7
  179.8 6.0 %collective-permute-done.5 = bf16[144,576]{1,0:T(8,128)(2,1)S(1)} collective-permute-done((bf16[144,576]{1,0:T(8,128)(2,1)S(1)}, bf16[144,576]{1,0:T(8,128)(2,1)S(1)}, u32[]{:S(2)}, u32[]{:S(2)}) %collective-permute-start.5) | collective-permute-done | bytes 165920 | tf_op jit(solution)/shard_map/ppermute | solution.py:98
  185.9 0.7 constant_dynamic-update-slice_fusion.6
  186.6 0.0 collective-permute-start.6
  186.6 9.7 %collective-permute-done.6 = bf16[288,576]{1,0:T(8,128)(2,1)S(1)} collective-permute-done((bf16[288,576]{1,0:T(8,128)(2,1)S(1)}, bf16[288,576]{1,0:T(8,128)(2,1)S(1)}, u32[]{:S(2)}, u32[]{:S(2)}) %collective-permute-start.6) | collective-permute-done | bytes 331808 | tf_op jit(solution)/shard_map/ppermute | solution.py:98
  196.3 0.8 constant_dynamic-update-slice_fusion.5
  197.1 0.0 collective-permute-start.7
  197.1 0.0 copy-done.4
  197.3 16.7 %collective-permute-done.7 = bf16[576,576]{1,0:T(8,128)(2,1)S(1)} collective-permute-done((bf16[576,576]{1,0:T(8,128)(2,1)S(1)}, bf16[576,576]{1,0:T(8,128)(2,1)S(1)}, u32[]{:S(2)}, u32[]{:S(2)}) %collective-permute-start.7) | collective-permute-done | bytes 663584 | tf_op jit(solution)/shard_map/ppermute | solution.py:98
  213.9 0.9 constant_dynamic-update-slice_fusion.11
  214.9 3.9 %gather_fusion.1 = bf16[512,576]{1,0:T(8,128)(2,1)S(1)} fusion(bf16[1152,576]{1,0:T(8,128)(2,1)} %constant_dynamic-update-slice_fusion.11, s32[1024]{0:T(1024)S(1)} %pad_clamp_fusion), kind=kCustom, calls=%fused_computation.1 | custom fusion | bytes 1181696 | tf_op jit(solution)/shard_map/jit(_take)/gather | solution.py:104
  218.8 1.1 copy.39
  219.9 1.1 select_select_fusion
  221.0 3.4 %copy.40 = bf16[512,18,32]{2,1,0:T(8,128)(2,1)} copy(bf16[512,18,32]{0,2,1:T(8,128)(2,1)S(1)} %select_select_fusion) | data formatting | bytes 1179648 | tf_op jit(solution)/shard_map/jit(_where)/select_n | solution.py:105
  224.4 7.8 %fusion.4.spread_ref = f32[512,32,128]{2,1,0:T(8,128)} fusion(bf16[512,18,32]{2,1,0:T(8,128)(2,1)} %copy.40, bf16[512,18,128]{2,0,1:T(8,128)(2,1)S(1)} %bitcast.50), kind=kOutput, calls=%fused_computation.7 | convolution fusion | flops 75497472 | bytes 11337728 | tf_op jit(solution)/shard_map/pjk,pjn->pnk/dot_general | solution.py:107
  232.2 15.4 %shard_map.55 = bf16[32,512,128]{2,1,0:T(8,128)(2,1)S(1)} custom-call(s32[512]{0:T(512)S(1)} %bitcast.52, f32[512,32,128]{2,1,0:T(8,128)} %fusion.4.spread_ref), custom_call_target="tpu_custom_call" | custom-call | tf_op jit(solution)/shard_map/pallas_call | solution.py:44
  247.7 0.0 copy-start.1
  247.7 2.0 copy-done.1
  249.7 10.5 %all_to_all.33 = bf16[16,2,65536]{2,1,0:T(2,128)(2,1)} reshape(bf16[32,512,128]{2,1,0:T(8,128)(2,1)} %copy-done.1) | data formatting | bytes 8388608 | tf_op jit(solution)/shard_map/all_to_all | solution.py:110
  260.1 52.9 %all_to_all.40 = bf16[16,2,65536]{2,1,0:T(2,128)(2,1)S(1)} all-to-all(bf16[16,2,65536]{2,1,0:T(2,128)(2,1)} %all_to_all.33), channel_id=1, replica_groups=mesh['band'=16,'slab'=16] {'band'}, dimensions={0} | all-to-all | bytes 8388608 | tf_op jit(solution)/shard_map/all_to_all | solution.py:110
  313.0 2.0 copy.65
  (12 shorter events, 0.1 us)
Async XLA Ops:
  0.0 94.2 %copy-start = (bf16[1,1,512,18,128]{4,2,3,1,0:T(8,128)(2,1)S(1)}, bf16[1,1,512,18,128]{4,2,3,1,0:T(8,128)(2,1)}, u32[]{:S(2)}) copy-start(bf16[1,1,512,18,128]{4,2,3,1,0:T(8,128)(2,1)} %param.6) | copy-start | bytes 7077892
  0.0 7.3 %copy-start.2 = (s32[1,1,512]{2,1,0:T(1,128)S(1)}, s32[1,1,512]{2,1,0:T(1,128)}, u32[]{:S(2)}) copy-start(s32[1,1,512]{2,1,0:T(1,128)} %param.7) | copy-start | bytes 6148
  0.0 7.3 %copy-start.3 = (s32[1,1,512]{2,1,0:T(1,128)S(1)}, s32[1,1,512]{2,1,0:T(1,128)}, u32[]{:S(2)}) copy-start(s32[1,1,512]{2,1,0:T(1,128)} %param.8) | copy-start | bytes 6148
  0.0 70.5 %all-to-all-start = ((bf16[2,16,65536]{2,0,1:T(2,128)(2,1)}), bf16[2,16,65536]{2,0,1:T(2,128)(2,1)}, u32[]{:S(2)}, u32[]{:S(2)}) async-start(bf16[2,16,65536]{2,0,1:T(2,128)(2,1)} %bitcast.55), calls=%async_computation | async-start | bytes 8388608 | tf_op jit(solution)/shard_map/all_to_all | solution.py:58
  122.7 12.8 %collective-permute-start.1 = (f32[384,576]{0,1:T(8,128)}, f32[384,576]{0,1:T(8,128)}, u32[]{:S(2)}, u32[]{:S(2)}) collective-permute-start(f32[384,576]{0,1:T(8,128)} %copy.37), channel_id=1, source_target_pairs={{0,1},{1,2},{2,3},{3,4},{4,5},{5,6},{6,7},{7,8},{8,9},{9,10},{10,1... | collective-permute-start | bytes 2654216 | tf_op jit(solution)/shard_map/ppermute | solution.py:14
  123.9 13.0 %collective-permute-start = (f32[384,576]{0,1:T(8,128)}, f32[384,576]{0,1:T(8,128)}, u32[]{:S(2)}, u32[]{:S(2)}) collective-permute-start(f32[384,576]{0,1:T(8,128)} %copy.35), channel_id=1, source_target_pairs={{0,15},{1,0},{2,1},{3,2},{4,3},{5,4},{6,5},{7,6},{8,7},{9,8},{10,9... | collective-permute-start | bytes 2654216 | tf_op jit(solution)/shard_map/ppermute | solution.py:14
  142.1 20.1 %all-to-all-start.1 = ((f32[16,24,576]{2,1,0:T(8,128)}), f32[16,24,576]{2,1,0:T(8,128)S(1)}, u32[]{:S(2)}, u32[]{:S(2)}) async-start(f32[16,24,576]{2,1,0:T(8,128)} %bitcast.56), calls=%async_computation.1 | async-start | bytes 1966080 | tf_op jit(solution)/shard_map/all_to_all | solution.py:82
  148.0 49.2 %copy-start.4 = (s32[512,1]{0,1:T(1,128)S(1)}, s32[512,1]{0,1:T(1,128)}, u32[]{:S(2)}) copy-start(s32[512,1]{0,1:T(1,128)} %get-tuple-element.28) | copy-start | bytes 6148
  164.1 4.6 %collective-permute-start.3 = (bf16[24,576]{1,0:T(8,128)(2,1)S(1)}, bf16[24,576]{1,0:T(8,128)(2,1)S(1)}, u32[]{:S(2)}, u32[]{:S(2)}) collective-permute-start(bf16[24,576]{1,0:T(8,128)(2,1)S(1)} %reshape.486), channel_id=1, source_target_pairs={{0,15},{1,0},{2,1},{3,2},{4,3},{5,4},{6,5},{7,6},{8,7},{9,8},{10,9... | collective-permute-start | bytes 82952 | tf_op jit(solution)/shard_map/ppermute | solution.py:14
  167.1 3.3 %collective-permute-start.2 = (bf16[24,576]{1,0:T(8,128)(2,1)S(1)}, bf16[24,576]{1,0:T(8,128)(2,1)S(1)}, u32[]{:S(2)}, u32[]{:S(2)}) collective-permute-start(bf16[24,576]{1,0:T(8,128)(2,1)S(1)} %reshape.486), channel_id=1, source_target_pairs={{0,1},{1,2},{2,3},{3,4},{4,5},{5,6},{6,7},{7,8},{8,9},{9,10},{10,1... | collective-permute-start | bytes 82952 | tf_op jit(solution)/shard_map/ppermute | solution.py:14
  170.5 7.1 %collective-permute-start.4 = (bf16[72,576]{1,0:T(8,128)(2,1)S(1)}, bf16[72,576]{1,0:T(8,128)(2,1)S(1)}, u32[]{:S(2)}, u32[]{:S(2)}) collective-permute-start(bf16[72,576]{1,0:T(8,128)(2,1)S(1)} %pad_maximum_fusion.1), channel_id=1, source_target_pairs={{0,32},{16,48},{32,0},{48,16},{64,96},{80,112},{96,64},{112,80},{1... | collective-permute-start | bytes 248840 | tf_op jit(solution)/shard_map/ppermute | solution.py:98
  177.6 8.2 %collective-permute-start.5 = (bf16[144,576]{1,0:T(8,128)(2,1)S(1)}, bf16[144,576]{1,0:T(8,128)(2,1)S(1)}, u32[]{:S(2)}, u32[]{:S(2)}) collective-permute-start(bf16[144,576]{1,0:T(8,128)(2,1)S(1)} %pad_maximum_fusion), channel_id=1, source_target_pairs={{0,128},{16,144},{32,160},{48,176},{64,192},{80,208},{96,224},{112... | collective-permute-start | bytes 497672 | tf_op jit(solution)/shard_map/ppermute | solution.py:98
  186.6 9.8 %collective-permute-start.6 = (bf16[288,576]{1,0:T(8,128)(2,1)S(1)}, bf16[288,576]{1,0:T(8,128)(2,1)S(1)}, u32[]{:S(2)}, u32[]{:S(2)}) collective-permute-start(bf16[288,576]{1,0:T(8,128)(2,1)S(1)} %get-tuple-element.13), channel_id=1, source_target_pairs={{0,16},{16,0},{32,48},{48,32},{64,80},{80,64},{96,112},{112,96},{1... | collective-permute-start | bytes 995336 | tf_op jit(solution)/shard_map/ppermute | solution.py:98
  197.1 16.8 %collective-permute-start.7 = (bf16[576,576]{1,0:T(8,128)(2,1)S(1)}, bf16[576,576]{1,0:T(8,128)(2,1)S(1)}, u32[]{:S(2)}, u32[]{:S(2)}) collective-permute-start(bf16[576,576]{1,0:T(8,128)(2,1)S(1)} %get-tuple-element.9), channel_id=1, source_target_pairs={{0,64},{16,80},{32,96},{48,112},{64,0},{80,16},{96,32},{112,48},{1... | collective-permute-start | bytes 1990664 | tf_op jit(solution)/shard_map/ppermute | solution.py:98
  247.7 2.0 copy-start.1

commit v7 on v5

--- a/solution.py
+++ b/solution.py
@@ -12,6 +12,26 @@
 def shift(cells, axis, step):
     count = lax.axis_size(axis)
     return lax.ppermute(cells, axis, [(i, (i + step) % count) for i in range(count)])
+
+
+RING = 4
+TILE_ROWS = 16
+
+
+def ring_gather(rows, stride, count, split):
+    def step(cells, delta):
+        pairs = []
+        for i in range(count):
+            coord = (i // stride) % RING
+            pairs.append((i, i + (((coord + delta) % RING) - coord) * stride))
+        return lax.ppermute(cells, "band", pairs)
+
+    left = step(rows, 1)
+    right = step(rows, -1)
+    if split:
+        half = rows.shape[0] // 2
+        return jnp.concatenate([rows, left, right, step(left[:half], 1), step(right[half:], -1)])
+    return jnp.concatenate([rows, left, right, step(left, 1)])
 
 
 def _scatter_body(blk_ref, spread_ref, out_ref, acc_ref):
@@ -85,15 +105,19 @@
         precision=lax.Precision.HIGHEST,
     ).astype(jnp.bfloat16).reshape(share, PROJ * band_count)
     every = jnp.concatenate([shift(dressed, "slab", 1), dressed, shift(dressed, "slab", -1)])
-    mask = 1
-    while mask < band_size:
-        swap = [(i, i ^ mask) for i in range(band_size)]
-        every = jnp.concatenate([every, lax.ppermute(every, "band", swap)])
-        mask *= 2
+    block_rows = -(-every.shape[0] // TILE_ROWS) * TILE_ROWS
+    every = jnp.pad(every, ((0, block_rows - every.shape[0]), (0, 0)))
+    every = ring_gather(every, 1, band_size, False)
+    every = ring_gather(every, RING, band_size, True)
     side_of = index_atom // slot_count
     slot_of = index_atom % slot_count
-    place = lax.axis_index("band") ^ (slot_of // share)
-    row_of = place * (3 * share) + side_of * share + slot_of % share
+    source = slot_of // share
+    me = lax.axis_index("band")
+    order = jnp.array([0, 2, 3, 1], jnp.int32)
+    place_x = order[(source % RING - me % RING) % RING]
+    place_y = order[(source // RING - me // RING) % RING]
+    place = place_y * RING + place_x
+    row_of = place * block_rows + side_of * share + slot_of % share
     chosen = jnp.take(every, jnp.where(is_live, row_of, 0), axis=0)
     chosen = jnp.where(is_live[:, None], chosen, jnp.zeros((), jnp.bfloat16))
     chosen = chosen.reshape(pieces, PROJ, band_count)

time: 316 us -> 306 us (0.968)
  waiting for transfers between devices: 128 us -> 109 us
  starting transfers between devices: 17.4 us -> 24.3 us
    ppermute x4 -> x7, waiting for transfers between devices: 38.6 us -> 19.8 us  [step(): return lax.ppermute(cells, 'band', pairs)]
    ppermute x4 -> x7, starting transfers between devices: 0.7 us -> 7.6 us  [step(): return lax.ppermute(cells, 'band', pairs)]
    unnamed x16 -> x15, local copies, waits for them, and re-layouts: 7.28 us -> 8.25 us
  transfers between devices with their start and end apart: 10 -> 13, of which waited for: 9 -> 9; matrix products, arithmetic and copies ran while one was open for 3% -> 4% of each run, Pallas kernels for 0% -> 0%
where the time goes in v7:
time: 306 us; the launch traced here: 304 us
  waiting for transfers between devices  109 us (36%)
  local copies, waits for them, and re-layouts  70.1 us (23%)
  blocking collectives  52.1 us (17%)
  starting transfers between devices  24.3 us (8%)
  matrix products  20.3 us (7%)
  Pallas kernels  15.4 us (5%)
  other arithmetic  13.2 us (4%)
    all_to_all x1, waiting for transfers between devices, body(): lax.all_to_all(orbitals, 'band', split_axis=1, concat_axis=0, tiled=True)  62.5 us
    all_to_all x1, blocking collectives, body(): lax.all_to_all(result, 'band', split_axis=0, concat_axis=1, tiled=True)  52.1 us
    ppermute x7, waiting for transfers between devices, step(): return lax.ppermute(cells, 'band', pairs)  19.8 us
    reshape x2, local copies, waits for them, and re-layouts, body(): blocks = slab_waves.reshape(band_count, -1, BLOCK)  18.2 us
    pallas_call x1, Pallas kernels, scatter_blocks(): pl.pallas_call(_scatter_body, out_shape=jax.ShapeDtypeStruct((bands, bloc...  15.4 us
    all_to_all x1, waiting for transfers between devices, body(): lax.all_to_all(own_total.reshape(band_size, share, -1), 'band', split_axi...  13.4 us
    ppermute x4, waiting for transfers between devices, shift(): lax.ppermute(cells, axis, [(i, (i + step) % count) for i in range(count)])  13.1 us
    dot_general x1, matrix products, body(): jnp.einsum('pjk,npk->pjn', proj_local, picked, preferred_element_type=jnp...  10.9 us
  transfers between devices with their start and end apart: 13, of which 9 were waited for; matrix products, arithmetic and copies ran while one was open for 4% of the time, Pallas kernels for 0%

profile of v7, /device:TPU:96, one launch (start us, length us, event | category | flops | bytes accessed | tf_op | source)
XLA Modules:
  0.0 304.4 jit_solution(6223173169346706746)
XLA Ops:
  0.0 7.2 %all-to-all-start = ((bf16[2,16,65536]{2,0,1:T(2,128)(2,1)}), bf16[2,16,65536]{2,0,1:T(2,128)(2,1)}, u32[]{:S(2)}, u32[]{:S(2)}) async-start(bf16[2,16,65536]{2,0,1:T(2,128)(2,1)} %bitcast.59), calls=%async_computation | async-start | bytes 8388608 | tf_op jit(solution)/shard_map/all_to_all | solution.py:71
  7.3 0.7 compare_select_fusion
  8.0 62.5 %all-to-all-done = bf16[2,16,65536]{2,0,1:T(2,128)(2,1)} async-done(((bf16[2,16,65536]{2,0,1:T(2,128)(2,1)}), bf16[2,16,65536]{2,0,1:T(2,128)(2,1)}, u32[]{:S(2)}, u32[]{:S(2)}) %all-to-all-start) | async-done | bytes 4194336 | tf_op jit(solution)/shard_map/all_to_all | solution.py:71
  70.5 11.4 %reshape.418 = bf16[32,512,128]{2,1,0:T(8,128)(2,1)} reshape(bf16[16,2,65536]{2,1,0:T(2,128)(2,1)} %bitcast.7) | data formatting | bytes 8388608 | tf_op jit(solution)/shard_map/reshape | solution.py:73
  81.9 6.8 %copy.32 = bf16[32,512,128]{2,0,1:T(8,128)(2,1)} copy(bf16[32,512,128]{2,1,0:T(8,128)(2,1)} %reshape.418) | data formatting | bytes 8388608 | tf_op jit(solution)/shard_map/reshape | solution.py:73
  88.8 5.4 %gather_fusion = bf16[512,32,128]{2,1,0:T(8,128)(2,1)} fusion(bf16[32,512,128]{2,0,1:T(8,128)(2,1)} %copy.32, s32[1024]{0:T(1024)S(1)} %pad_clamp_fusion.1), kind=kCustom, calls=%fused_computation | custom fusion | bytes 8390656 | tf_op jit(solution)/shard_map/jit(_take)/gather | solution.py:81
  94.2 10.9 %fusion.7 = f32[512,18,32]{2,1,0:T(8,128)} fusion(bf16[512,18,128]{2,0,1:T(8,128)(2,1)S(1)} %bitcast.53, bf16[512,32,128]{2,1,0:T(8,128)(2,1)} %gather_fusion, pred[512]{0:T(512)(128)(4,1)S(1)} %compare_and_fusion), kind=kOutput, calls=%fused_computation.10 | convolution fusion | flops 77594624 | bytes 7733760 | tf_op jit(solution)/shard_map/pjk,npk->pjn/dot_general | solution.py:82
  105.1 4.5 %copy.34 = f32[512,18,32]{0,2,1:T(8,128)S(1)} copy(f32[512,18,32]{2,1,0:T(8,128)} %fusion.7) | data formatting | bytes 2359296 | tf_op jit(solution)/shard_map/pjk,npk->pjn/dot_general | solution.py:82
  109.6 1.5 copy.35
  111.1 6.5 %scatter_custom_fusion = f32[1153,576]{1,0:T(8,128)} fusion(s32[512]{0:T(512)S(1)} %bitcast.67, f32[512,576]{1,0:T(8,128)} %copy.35, f32[]{:T(128)} %constant.121.clone.1), kind=kCustom, calls=%fused_computation.12 | custom fusion | flops 294912 | bytes 2657024 | tf_op jit(solution)/shard_map/scatter-add | solution.py:84
  117.6 2.6 fusion.37
  120.2 2.5 copy.38
  122.7 0.0 collective-permute-start.1
  122.7 1.2 copy.36
  124.0 1.7 collective-permute-start
  125.7 9.8 %collective-permute-done.1 = f32[384,576]{0,1:T(8,128)} collective-permute-done((f32[384,576]{0,1:T(8,128)}, f32[384,576]{0,1:T(8,128)}, u32[]{:S(2)}, u32[]{:S(2)}) %collective-permute-start.1) | collective-permute-done | bytes 884768 | tf_op jit(solution)/shard_map/ppermute | solution.py:14
  135.5 1.5 copy.39
  137.0 2.5 copy.37
  139.5 2.7 fusion.15
  142.1 4.7 %all-to-all-start.1 = ((f32[16,24,576]{2,1,0:T(8,128)}), f32[16,24,576]{2,1,0:T(8,128)S(1)}, u32[]{:S(2)}, u32[]{:S(2)}) async-start(f32[16,24,576]{2,1,0:T(8,128)} %bitcast.60), calls=%async_computation.1 | async-start | bytes 1966080 | tf_op jit(solution)/shard_map/all_to_all | solution.py:95
  146.8 1.1 constant_dynamic-slice_fusion
  147.9 0.1 copy.30
  148.0 0.9 reshape.417
  148.9 13.4 %all-to-all-done.1 = f32[16,24,576]{2,1,0:T(8,128)S(1)} async-done(((f32[16,24,576]{2,1,0:T(8,128)}), f32[16,24,576]{2,1,0:T(8,128)S(1)}, u32[]{:S(2)}, u32[]{:S(2)}) %all-to-all-start.1) | async-done | bytes 884768 | tf_op jit(solution)/shard_map/all_to_all | solution.py:95
  162.3 0.1 reduce_sum.9
  162.3 0.1 reshape.421
  162.4 1.6 convolution_convert_fusion
  164.0 0.1 reshape.422
  164.2 3.0 collective-permute-start.3
  167.2 0.0 collective-permute-start.2
  167.2 1.6 collective-permute-done.3
  168.8 1.7 collective-permute-done.2
  170.5 0.7 fusion.20
  171.2 3.3 %collective-permute-start.5 = (bf16[80,576]{1,0:T(8,128)(2,1)S(1)}, bf16[80,576]{1,0:T(8,128)(2,1)S(1)}, u32[]{:S(2)}, u32[]{:S(2)}) collective-permute-start(bf16[80,576]{1,0:T(8,128)(2,1)S(1)} %get-tuple-element.11), channel_id=1, source_target_pairs={{0,48},{16,0},{32,16},{48,32},{64,112},{80,64},{96,80},{112,96},{1... | collective-permute-start | bytes 276488 | tf_op jit(solution)/shard_map/ppermute | solution.py:27
  174.5 3.6 %collective-permute-done.4 = bf16[80,576]{1,0:T(8,128)(2,1)S(1)} collective-permute-done((bf16[80,576]{1,0:T(8,128)(2,1)S(1)}, bf16[80,576]{1,0:T(8,128)(2,1)S(1)}, u32[]{:S(2)}, u32[]{:S(2)}) %collective-permute-start.4) | collective-permute-done | bytes 92192 | tf_op jit(solution)/shard_map/ppermute | solution.py:27
  178.1 0.0 collective-permute-start.6
  178.1 0.7 compare_and_fusion.1
  178.8 0.0 collective-permute-done.5
  178.8 5.4 %collective-permute-done.6 = bf16[80,576]{1,0:T(8,128)(2,1)S(1)} collective-permute-done((bf16[80,576]{1,0:T(8,128)(2,1)S(1)}, bf16[80,576]{1,0:T(8,128)(2,1)S(1)}, u32[]{:S(2)}, u32[]{:S(2)}) %collective-permute-start.6) | collective-permute-done | bytes 92192 | tf_op jit(solution)/shard_map/ppermute | solution.py:27
  184.3 0.3 collective-permute-start.8
  184.6 1.8 collective-permute-start.7
  186.4 0.7 pad_clamp_fusion
  187.0 0.7 constant_dynamic-update-slice_fusion.6
  187.7 0.7 constant_dynamic-update-slice_fusion.5
  188.3 0.7 constant_dynamic-update-slice_fusion.4
  189.0 6.0 %collective-permute-done.8 = bf16[320,576]{1,0:T(8,128)(2,1)S(1)} collective-permute-done((bf16[320,576]{1,0:T(8,128)(2,1)S(1)}, bf16[320,576]{1,0:T(8,128)(2,1)S(1)}, u32[]{:S(2)}, u32[]{:S(2)}) %collective-permute-start.8) | collective-permute-done | bytes 368672 | tf_op jit(solution)/shard_map/ppermute | solution.py:27
  195.0 1.6 collective-permute-start.10
  196.6 0.6 collective-permute-start.9
  197.2 0.8 constant_dynamic-update-slice_fusion.3
  198.0 0.8 constant_dynamic-update-slice_fusion.2
  198.8 4.9 %collective-permute-done.9 = bf16[160,576]{1,0:T(8,128)(2,1)S(1)} collective-permute-done((bf16[160,576]{1,0:T(8,128)(2,1)S(1)}, bf16[160,576]{1,0:T(8,128)(2,1)S(1)}, u32[]{:S(2)}, u32[]{:S(2)}) %collective-permute-start.9) | collective-permute-done | bytes 184352 | tf_op jit(solution)/shard_map/ppermute | solution.py:27
  203.6 0.7 constant_dynamic-update-slice_fusion.1
  204.3 0.7 constant_dynamic-update-slice_fusion
  205.0 4.0 %gather_fusion.1 = bf16[512,576]{1,0:T(8,128)(2,1)S(1)} fusion(bf16[1280,576]{1,0:T(8,128)(2,1)} %constant_dynamic-update-slice_fusion, s32[1024]{0:T(1024)S(1)} %pad_clamp_fusion), kind=kCustom, calls=%fused_computation.1 | custom fusion | bytes 1181696 | tf_op jit(solution)/shard_map/jit(_take)/gather | solution.py:121
  209.0 1.1 copy.40
  210.1 1.1 select_select_fusion
  211.2 3.4 %copy.41 = bf16[512,18,32]{2,1,0:T(8,128)(2,1)} copy(bf16[512,18,32]{0,2,1:T(8,128)(2,1)S(1)} %select_select_fusion) | data formatting | bytes 1179648 | tf_op jit(solution)/shard_map/jit(_where)/select_n | solution.py:122
  214.7 7.8 %fusion.4.spread_ref = f32[512,32,128]{2,1,0:T(8,128)} fusion(bf16[512,18,32]{2,1,0:T(8,128)(2,1)} %copy.41, bf16[512,18,128]{2,0,1:T(8,128)(2,1)S(1)} %bitcast.54), kind=kOutput, calls=%fused_computation.7 | convolution fusion | flops 75497472 | bytes 11337728 | tf_op jit(solution)/shard_map/pjk,pjn->pnk/dot_general | solution.py:124
  222.5 15.4 %shard_map.64 = bf16[32,512,128]{2,1,0:T(8,128)(2,1)S(1)} custom-call(s32[512]{0:T(512)S(1)} %bitcast.56, f32[512,32,128]{2,1,0:T(8,128)} %fusion.4.spread_ref), custom_call_target="tpu_custom_call" | custom-call | tf_op jit(solution)/shard_map/pallas_call | solution.py:57
  237.9 0.0 copy-start.1
  237.9 2.0 copy-done.1
  239.9 10.5 %all_to_all.33 = bf16[16,2,65536]{2,1,0:T(2,128)(2,1)} reshape(bf16[32,512,128]{2,1,0:T(8,128)(2,1)} %copy-done.1) | data formatting | bytes 8388608 | tf_op jit(solution)/shard_map/all_to_all | solution.py:127
  250.4 52.1 %all_to_all.40 = bf16[16,2,65536]{2,1,0:T(2,128)(2,1)S(1)} all-to-all(bf16[16,2,65536]{2,1,0:T(2,128)(2,1)} %all_to_all.33), channel_id=1, replica_groups=mesh['band'=16,'slab'=16] {'band'}, dimensions={0} | all-to-all | bytes 8388608 | tf_op jit(solution)/shard_map/all_to_all | solution.py:127
  302.4 2.0 copy.58
  (18 shorter events, 0.2 us)
Async XLA Ops:
  0.0 94.2 %copy-start = (bf16[1,1,512,18,128]{4,2,3,1,0:T(8,128)(2,1)S(1)}, bf16[1,1,512,18,128]{4,2,3,1,0:T(8,128)(2,1)}, u32[]{:S(2)}) copy-start(bf16[1,1,512,18,128]{4,2,3,1,0:T(8,128)(2,1)} %param.7) | copy-start | bytes 7077892
  0.0 7.3 %copy-start.2 = (s32[1,1,512]{2,1,0:T(1,128)S(1)}, s32[1,1,512]{2,1,0:T(1,128)}, u32[]{:S(2)}) copy-start(s32[1,1,512]{2,1,0:T(1,128)} %param.8) | copy-start | bytes 6148
  0.0 7.3 %copy-start.3 = (s32[1,1,512]{2,1,0:T(1,128)S(1)}, s32[1,1,512]{2,1,0:T(1,128)}, u32[]{:S(2)}) copy-start(s32[1,1,512]{2,1,0:T(1,128)} %param.9) | copy-start | bytes 6148
  0.0 70.5 %all-to-all-start = ((bf16[2,16,65536]{2,0,1:T(2,128)(2,1)}), bf16[2,16,65536]{2,0,1:T(2,128)(2,1)}, u32[]{:S(2)}, u32[]{:S(2)}) async-start(bf16[2,16,65536]{2,0,1:T(2,128)(2,1)} %bitcast.59), calls=%async_computation | async-start | bytes 8388608 | tf_op jit(solution)/shard_map/all_to_all | solution.py:71
  122.7 12.8 %collective-permute-start.1 = (f32[384,576]{0,1:T(8,128)}, f32[384,576]{0,1:T(8,128)}, u32[]{:S(2)}, u32[]{:S(2)}) collective-permute-start(f32[384,576]{0,1:T(8,128)} %copy.38), channel_id=1, source_target_pairs={{0,1},{1,2},{2,3},{3,4},{4,5},{5,6},{6,7},{7,8},{8,9},{9,10},{10,1... | collective-permute-start | bytes 2654216 | tf_op jit(solution)/shard_map/ppermute | solution.py:14
  124.0 13.0 %collective-permute-start = (f32[384,576]{0,1:T(8,128)}, f32[384,576]{0,1:T(8,128)}, u32[]{:S(2)}, u32[]{:S(2)}) collective-permute-start(f32[384,576]{0,1:T(8,128)} %copy.36), channel_id=1, source_target_pairs={{0,15},{1,0},{2,1},{3,2},{4,3},{5,4},{6,5},{7,6},{8,7},{9,8},{10,9... | collective-permute-start | bytes 2654216 | tf_op jit(solution)/shard_map/ppermute | solution.py:14
  142.1 20.1 %all-to-all-start.1 = ((f32[16,24,576]{2,1,0:T(8,128)}), f32[16,24,576]{2,1,0:T(8,128)S(1)}, u32[]{:S(2)}, u32[]{:S(2)}) async-start(f32[16,24,576]{2,1,0:T(8,128)} %bitcast.60), calls=%async_computation.1 | async-start | bytes 1966080 | tf_op jit(solution)/shard_map/all_to_all | solution.py:95
  164.2 4.6 %collective-permute-start.3 = (bf16[24,576]{1,0:T(8,128)(2,1)S(1)}, bf16[24,576]{1,0:T(8,128)(2,1)S(1)}, u32[]{:S(2)}, u32[]{:S(2)}) collective-permute-start(bf16[24,576]{1,0:T(8,128)(2,1)S(1)} %reshape.422), channel_id=1, source_target_pairs={{0,15},{1,0},{2,1},{3,2},{4,3},{5,4},{6,5},{7,6},{8,7},{9,8},{10,9... | collective-permute-start | bytes 82952 | tf_op jit(solution)/shard_map/ppermute | solution.py:14
  167.2 3.3 %collective-permute-start.2 = (bf16[24,576]{1,0:T(8,128)(2,1)S(1)}, bf16[24,576]{1,0:T(8,128)(2,1)S(1)}, u32[]{:S(2)}, u32[]{:S(2)}) collective-permute-start(bf16[24,576]{1,0:T(8,128)(2,1)S(1)} %reshape.422), channel_id=1, source_target_pairs={{0,1},{1,2},{2,3},{3,4},{4,5},{5,6},{6,7},{7,8},{8,9},{9,10},{10,1... | collective-permute-start | bytes 82952 | tf_op jit(solution)/shard_map/ppermute | solution.py:14
  171.2 7.0 %collective-permute-start.4 = (bf16[80,576]{1,0:T(8,128)(2,1)S(1)}, bf16[80,576]{1,0:T(8,128)(2,1)S(1)}, u32[]{:S(2)}, u32[]{:S(2)}) collective-permute-start(bf16[80,576]{1,0:T(8,128)(2,1)S(1)} %get-tuple-element.11), channel_id=1, source_target_pairs={{0,16},{16,32},{32,48},{48,0},{64,80},{80,96},{96,112},{112,64},{1... | collective-permute-start | bytes 276488 | tf_op jit(solution)/shard_map/ppermute | solution.py:27
  171.2 7.6 %collective-permute-start.5 = (bf16[80,576]{1,0:T(8,128)(2,1)S(1)}, bf16[80,576]{1,0:T(8,128)(2,1)S(1)}, u32[]{:S(2)}, u32[]{:S(2)}) collective-permute-start(bf16[80,576]{1,0:T(8,128)(2,1)S(1)} %get-tuple-element.11), channel_id=1, source_target_pairs={{0,48},{16,0},{32,16},{48,32},{64,112},{80,64},{96,80},{112,96},{1... | collective-permute-start | bytes 276488 | tf_op jit(solution)/shard_map/ppermute | solution.py:27
  178.1 6.1 %collective-permute-start.6 = (bf16[80,576]{1,0:T(8,128)(2,1)S(1)}, bf16[80,576]{1,0:T(8,128)(2,1)S(1)}, u32[]{:S(2)}, u32[]{:S(2)}) collective-permute-start(bf16[80,576]{1,0:T(8,128)(2,1)S(1)} %collective-permute-done.4), channel_id=1, source_target_pairs={{0,16},{16,32},{32,48},{48,0},{64,80},{80,96},{96,112},{112,64},{1... | collective-permute-start | bytes 276488 | tf_op jit(solution)/shard_map/ppermute | solution.py:27
  184.3 10.7 %collective-permute-start.8 = (bf16[320,576]{1,0:T(8,128)(2,1)S(1)}, bf16[320,576]{1,0:T(8,128)(2,1)S(1)}, u32[]{:S(2)}, u32[]{:S(2)}) collective-permute-start(bf16[320,576]{1,0:T(8,128)(2,1)S(1)} %pad_maximum_fusion), channel_id=1, source_target_pairs={{0,192},{16,208},{32,224},{48,240},{64,0},{80,16},{96,32},{112,48}... | collective-permute-start | bytes 1105928 | tf_op jit(solution)/shard_map/ppermute | solution.py:27
  184.6 12.0 %collective-permute-start.7 = (bf16[320,576]{1,0:T(8,128)(2,1)S(1)}, bf16[320,576]{1,0:T(8,128)(2,1)S(1)}, u32[]{:S(2)}, u32[]{:S(2)}) collective-permute-start(bf16[320,576]{1,0:T(8,128)(2,1)S(1)} %pad_maximum_fusion), channel_id=1, source_target_pairs={{0,64},{16,80},{32,96},{48,112},{64,128},{80,144},{96,160},{112,17... | collective-permute-start | bytes 1105928 | tf_op jit(solution)/shard_map/ppermute | solution.py:27
  195.0 9.3 %collective-permute-start.10 = (bf16[160,576]{1,0:T(8,128)(2,1)S(1)}, bf16[160,576]{1,0:T(8,128)(2,1)S(1)}, u32[]{:S(2)}, u32[]{:S(2)}) collective-permute-start(bf16[160,576]{1,0:T(8,128)(2,1)S(1)} %slice.45), channel_id=1, source_target_pairs={{0,192},{16,208},{32,224},{48,240},{64,0},{80,16},{96,32},{112,48}... | collective-permute-start | bytes 552968 | tf_op jit(solution)/shard_map/ppermute | solution.py:27
  196.6 7.0 %collective-permute-start.9 = (bf16[160,576]{1,0:T(8,128)(2,1)S(1)}, bf16[160,576]{1,0:T(8,128)(2,1)S(1)}, u32[]{:S(2)}, u32[]{:S(2)}) collective-permute-start(bf16[160,576]{1,0:T(8,128)(2,1)S(1)} %slice.44), channel_id=1, source_target_pairs={{0,64},{16,80},{32,96},{48,112},{64,128},{80,144},{96,160},{112,17... | collective-permute-start | bytes 552968 | tf_op jit(solution)/shard_map/ppermute | solution.py:27
  237.9 2.0 copy-start.1

commit v8 on v7

--- a/solution.py
+++ b/solution.py
@@ -37,19 +37,30 @@
 def _scatter_body(blk_ref, spread_ref, out_ref, acc_ref):
     bands = out_ref.shape[0]
     blocks = out_ref.shape[1]
-    acc_ref[...] = jnp.zeros(acc_ref.shape, jnp.float32)
+    group = spread_ref.shape[0]
+    g = pl.program_id(0)
+
+    @pl.when(g == 0)
+    def _():
+        acc_ref[...] = jnp.zeros(acc_ref.shape, jnp.float32)
 
     def step(p, carry):
-        row = pl.multiple_of(blk_ref[p] * bands, bands)
+        row = pl.multiple_of(blk_ref[g * group + p] * bands, bands)
         acc_ref[pl.ds(row, bands), :] += spread_ref[p]
         return carry
 
-    lax.fori_loop(0, spread_ref.shape[0], step, 0, unroll=2)
-    def emit(n, carry):
-        out_ref[n] = acc_ref[pl.ds(n, blocks, stride=bands), :].astype(out_ref.dtype)
-        return carry
+    lax.fori_loop(0, group, step, 0, unroll=2)
 
-    lax.fori_loop(0, bands, emit, 0)
+    @pl.when(g == pl.num_programs(0) - 1)
+    def _():
+        def emit(n, carry):
+            out_ref[n] = acc_ref[pl.ds(n, blocks, stride=bands), :].astype(out_ref.dtype)
+            return carry
+
+        lax.fori_loop(0, bands, emit, 0)
+
+
+GROUP = 64
 
 
 def scatter_blocks(index_block, spread, block_count):
@@ -57,12 +68,13 @@
     return pl.pallas_call(
         _scatter_body,
         out_shape=jax.ShapeDtypeStruct((bands, block_count, width), jnp.bfloat16),
-        in_specs=[
-            pl.BlockSpec(memory_space=pltpu.SMEM),
-            pl.BlockSpec(memory_space=pltpu.VMEM),
-        ],
-        out_specs=pl.BlockSpec(memory_space=pltpu.VMEM),
-        scratch_shapes=[pltpu.VMEM((block_count * bands, width), jnp.float32)],
+        grid_spec=pltpu.PrefetchScalarGridSpec(
+            num_scalar_prefetch=1,
+            grid=(pieces // GROUP,),
+            in_specs=[pl.BlockSpec((GROUP, bands, width), lambda g, blk: (g, 0, 0))],
+            out_specs=pl.BlockSpec((bands, block_count, width), lambda g, blk: (0, 0, 0)),
+            scratch_shapes=[pltpu.VMEM((block_count * bands, width), jnp.float32)],
+        ),
         compiler_params=pltpu.CompilerParams(vmem_limit_bytes=48 * 1024 * 1024),
     )(index_block, spread)
 

time: 306 us -> 307 us (level)
  no operation moved by 1% of the time
where the time goes in v8:
time: 307 us; the launch traced here: 306 us
  waiting for transfers between devices  109 us (36%)
  local copies, waits for them, and re-layouts  70.1 us (23%)
  blocking collectives  52 us (17%)
  starting transfers between devices  24.3 us (8%)
  matrix products  20.3 us (7%)
  Pallas kernels  16.9 us (6%)
  other arithmetic  13.2 us (4%)
    all_to_all x1, waiting for transfers between devices, body(): lax.all_to_all(orbitals, 'band', split_axis=1, concat_axis=0, tiled=True)  62.5 us
    all_to_all x1, blocking collectives, body(): lax.all_to_all(result, 'band', split_axis=0, concat_axis=1, tiled=True)  52 us
    ppermute x7, waiting for transfers between devices, step(): return lax.ppermute(cells, 'band', pairs)  19.8 us
    reshape x2, local copies, waits for them, and re-layouts, body(): blocks = slab_waves.reshape(band_count, -1, BLOCK)  18.2 us
    pallas_call x1, Pallas kernels, scatter_blocks(): pl.pallas_call(_scatter_body, out_shape=jax.ShapeDtypeStruct((bands, bloc...  16.9 us
    all_to_all x1, waiting for transfers between devices, body(): lax.all_to_all(own_total.reshape(band_size, share, -1), 'band', split_axi...  13.4 us
    ppermute x4, waiting for transfers between devices, shift(): lax.ppermute(cells, axis, [(i, (i + step) % count) for i in range(count)])  13.1 us
    dot_general x1, matrix products, body(): jnp.einsum('pjk,npk->pjn', proj_local, picked, preferred_element_type=jnp...  10.9 us
  transfers between devices with their start and end apart: 13, of which 9 were waited for; matrix products, arithmetic and copies ran while one was open for 4% of the time, Pallas kernels for 0%

profile of v8, /device:TPU:96, one launch (start us, length us, event | category | flops | bytes accessed | tf_op | source)
XLA Modules:
  0.0 305.8 jit_solution(6540039988463461167)
XLA Ops:
  0.0 7.2 %all-to-all-start = ((bf16[2,16,65536]{2,0,1:T(2,128)(2,1)}), bf16[2,16,65536]{2,0,1:T(2,128)(2,1)}, u32[]{:S(2)}, u32[]{:S(2)}) async-start(bf16[2,16,65536]{2,0,1:T(2,128)(2,1)} %bitcast.59), calls=%async_computation | async-start | bytes 8388608 | tf_op jit(solution)/shard_map/all_to_all | solution.py:83
  7.3 0.7 compare_select_fusion
  8.0 62.5 %all-to-all-done = bf16[2,16,65536]{2,0,1:T(2,128)(2,1)} async-done(((bf16[2,16,65536]{2,0,1:T(2,128)(2,1)}), bf16[2,16,65536]{2,0,1:T(2,128)(2,1)}, u32[]{:S(2)}, u32[]{:S(2)}) %all-to-all-start) | async-done | bytes 4194336 | tf_op jit(solution)/shard_map/all_to_all | solution.py:83
  70.5 11.4 %reshape.418 = bf16[32,512,128]{2,1,0:T(8,128)(2,1)} reshape(bf16[16,2,65536]{2,1,0:T(2,128)(2,1)} %bitcast.7) | data formatting | bytes 8388608 | tf_op jit(solution)/shard_map/reshape | solution.py:85
  81.9 6.8 %copy.32 = bf16[32,512,128]{2,0,1:T(8,128)(2,1)} copy(bf16[32,512,128]{2,1,0:T(8,128)(2,1)} %reshape.418) | data formatting | bytes 8388608 | tf_op jit(solution)/shard_map/reshape | solution.py:85
  88.8 5.4 %gather_fusion = bf16[512,32,128]{2,1,0:T(8,128)(2,1)} fusion(bf16[32,512,128]{2,0,1:T(8,128)(2,1)} %copy.32, s32[1024]{0:T(1024)S(1)} %pad_clamp_fusion.1), kind=kCustom, calls=%fused_computation | custom fusion | bytes 8390656 | tf_op jit(solution)/shard_map/jit(_take)/gather | solution.py:93
  94.2 10.9 %fusion.7 = f32[512,18,32]{2,1,0:T(8,128)} fusion(bf16[512,18,128]{2,0,1:T(8,128)(2,1)S(1)} %bitcast.53, bf16[512,32,128]{2,1,0:T(8,128)(2,1)} %gather_fusion, pred[512]{0:T(512)(128)(4,1)S(1)} %compare_and_fusion), kind=kOutput, calls=%fused_computation.10 | convolution fusion | flops 77594624 | bytes 7733760 | tf_op jit(solution)/shard_map/pjk,npk->pjn/dot_general | solution.py:94
  105.1 4.5 %copy.34 = f32[512,18,32]{0,2,1:T(8,128)S(1)} copy(f32[512,18,32]{2,1,0:T(8,128)} %fusion.7) | data formatting | bytes 2359296 | tf_op jit(solution)/shard_map/pjk,npk->pjn/dot_general | solution.py:94
  109.6 1.5 copy.35
  111.1 6.5 %scatter_custom_fusion = f32[1153,576]{1,0:T(8,128)} fusion(s32[512]{0:T(512)S(1)} %bitcast.67, f32[512,576]{1,0:T(8,128)} %copy.35, f32[]{:T(128)} %constant.121.clone.1), kind=kCustom, calls=%fused_computation.12 | custom fusion | flops 294912 | bytes 2657024 | tf_op jit(solution)/shard_map/scatter-add | solution.py:96
  117.6 2.6 fusion.37
  120.2 2.5 copy.38
  122.7 1.2 copy.36
  124.0 1.7 collective-permute-start
  125.7 9.8 %collective-permute-done.1 = f32[384,576]{0,1:T(8,128)} collective-permute-done((f32[384,576]{0,1:T(8,128)}, f32[384,576]{0,1:T(8,128)}, u32[]{:S(2)}, u32[]{:S(2)}) %collective-permute-start.1) | collective-permute-done | bytes 884768 | tf_op jit(solution)/shard_map/ppermute | solution.py:14
  135.5 1.5 copy.39
  137.0 2.5 copy.37
  139.5 2.7 fusion.15
  142.1 4.7 %all-to-all-start.1 = ((f32[16,24,576]{2,1,0:T(8,128)}), f32[16,24,576]{2,1,0:T(8,128)S(1)}, u32[]{:S(2)}, u32[]{:S(2)}) async-start(f32[16,24,576]{2,1,0:T(8,128)} %bitcast.60), calls=%async_computation.1 | async-start | bytes 1966080 | tf_op jit(solution)/shard_map/all_to_all | solution.py:107
  146.8 1.1 constant_dynamic-slice_fusion
  147.9 0.1 copy.30
  148.0 0.9 reshape.417
  148.9 13.4 %all-to-all-done.1 = f32[16,24,576]{2,1,0:T(8,128)S(1)} async-done(((f32[16,24,576]{2,1,0:T(8,128)}), f32[16,24,576]{2,1,0:T(8,128)S(1)}, u32[]{:S(2)}, u32[]{:S(2)}) %all-to-all-start.1) | async-done | bytes 884768 | tf_op jit(solution)/shard_map/all_to_all | solution.py:107
  162.3 0.1 reduce_sum.9
  162.3 0.1 reshape.421
  162.4 1.6 convolution_convert_fusion
  164.0 0.1 reshape.422
  164.2 3.0 collective-permute-start.3
  167.2 1.6 collective-permute-done.3
  168.8 1.7 collective-permute-done.2
  170.5 0.7 fusion.20
  171.2 0.0 collective-permute-start.4
  171.2 3.3 %collective-permute-start.5 = (bf16[80,576]{1,0:T(8,128)(2,1)S(1)}, bf16[80,576]{1,0:T(8,128)(2,1)S(1)}, u32[]{:S(2)}, u32[]{:S(2)}) collective-permute-start(bf16[80,576]{1,0:T(8,128)(2,1)S(1)} %get-tuple-element.11), channel_id=1, source_target_pairs={{0,48},{16,0},{32,16},{48,32},{64,112},{80,64},{96,80},{112,96},{1... | collective-permute-start | bytes 276488 | tf_op jit(solution)/shard_map/ppermute | solution.py:27
  174.5 3.6 %collective-permute-done.4 = bf16[80,576]{1,0:T(8,128)(2,1)S(1)} collective-permute-done((bf16[80,576]{1,0:T(8,128)(2,1)S(1)}, bf16[80,576]{1,0:T(8,128)(2,1)S(1)}, u32[]{:S(2)}, u32[]{:S(2)}) %collective-permute-start.4) | collective-permute-done | bytes 92192 | tf_op jit(solution)/shard_map/ppermute | solution.py:27
  178.1 0.0 collective-permute-start.6
  178.1 0.7 compare_and_fusion.1
  178.8 0.0 collective-permute-done.5
  178.8 5.4 %collective-permute-done.6 = bf16[80,576]{1,0:T(8,128)(2,1)S(1)} collective-permute-done((bf16[80,576]{1,0:T(8,128)(2,1)S(1)}, bf16[80,576]{1,0:T(8,128)(2,1)S(1)}, u32[]{:S(2)}, u32[]{:S(2)}) %collective-permute-start.6) | collective-permute-done | bytes 92192 | tf_op jit(solution)/shard_map/ppermute | solution.py:27
  184.2 0.3 collective-permute-start.8
  184.6 1.8 collective-permute-start.7
  186.3 0.7 pad_clamp_fusion
  187.0 0.7 constant_dynamic-update-slice_fusion.6
  187.7 0.7 constant_dynamic-update-slice_fusion.5
  188.3 0.7 constant_dynamic-update-slice_fusion.4
  189.0 5.9 %collective-permute-done.8 = bf16[320,576]{1,0:T(8,128)(2,1)S(1)} collective-permute-done((bf16[320,576]{1,0:T(8,128)(2,1)S(1)}, bf16[320,576]{1,0:T(8,128)(2,1)S(1)}, u32[]{:S(2)}, u32[]{:S(2)}) %collective-permute-start.8) | collective-permute-done | bytes 368672 | tf_op jit(solution)/shard_map/ppermute | solution.py:27
  194.9 1.6 collective-permute-start.10
  196.5 0.0 collective-permute-done.7
  196.5 0.6 collective-permute-start.9
  197.1 0.8 constant_dynamic-update-slice_fusion.3
  197.9 0.8 constant_dynamic-update-slice_fusion.2
  198.7 4.9 %collective-permute-done.9 = bf16[160,576]{1,0:T(8,128)(2,1)S(1)} collective-permute-done((bf16[160,576]{1,0:T(8,128)(2,1)S(1)}, bf16[160,576]{1,0:T(8,128)(2,1)S(1)}, u32[]{:S(2)}, u32[]{:S(2)}) %collective-permute-start.9) | collective-permute-done | bytes 184352 | tf_op jit(solution)/shard_map/ppermute | solution.py:27
  203.6 0.7 constant_dynamic-update-slice_fusion.1
  204.3 0.7 constant_dynamic-update-slice_fusion
  205.0 4.0 %gather_fusion.1 = bf16[512,576]{1,0:T(8,128)(2,1)S(1)} fusion(bf16[1280,576]{1,0:T(8,128)(2,1)} %constant_dynamic-update-slice_fusion, s32[1024]{0:T(1024)S(1)} %pad_clamp_fusion), kind=kCustom, calls=%fused_computation.1 | custom fusion | bytes 1181696 | tf_op jit(solution)/shard_map/jit(_take)/gather | solution.py:133
  209.0 1.1 copy.40
  210.0 1.1 select_select_fusion
  211.2 3.4 %copy.41 = bf16[512,18,32]{2,1,0:T(8,128)(2,1)} copy(bf16[512,18,32]{0,2,1:T(8,128)(2,1)S(1)} %select_select_fusion) | data formatting | bytes 1179648 | tf_op jit(solution)/shard_map/jit(_where)/select_n | solution.py:134
  214.6 7.8 %fusion.4.spread_ref = f32[512,32,128]{2,1,0:T(8,128)} fusion(bf16[512,18,32]{2,1,0:T(8,128)(2,1)} %copy.41, bf16[512,18,128]{2,0,1:T(8,128)(2,1)S(1)} %bitcast.54), kind=kOutput, calls=%fused_computation.7 | convolution fusion | flops 75497472 | bytes 11337728 | tf_op jit(solution)/shard_map/pjk,pjn->pnk/dot_general | solution.py:136
  222.4 16.9 %shard_map.64 = bf16[32,512,128]{2,1,0:T(8,128)(2,1)S(1)} custom-call(s32[512]{0:T(512)S(1)} %bitcast.56, f32[512,32,128]{2,1,0:T(8,128)} %fusion.4.spread_ref), custom_call_target="tpu_custom_call" | custom-call | tf_op jit(solution)/shard_map/pallas_call | solution.py:68
  239.3 0.0 copy-start.1
  239.3 2.0 copy-done.1
  241.3 10.5 %all_to_all.33 = bf16[16,2,65536]{2,1,0:T(2,128)(2,1)} reshape(bf16[32,512,128]{2,1,0:T(8,128)(2,1)} %copy-done.1) | data formatting | bytes 8388608 | tf_op jit(solution)/shard_map/all_to_all | solution.py:139
  251.8 52.0 %all_to_all.40 = bf16[16,2,65536]{2,1,0:T(2,128)(2,1)S(1)} all-to-all(bf16[16,2,65536]{2,1,0:T(2,128)(2,1)} %all_to_all.33), channel_id=1, replica_groups=mesh['band'=16,'slab'=16] {'band'}, dimensions={0} | all-to-all | bytes 8388608 | tf_op jit(solution)/shard_map/all_to_all | solution.py:139
  303.8 2.0 copy.58
  (18 shorter events, 0.2 us)
Async XLA Ops:
  0.0 94.2 %copy-start = (bf16[1,1,512,18,128]{4,2,3,1,0:T(8,128)(2,1)S(1)}, bf16[1,1,512,18,128]{4,2,3,1,0:T(8,128)(2,1)}, u32[]{:S(2)}) copy-start(bf16[1,1,512,18,128]{4,2,3,1,0:T(8,128)(2,1)} %param.7) | copy-start | bytes 7077892
  0.0 7.3 %copy-start.2 = (s32[1,1,512]{2,1,0:T(1,128)S(1)}, s32[1,1,512]{2,1,0:T(1,128)}, u32[]{:S(2)}) copy-start(s32[1,1,512]{2,1,0:T(1,128)} %param.8) | copy-start | bytes 6148
  0.0 7.3 %copy-start.3 = (s32[1,1,512]{2,1,0:T(1,128)S(1)}, s32[1,1,512]{2,1,0:T(1,128)}, u32[]{:S(2)}) copy-start(s32[1,1,512]{2,1,0:T(1,128)} %param.9) | copy-start | bytes 6148
  0.0 70.5 %all-to-all-start = ((bf16[2,16,65536]{2,0,1:T(2,128)(2,1)}), bf16[2,16,65536]{2,0,1:T(2,128)(2,1)}, u32[]{:S(2)}, u32[]{:S(2)}) async-start(bf16[2,16,65536]{2,0,1:T(2,128)(2,1)} %bitcast.59), calls=%async_computation | async-start | bytes 8388608 | tf_op jit(solution)/shard_map/all_to_all | solution.py:83
  122.7 12.8 %collective-permute-start.1 = (f32[384,576]{0,1:T(8,128)}, f32[384,576]{0,1:T(8,128)}, u32[]{:S(2)}, u32[]{:S(2)}) collective-permute-start(f32[384,576]{0,1:T(8,128)} %copy.38), channel_id=1, source_target_pairs={{0,1},{1,2},{2,3},{3,4},{4,5},{5,6},{6,7},{7,8},{8,9},{9,10},{10,1... | collective-permute-start | bytes 2654216 | tf_op jit(solution)/shard_map/ppermute | solution.py:14
  124.0 13.0 %collective-permute-start = (f32[384,576]{0,1:T(8,128)}, f32[384,576]{0,1:T(8,128)}, u32[]{:S(2)}, u32[]{:S(2)}) collective-permute-start(f32[384,576]{0,1:T(8,128)} %copy.36), channel_id=1, source_target_pairs={{0,15},{1,0},{2,1},{3,2},{4,3},{5,4},{6,5},{7,6},{8,7},{9,8},{10,9... | collective-permute-start | bytes 2654216 | tf_op jit(solution)/shard_map/ppermute | solution.py:14
  142.1 20.1 %all-to-all-start.1 = ((f32[16,24,576]{2,1,0:T(8,128)}), f32[16,24,576]{2,1,0:T(8,128)S(1)}, u32[]{:S(2)}, u32[]{:S(2)}) async-start(f32[16,24,576]{2,1,0:T(8,128)} %bitcast.60), calls=%async_computation.1 | async-start | bytes 1966080 | tf_op jit(solution)/shard_map/all_to_all | solution.py:107
  164.2 4.6 %collective-permute-start.3 = (bf16[24,576]{1,0:T(8,128)(2,1)S(1)}, bf16[24,576]{1,0:T(8,128)(2,1)S(1)}, u32[]{:S(2)}, u32[]{:S(2)}) collective-permute-start(bf16[24,576]{1,0:T(8,128)(2,1)S(1)} %reshape.422), channel_id=1, source_target_pairs={{0,15},{1,0},{2,1},{3,2},{4,3},{5,4},{6,5},{7,6},{8,7},{9,8},{10,9... | collective-permute-start | bytes 82952 | tf_op jit(solution)/shard_map/ppermute | solution.py:14
  167.2 3.3 %collective-permute-start.2 = (bf16[24,576]{1,0:T(8,128)(2,1)S(1)}, bf16[24,576]{1,0:T(8,128)(2,1)S(1)}, u32[]{:S(2)}, u32[]{:S(2)}) collective-permute-start(bf16[24,576]{1,0:T(8,128)(2,1)S(1)} %reshape.422), channel_id=1, source_target_pairs={{0,1},{1,2},{2,3},{3,4},{4,5},{5,6},{6,7},{7,8},{8,9},{9,10},{10,1... | collective-permute-start | bytes 82952 | tf_op jit(solution)/shard_map/ppermute | solution.py:14
  171.2 6.9 %collective-permute-start.4 = (bf16[80,576]{1,0:T(8,128)(2,1)S(1)}, bf16[80,576]{1,0:T(8,128)(2,1)S(1)}, u32[]{:S(2)}, u32[]{:S(2)}) collective-permute-start(bf16[80,576]{1,0:T(8,128)(2,1)S(1)} %get-tuple-element.11), channel_id=1, source_target_pairs={{0,16},{16,32},{32,48},{48,0},{64,80},{80,96},{96,112},{112,64},{1... | collective-permute-start | bytes 276488 | tf_op jit(solution)/shard_map/ppermute | solution.py:27
  171.2 7.6 %collective-permute-start.5 = (bf16[80,576]{1,0:T(8,128)(2,1)S(1)}, bf16[80,576]{1,0:T(8,128)(2,1)S(1)}, u32[]{:S(2)}, u32[]{:S(2)}) collective-permute-start(bf16[80,576]{1,0:T(8,128)(2,1)S(1)} %get-tuple-element.11), channel_id=1, source_target_pairs={{0,48},{16,0},{32,16},{48,32},{64,112},{80,64},{96,80},{112,96},{1... | collective-permute-start | bytes 276488 | tf_op jit(solution)/shard_map/ppermute | solution.py:27
  178.1 6.1 %collective-permute-start.6 = (bf16[80,576]{1,0:T(8,128)(2,1)S(1)}, bf16[80,576]{1,0:T(8,128)(2,1)S(1)}, u32[]{:S(2)}, u32[]{:S(2)}) collective-permute-start(bf16[80,576]{1,0:T(8,128)(2,1)S(1)} %collective-permute-done.4), channel_id=1, source_target_pairs={{0,16},{16,32},{32,48},{48,0},{64,80},{80,96},{96,112},{112,64},{1... | collective-permute-start | bytes 276488 | tf_op jit(solution)/shard_map/ppermute | solution.py:27
  184.2 10.7 %collective-permute-start.8 = (bf16[320,576]{1,0:T(8,128)(2,1)S(1)}, bf16[320,576]{1,0:T(8,128)(2,1)S(1)}, u32[]{:S(2)}, u32[]{:S(2)}) collective-permute-start(bf16[320,576]{1,0:T(8,128)(2,1)S(1)} %pad_maximum_fusion), channel_id=1, source_target_pairs={{0,192},{16,208},{32,224},{48,240},{64,0},{80,16},{96,32},{112,48}... | collective-permute-start | bytes 1105928 | tf_op jit(solution)/shard_map/ppermute | solution.py:27
  184.6 11.9 %collective-permute-start.7 = (bf16[320,576]{1,0:T(8,128)(2,1)S(1)}, bf16[320,576]{1,0:T(8,128)(2,1)S(1)}, u32[]{:S(2)}, u32[]{:S(2)}) collective-permute-start(bf16[320,576]{1,0:T(8,128)(2,1)S(1)} %pad_maximum_fusion), channel_id=1, source_target_pairs={{0,64},{16,80},{32,96},{48,112},{64,128},{80,144},{96,160},{112,17... | collective-permute-start | bytes 1105928 | tf_op jit(solution)/shard_map/ppermute | solution.py:27
  194.9 9.3 %collective-permute-start.10 = (bf16[160,576]{1,0:T(8,128)(2,1)S(1)}, bf16[160,576]{1,0:T(8,128)(2,1)S(1)}, u32[]{:S(2)}, u32[]{:S(2)}) collective-permute-start(bf16[160,576]{1,0:T(8,128)(2,1)S(1)} %slice.45), channel_id=1, source_target_pairs={{0,192},{16,208},{32,224},{48,240},{64,0},{80,16},{96,32},{112,48}... | collective-permute-start | bytes 552968 | tf_op jit(solution)/shard_map/ppermute | solution.py:27
  196.5 7.0 %collective-permute-start.9 = (bf16[160,576]{1,0:T(8,128)(2,1)S(1)}, bf16[160,576]{1,0:T(8,128)(2,1)S(1)}, u32[]{:S(2)}, u32[]{:S(2)}) collective-permute-start(bf16[160,576]{1,0:T(8,128)(2,1)S(1)} %slice.44), channel_id=1, source_target_pairs={{0,64},{16,80},{32,96},{48,112},{64,128},{80,144},{96,160},{112,17... | collective-permute-start | bytes 552968 | tf_op jit(solution)/shard_map/ppermute | solution.py:27
  239.3 2.0 copy-start.1

commit v9 on v7

--- a/solution.py
+++ b/solution.py
@@ -44,7 +44,7 @@
         acc_ref[pl.ds(row, bands), :] += spread_ref[p]
         return carry
 
-    lax.fori_loop(0, spread_ref.shape[0], step, 0, unroll=2)
+    lax.fori_loop(0, spread_ref.shape[0], step, 0, unroll=8)
     def emit(n, carry):
         out_ref[n] = acc_ref[pl.ds(n, blocks, stride=bands), :].astype(out_ref.dtype)
         return carry

time: 306 us -> 305 us (level)
  no operation moved by 1% of the time
where the time goes in v9:
time: 305 us; the launch traced here: 304 us
  waiting for transfers between devices  109 us (36%)
  local copies, waits for them, and re-layouts  70.1 us (23%)
  blocking collectives  52.1 us (17%)
  starting transfers between devices  24.3 us (8%)
  matrix products  20.3 us (7%)
  Pallas kernels  14.6 us (5%)
  other arithmetic  13.2 us (4%)
    all_to_all x1, waiting for transfers between devices, body(): lax.all_to_all(orbitals, 'band', split_axis=1, concat_axis=0, tiled=True)  62.5 us
    all_to_all x1, blocking collectives, body(): lax.all_to_all(result, 'band', split_axis=0, concat_axis=1, tiled=True)  52.1 us
    ppermute x7, waiting for transfers between devices, step(): return lax.ppermute(cells, 'band', pairs)  19.8 us
    reshape x2, local copies, waits for them, and re-layouts, body(): blocks = slab_waves.reshape(band_count, -1, BLOCK)  18.2 us
    pallas_call x1, Pallas kernels, scatter_blocks(): pl.pallas_call(_scatter_body, out_shape=jax.ShapeDtypeStruct((bands, bloc...  14.6 us
    all_to_all x1, waiting for transfers between devices, body(): lax.all_to_all(own_total.reshape(band_size, share, -1), 'band', split_axi...  13.4 us
    ppermute x4, waiting for transfers between devices, shift(): lax.ppermute(cells, axis, [(i, (i + step) % count) for i in range(count)])  13.1 us
    dot_general x1, matrix products, body(): jnp.einsum('pjk,npk->pjn', proj_local, picked, preferred_element_type=jnp...  10.9 us
  transfers between devices with their start and end apart: 13, of which 9 were waited for; matrix products, arithmetic and copies ran while one was open for 4% of the time, Pallas kernels for 0%

profile of v9, /device:TPU:96, one launch (start us, length us, event | category | flops | bytes accessed | tf_op | source)
XLA Modules:
  0.0 303.6 jit_solution(31113124644626486)
XLA Ops:
  0.0 7.2 %all-to-all-start = ((bf16[2,16,65536]{2,0,1:T(2,128)(2,1)}), bf16[2,16,65536]{2,0,1:T(2,128)(2,1)}, u32[]{:S(2)}, u32[]{:S(2)}) async-start(bf16[2,16,65536]{2,0,1:T(2,128)(2,1)} %bitcast.59), calls=%async_computation | async-start | bytes 8388608 | tf_op jit(solution)/shard_map/all_to_all | solution.py:71
  7.3 0.7 compare_select_fusion
  8.0 62.5 %all-to-all-done = bf16[2,16,65536]{2,0,1:T(2,128)(2,1)} async-done(((bf16[2,16,65536]{2,0,1:T(2,128)(2,1)}), bf16[2,16,65536]{2,0,1:T(2,128)(2,1)}, u32[]{:S(2)}, u32[]{:S(2)}) %all-to-all-start) | async-done | bytes 4194336 | tf_op jit(solution)/shard_map/all_to_all | solution.py:71
  70.5 11.4 %reshape.418 = bf16[32,512,128]{2,1,0:T(8,128)(2,1)} reshape(bf16[16,2,65536]{2,1,0:T(2,128)(2,1)} %bitcast.7) | data formatting | bytes 8388608 | tf_op jit(solution)/shard_map/reshape | solution.py:73
  81.9 6.8 %copy.32 = bf16[32,512,128]{2,0,1:T(8,128)(2,1)} copy(bf16[32,512,128]{2,1,0:T(8,128)(2,1)} %reshape.418) | data formatting | bytes 8388608 | tf_op jit(solution)/shard_map/reshape | solution.py:73
  88.8 5.4 %gather_fusion = bf16[512,32,128]{2,1,0:T(8,128)(2,1)} fusion(bf16[32,512,128]{2,0,1:T(8,128)(2,1)} %copy.32, s32[1024]{0:T(1024)S(1)} %pad_clamp_fusion.1), kind=kCustom, calls=%fused_computation | custom fusion | bytes 8390656 | tf_op jit(solution)/shard_map/jit(_take)/gather | solution.py:81
  94.2 10.9 %fusion.7 = f32[512,18,32]{2,1,0:T(8,128)} fusion(bf16[512,18,128]{2,0,1:T(8,128)(2,1)S(1)} %bitcast.53, bf16[512,32,128]{2,1,0:T(8,128)(2,1)} %gather_fusion, pred[512]{0:T(512)(128)(4,1)S(1)} %compare_and_fusion), kind=kOutput, calls=%fused_computation.10 | convolution fusion | flops 77594624 | bytes 7733760 | tf_op jit(solution)/shard_map/pjk,npk->pjn/dot_general | solution.py:82
  105.1 4.5 %copy.34 = f32[512,18,32]{0,2,1:T(8,128)S(1)} copy(f32[512,18,32]{2,1,0:T(8,128)} %fusion.7) | data formatting | bytes 2359296 | tf_op jit(solution)/shard_map/pjk,npk->pjn/dot_general | solution.py:82
  109.6 1.5 copy.35
  111.1 6.5 %scatter_custom_fusion = f32[1153,576]{1,0:T(8,128)} fusion(s32[512]{0:T(512)S(1)} %bitcast.67, f32[512,576]{1,0:T(8,128)} %copy.35, f32[]{:T(128)} %constant.121.clone.1), kind=kCustom, calls=%fused_computation.12 | custom fusion | flops 294912 | bytes 2657024 | tf_op jit(solution)/shard_map/scatter-add | solution.py:84
  117.6 2.6 fusion.37
  120.2 2.5 copy.38
  122.7 0.0 collective-permute-start.1
  122.7 1.2 copy.36
  124.0 1.7 collective-permute-start
  125.7 9.8 %collective-permute-done.1 = f32[384,576]{0,1:T(8,128)} collective-permute-done((f32[384,576]{0,1:T(8,128)}, f32[384,576]{0,1:T(8,128)}, u32[]{:S(2)}, u32[]{:S(2)}) %collective-permute-start.1) | collective-permute-done | bytes 884768 | tf_op jit(solution)/shard_map/ppermute | solution.py:14
  135.5 1.5 copy.39
  137.0 0.0 collective-permute-done
  137.0 2.5 copy.37
  139.5 2.7 fusion.15
  142.1 4.7 %all-to-all-start.1 = ((f32[16,24,576]{2,1,0:T(8,128)}), f32[16,24,576]{2,1,0:T(8,128)S(1)}, u32[]{:S(2)}, u32[]{:S(2)}) async-start(f32[16,24,576]{2,1,0:T(8,128)} %bitcast.60), calls=%async_computation.1 | async-start | bytes 1966080 | tf_op jit(solution)/shard_map/all_to_all | solution.py:95
  146.8 1.1 constant_dynamic-slice_fusion
  147.9 0.1 copy.30
  148.0 0.9 reshape.417
  148.9 13.4 %all-to-all-done.1 = f32[16,24,576]{2,1,0:T(8,128)S(1)} async-done(((f32[16,24,576]{2,1,0:T(8,128)}), f32[16,24,576]{2,1,0:T(8,128)S(1)}, u32[]{:S(2)}, u32[]{:S(2)}) %all-to-all-start.1) | async-done | bytes 884768 | tf_op jit(solution)/shard_map/all_to_all | solution.py:95
  162.3 0.1 reduce_sum.9
  162.3 0.1 reshape.421
  162.4 1.6 convolution_convert_fusion
  164.0 0.1 reshape.422
  164.2 3.0 collective-permute-start.3
  167.2 1.6 collective-permute-done.3
  168.8 1.7 collective-permute-done.2
  170.5 0.7 fusion.20
  171.2 0.0 collective-permute-start.4
  171.2 3.3 %collective-permute-start.5 = (bf16[80,576]{1,0:T(8,128)(2,1)S(1)}, bf16[80,576]{1,0:T(8,128)(2,1)S(1)}, u32[]{:S(2)}, u32[]{:S(2)}) collective-permute-start(bf16[80,576]{1,0:T(8,128)(2,1)S(1)} %get-tuple-element.11), channel_id=1, source_target_pairs={{0,48},{16,0},{32,16},{48,32},{64,112},{80,64},{96,80},{112,96},{1... | collective-permute-start | bytes 276488 | tf_op jit(solution)/shard_map/ppermute | solution.py:27
  174.5 3.6 %collective-permute-done.4 = bf16[80,576]{1,0:T(8,128)(2,1)S(1)} collective-permute-done((bf16[80,576]{1,0:T(8,128)(2,1)S(1)}, bf16[80,576]{1,0:T(8,128)(2,1)S(1)}, u32[]{:S(2)}, u32[]{:S(2)}) %collective-permute-start.4) | collective-permute-done | bytes 92192 | tf_op jit(solution)/shard_map/ppermute | solution.py:27
  178.1 0.0 collective-permute-start.6
  178.1 0.7 compare_and_fusion.1
  178.8 5.4 %collective-permute-done.6 = bf16[80,576]{1,0:T(8,128)(2,1)S(1)} collective-permute-done((bf16[80,576]{1,0:T(8,128)(2,1)S(1)}, bf16[80,576]{1,0:T(8,128)(2,1)S(1)}, u32[]{:S(2)}, u32[]{:S(2)}) %collective-permute-start.6) | collective-permute-done | bytes 92192 | tf_op jit(solution)/shard_map/ppermute | solution.py:27
  184.3 0.3 collective-permute-start.8
  184.6 1.8 collective-permute-start.7
  186.4 0.7 pad_clamp_fusion
  187.0 0.7 constant_dynamic-update-slice_fusion.6
  187.7 0.7 constant_dynamic-update-slice_fusion.5
  188.3 0.7 constant_dynamic-update-slice_fusion.4
  189.0 6.0 %collective-permute-done.8 = bf16[320,576]{1,0:T(8,128)(2,1)S(1)} collective-permute-done((bf16[320,576]{1,0:T(8,128)(2,1)S(1)}, bf16[320,576]{1,0:T(8,128)(2,1)S(1)}, u32[]{:S(2)}, u32[]{:S(2)}) %collective-permute-start.8) | collective-permute-done | bytes 368672 | tf_op jit(solution)/shard_map/ppermute | solution.py:27
  195.0 1.6 collective-permute-start.10
  196.6 0.6 collective-permute-start.9
  197.2 0.8 constant_dynamic-update-slice_fusion.3
  198.0 0.8 constant_dynamic-update-slice_fusion.2
  198.8 4.9 %collective-permute-done.9 = bf16[160,576]{1,0:T(8,128)(2,1)S(1)} collective-permute-done((bf16[160,576]{1,0:T(8,128)(2,1)S(1)}, bf16[160,576]{1,0:T(8,128)(2,1)S(1)}, u32[]{:S(2)}, u32[]{:S(2)}) %collective-permute-start.9) | collective-permute-done | bytes 184352 | tf_op jit(solution)/shard_map/ppermute | solution.py:27
  203.6 0.7 constant_dynamic-update-slice_fusion.1
  204.3 0.7 constant_dynamic-update-slice_fusion
  205.0 4.0 %gather_fusion.1 = bf16[512,576]{1,0:T(8,128)(2,1)S(1)} fusion(bf16[1280,576]{1,0:T(8,128)(2,1)} %constant_dynamic-update-slice_fusion, s32[1024]{0:T(1024)S(1)} %pad_clamp_fusion), kind=kCustom, calls=%fused_computation.1 | custom fusion | bytes 1181696 | tf_op jit(solution)/shard_map/jit(_take)/gather | solution.py:121
  209.0 1.1 copy.40
  210.1 1.1 select_select_fusion
  211.2 3.4 %copy.41 = bf16[512,18,32]{2,1,0:T(8,128)(2,1)} copy(bf16[512,18,32]{0,2,1:T(8,128)(2,1)S(1)} %select_select_fusion) | data formatting | bytes 1179648 | tf_op jit(solution)/shard_map/jit(_where)/select_n | solution.py:122
  214.7 7.8 %fusion.4.spread_ref = f32[512,32,128]{2,1,0:T(8,128)} fusion(bf16[512,18,32]{2,1,0:T(8,128)(2,1)} %copy.41, bf16[512,18,128]{2,0,1:T(8,128)(2,1)S(1)} %bitcast.54), kind=kOutput, calls=%fused_computation.7 | convolution fusion | flops 75497472 | bytes 11337728 | tf_op jit(solution)/shard_map/pjk,pjn->pnk/dot_general | solution.py:124
  222.5 14.6 %shard_map.64 = bf16[32,512,128]{2,1,0:T(8,128)(2,1)S(1)} custom-call(s32[512]{0:T(512)S(1)} %bitcast.56, f32[512,32,128]{2,1,0:T(8,128)} %fusion.4.spread_ref), custom_call_target="tpu_custom_call" | custom-call | tf_op jit(solution)/shard_map/pallas_call | solution.py:57
  237.1 0.0 copy-start.1
  237.1 2.0 copy-done.1
  239.1 10.5 %all_to_all.33 = bf16[16,2,65536]{2,1,0:T(2,128)(2,1)} reshape(bf16[32,512,128]{2,1,0:T(8,128)(2,1)} %copy-done.1) | data formatting | bytes 8388608 | tf_op jit(solution)/shard_map/all_to_all | solution.py:127
  249.5 52.1 %all_to_all.40 = bf16[16,2,65536]{2,1,0:T(2,128)(2,1)S(1)} all-to-all(bf16[16,2,65536]{2,1,0:T(2,128)(2,1)} %all_to_all.33), channel_id=1, replica_groups=mesh['band'=16,'slab'=16] {'band'}, dimensions={0} | all-to-all | bytes 8388608 | tf_op jit(solution)/shard_map/all_to_all | solution.py:127
  301.6 2.0 copy.58
  (18 shorter events, 0.2 us)
Async XLA Ops:
  0.0 94.2 %copy-start = (bf16[1,1,512,18,128]{4,2,3,1,0:T(8,128)(2,1)S(1)}, bf16[1,1,512,18,128]{4,2,3,1,0:T(8,128)(2,1)}, u32[]{:S(2)}) copy-start(bf16[1,1,512,18,128]{4,2,3,1,0:T(8,128)(2,1)} %param.7) | copy-start | bytes 7077892
  0.0 7.3 %copy-start.2 = (s32[1,1,512]{2,1,0:T(1,128)S(1)}, s32[1,1,512]{2,1,0:T(1,128)}, u32[]{:S(2)}) copy-start(s32[1,1,512]{2,1,0:T(1,128)} %param.8) | copy-start | bytes 6148
  0.0 7.3 %copy-start.3 = (s32[1,1,512]{2,1,0:T(1,128)S(1)}, s32[1,1,512]{2,1,0:T(1,128)}, u32[]{:S(2)}) copy-start(s32[1,1,512]{2,1,0:T(1,128)} %param.9) | copy-start | bytes 6148
  0.0 70.5 %all-to-all-start = ((bf16[2,16,65536]{2,0,1:T(2,128)(2,1)}), bf16[2,16,65536]{2,0,1:T(2,128)(2,1)}, u32[]{:S(2)}, u32[]{:S(2)}) async-start(bf16[2,16,65536]{2,0,1:T(2,128)(2,1)} %bitcast.59), calls=%async_computation | async-start | bytes 8388608 | tf_op jit(solution)/shard_map/all_to_all | solution.py:71
  122.7 12.8 %collective-permute-start.1 = (f32[384,576]{0,1:T(8,128)}, f32[384,576]{0,1:T(8,128)}, u32[]{:S(2)}, u32[]{:S(2)}) collective-permute-start(f32[384,576]{0,1:T(8,128)} %copy.38), channel_id=1, source_target_pairs={{0,1},{1,2},{2,3},{3,4},{4,5},{5,6},{6,7},{7,8},{8,9},{9,10},{10,1... | collective-permute-start | bytes 2654216 | tf_op jit(solution)/shard_map/ppermute | solution.py:14
  124.0 13.0 %collective-permute-start = (f32[384,576]{0,1:T(8,128)}, f32[384,576]{0,1:T(8,128)}, u32[]{:S(2)}, u32[]{:S(2)}) collective-permute-start(f32[384,576]{0,1:T(8,128)} %copy.36), channel_id=1, source_target_pairs={{0,15},{1,0},{2,1},{3,2},{4,3},{5,4},{6,5},{7,6},{8,7},{9,8},{10,9... | collective-permute-start | bytes 2654216 | tf_op jit(solution)/shard_map/ppermute | solution.py:14
  142.1 20.1 %all-to-all-start.1 = ((f32[16,24,576]{2,1,0:T(8,128)}), f32[16,24,576]{2,1,0:T(8,128)S(1)}, u32[]{:S(2)}, u32[]{:S(2)}) async-start(f32[16,24,576]{2,1,0:T(8,128)} %bitcast.60), calls=%async_computation.1 | async-start | bytes 1966080 | tf_op jit(solution)/shard_map/all_to_all | solution.py:95
  164.2 4.6 %collective-permute-start.3 = (bf16[24,576]{1,0:T(8,128)(2,1)S(1)}, bf16[24,576]{1,0:T(8,128)(2,1)S(1)}, u32[]{:S(2)}, u32[]{:S(2)}) collective-permute-start(bf16[24,576]{1,0:T(8,128)(2,1)S(1)} %reshape.422), channel_id=1, source_target_pairs={{0,15},{1,0},{2,1},{3,2},{4,3},{5,4},{6,5},{7,6},{8,7},{9,8},{10,9... | collective-permute-start | bytes 82952 | tf_op jit(solution)/shard_map/ppermute | solution.py:14
  167.2 3.3 %collective-permute-start.2 = (bf16[24,576]{1,0:T(8,128)(2,1)S(1)}, bf16[24,576]{1,0:T(8,128)(2,1)S(1)}, u32[]{:S(2)}, u32[]{:S(2)}) collective-permute-start(bf16[24,576]{1,0:T(8,128)(2,1)S(1)} %reshape.422), channel_id=1, source_target_pairs={{0,1},{1,2},{2,3},{3,4},{4,5},{5,6},{6,7},{7,8},{8,9},{9,10},{10,1... | collective-permute-start | bytes 82952 | tf_op jit(solution)/shard_map/ppermute | solution.py:14
  171.2 7.0 %collective-permute-start.4 = (bf16[80,576]{1,0:T(8,128)(2,1)S(1)}, bf16[80,576]{1,0:T(8,128)(2,1)S(1)}, u32[]{:S(2)}, u32[]{:S(2)}) collective-permute-start(bf16[80,576]{1,0:T(8,128)(2,1)S(1)} %get-tuple-element.11), channel_id=1, source_target_pairs={{0,16},{16,32},{32,48},{48,0},{64,80},{80,96},{96,112},{112,64},{1... | collective-permute-start | bytes 276488 | tf_op jit(solution)/shard_map/ppermute | solution.py:27
  171.2 7.6 %collective-permute-start.5 = (bf16[80,576]{1,0:T(8,128)(2,1)S(1)}, bf16[80,576]{1,0:T(8,128)(2,1)S(1)}, u32[]{:S(2)}, u32[]{:S(2)}) collective-permute-start(bf16[80,576]{1,0:T(8,128)(2,1)S(1)} %get-tuple-element.11), channel_id=1, source_target_pairs={{0,48},{16,0},{32,16},{48,32},{64,112},{80,64},{96,80},{112,96},{1... | collective-permute-start | bytes 276488 | tf_op jit(solution)/shard_map/ppermute | solution.py:27
  178.1 6.1 %collective-permute-start.6 = (bf16[80,576]{1,0:T(8,128)(2,1)S(1)}, bf16[80,576]{1,0:T(8,128)(2,1)S(1)}, u32[]{:S(2)}, u32[]{:S(2)}) collective-permute-start(bf16[80,576]{1,0:T(8,128)(2,1)S(1)} %collective-permute-done.4), channel_id=1, source_target_pairs={{0,16},{16,32},{32,48},{48,0},{64,80},{80,96},{96,112},{112,64},{1... | collective-permute-start | bytes 276488 | tf_op jit(solution)/shard_map/ppermute | solution.py:27
  184.3 10.7 %collective-permute-start.8 = (bf16[320,576]{1,0:T(8,128)(2,1)S(1)}, bf16[320,576]{1,0:T(8,128)(2,1)S(1)}, u32[]{:S(2)}, u32[]{:S(2)}) collective-permute-start(bf16[320,576]{1,0:T(8,128)(2,1)S(1)} %pad_maximum_fusion), channel_id=1, source_target_pairs={{0,192},{16,208},{32,224},{48,240},{64,0},{80,16},{96,32},{112,48}... | collective-permute-start | bytes 1105928 | tf_op jit(solution)/shard_map/ppermute | solution.py:27
  184.6 12.0 %collective-permute-start.7 = (bf16[320,576]{1,0:T(8,128)(2,1)S(1)}, bf16[320,576]{1,0:T(8,128)(2,1)S(1)}, u32[]{:S(2)}, u32[]{:S(2)}) collective-permute-start(bf16[320,576]{1,0:T(8,128)(2,1)S(1)} %pad_maximum_fusion), channel_id=1, source_target_pairs={{0,64},{16,80},{32,96},{48,112},{64,128},{80,144},{96,160},{112,17... | collective-permute-start | bytes 1105928 | tf_op jit(solution)/shard_map/ppermute | solution.py:27
  195.0 9.3 %collective-permute-start.10 = (bf16[160,576]{1,0:T(8,128)(2,1)S(1)}, bf16[160,576]{1,0:T(8,128)(2,1)S(1)}, u32[]{:S(2)}, u32[]{:S(2)}) collective-permute-start(bf16[160,576]{1,0:T(8,128)(2,1)S(1)} %slice.45), channel_id=1, source_target_pairs={{0,192},{16,208},{32,224},{48,240},{64,0},{80,16},{96,32},{112,48}... | collective-permute-start | bytes 552968 | tf_op jit(solution)/shard_map/ppermute | solution.py:27
  196.6 7.0 %collective-permute-start.9 = (bf16[160,576]{1,0:T(8,128)(2,1)S(1)}, bf16[160,576]{1,0:T(8,128)(2,1)S(1)}, u32[]{:S(2)}, u32[]{:S(2)}) collective-permute-start(bf16[160,576]{1,0:T(8,128)(2,1)S(1)} %slice.44), channel_id=1, source_target_pairs={{0,64},{16,80},{32,96},{48,112},{64,128},{80,144},{96,160},{112,17... | collective-permute-start | bytes 552968 | tf_op jit(solution)/shard_map/ppermute | solution.py:27
  237.1 2.0 copy-start.1

commit v10 on v9

--- a/solution.py
+++ b/solution.py
@@ -78,7 +78,10 @@
     pieces = index_block.shape[0]
     slot_count = coupling.shape[0]
     is_live = index_atom >= 0
-    picked = jnp.take(blocks, index_block, axis=1)
+    onehot = (index_block[:, None] == jnp.arange(block_count)[None, :]).astype(jnp.bfloat16)
+    picked = jnp.einsum(
+        "pb,nbk->npk", onehot, blocks, preferred_element_type=jnp.float32
+    ).astype(jnp.bfloat16)
     projected = jnp.einsum("pjk,npk->pjn", proj_local, picked, preferred_element_type=jnp.float32)
     target = jnp.where(is_live, index_atom, 3 * slot_count)
     partial_value = jax.ops.segment_sum(

time: 305 us -> 293 us (0.961)
  local copies, waits for them, and re-layouts: 70.1 us -> 57.7 us
    reshape x2 -> x1, local copies, waits for them, and re-layouts: 18.2 us -> 11.4 us  [body(): blocks = slab_waves.reshape(band_count, -1, BLOCK)]
    gather x1 -> x0, local copies, waits for them, and re-layouts: 5.42 us -> none  [body(): picked = jnp.take(blocks, index_block, axis=1)]
    dot_general x0 -> x1, matrix products: none -> 4.57 us  [body(): jnp.einsum('pb,nbk->npk', onehot, blocks, preferred_element_type=jnp.floa...]
    dot_general x1, matrix products: 10.9 us -> 7.26 us  [body(): jnp.einsum('pjk,npk->pjn', proj_local, picked, preferred_element_type=jnp...]
where the time goes in v10:
time: 293 us; the launch traced here: 292 us
  waiting for transfers between devices  109 us (37%)
  local copies, waits for them, and re-layouts  57.7 us (20%)
  blocking collectives  52.1 us (18%)
  starting transfers between devices  24.5 us (8%)
  matrix products  21.2 us (7%)
  Pallas kernels  14.6 us (5%)
  other arithmetic  13 us (4%)
    all_to_all x1, waiting for transfers between devices, body(): lax.all_to_all(orbitals, 'band', split_axis=1, concat_axis=0, tiled=True)  62.6 us
    all_to_all x1, blocking collectives, body(): lax.all_to_all(result, 'band', split_axis=0, concat_axis=1, tiled=True)  52.1 us
    ppermute x7, waiting for transfers between devices, step(): return lax.ppermute(cells, 'band', pairs)  19.8 us
    pallas_call x1, Pallas kernels, scatter_blocks(): pl.pallas_call(_scatter_body, out_shape=jax.ShapeDtypeStruct((bands, bloc...  14.6 us
    all_to_all x1, waiting for transfers between devices, body(): lax.all_to_all(own_total.reshape(band_size, share, -1), 'band', split_axi...  13.4 us
    ppermute x4, waiting for transfers between devices, shift(): lax.ppermute(cells, axis, [(i, (i + step) % count) for i in range(count)])  13.1 us
    reshape x1, local copies, waits for them, and re-layouts, body(): blocks = slab_waves.reshape(band_count, -1, BLOCK)  11.4 us
    all_to_all x1, local copies, waits for them, and re-layouts, body(): lax.all_to_all(result, 'band', split_axis=0, concat_axis=1, tiled=True)  10.5 us
  transfers between devices with their start and end apart: 13, of which 9 were waited for; matrix products, arithmetic and copies ran while one was open for 4% of the time, Pallas kernels for 0%

profile of v10, /device:TPU:96, one launch (start us, length us, event | category | flops | bytes accessed | tf_op | source)
XLA Modules:
  0.0 292.1 jit_solution(8983606913963570360)
XLA Ops:
  0.0 7.2 %all-to-all-start = ((bf16[2,16,65536]{2,0,1:T(2,128)(2,1)}), bf16[2,16,65536]{2,0,1:T(2,128)(2,1)}, u32[]{:S(2)}, u32[]{:S(2)}) async-start(bf16[2,16,65536]{2,0,1:T(2,128)(2,1)} %bitcast.57), calls=%async_computation | async-start | bytes 8388608 | tf_op jit(solution)/shard_map/all_to_all | solution.py:71
  7.3 0.7 compare_select_fusion
  7.9 62.6 %all-to-all-done = bf16[2,16,65536]{2,0,1:T(2,128)(2,1)} async-done(((bf16[2,16,65536]{2,0,1:T(2,128)(2,1)}), bf16[2,16,65536]{2,0,1:T(2,128)(2,1)}, u32[]{:S(2)}, u32[]{:S(2)}) %all-to-all-start) | async-done | bytes 4194336 | tf_op jit(solution)/shard_map/all_to_all | solution.py:71
  70.5 11.4 %reshape.385 = bf16[32,512,128]{2,1,0:T(8,128)(2,1)} reshape(bf16[16,2,65536]{2,1,0:T(2,128)(2,1)} %bitcast.8) | data formatting | bytes 8388608 | tf_op jit(solution)/shard_map/reshape | solution.py:73
  81.9 4.6 %convert_bitcast_fusion = bf16[32,512,128]{2,1,0:T(8,128)(2,1)S(1)} fusion(bf16[32,512,128]{2,1,0:T(8,128)(2,1)} %reshape.385, s32[512]{0:T(512)S(1)} %bitcast.53), kind=kOutput, calls=%fused_computation.4 | convolution fusion | flops 2149842944 | bytes 8390656 | tf_op jit(solution)/shard_map/pb,nbk->npk/dot_general | solution.py:82
  86.5 7.3 %fusion.5 = f32[512,18,32]{2,1,0:T(8,128)} fusion(bf16[512,18,128]{2,0,1:T(8,128)(2,1)S(1)} %bitcast.51, bf16[32,512,128]{2,1,0:T(8,128)(2,1)S(1)} %convert_bitcast_fusion), kind=kOutput, calls=%fused_computation.8 | convolution fusion | flops 75497472 | bytes 7733248 | tf_op jit(solution)/shard_map/pjk,npk->pjn/dot_general | solution.py:85
  93.8 4.5 %copy.33 = f32[512,18,32]{0,2,1:T(8,128)S(1)} copy(f32[512,18,32]{2,1,0:T(8,128)} %fusion.5) | data formatting | bytes 2359296 | tf_op jit(solution)/shard_map/pjk,npk->pjn/dot_general | solution.py:85
  98.2 1.5 copy.34
  99.7 6.4 %scatter_custom_fusion = f32[1153,576]{1,0:T(8,128)} fusion(s32[512]{0:T(512)S(1)} %bitcast.64, f32[512,576]{1,0:T(8,128)} %copy.34, f32[]{:T(128)} %constant.109.clone.1), kind=kCustom, calls=%fused_computation.9 | custom fusion | flops 294912 | bytes 2657024 | tf_op jit(solution)/shard_map/scatter-add | solution.py:87
  106.1 2.6 fusion.36
  108.7 2.5 copy.37
  111.2 0.0 collective-permute-start.1
  111.2 1.2 copy.35
  112.4 1.7 collective-permute-start
  114.2 9.8 %collective-permute-done.1 = f32[384,576]{0,1:T(8,128)} collective-permute-done((f32[384,576]{0,1:T(8,128)}, f32[384,576]{0,1:T(8,128)}, u32[]{:S(2)}, u32[]{:S(2)}) %collective-permute-start.1) | collective-permute-done | bytes 884768 | tf_op jit(solution)/shard_map/ppermute | solution.py:14
  124.0 1.5 copy.38
  125.5 0.0 collective-permute-done
  125.5 2.5 copy.36
  127.9 2.7 fusion.14
  130.6 4.7 %all-to-all-start.1 = ((f32[16,24,576]{2,1,0:T(8,128)}), f32[16,24,576]{2,1,0:T(8,128)S(1)}, u32[]{:S(2)}, u32[]{:S(2)}) async-start(f32[16,24,576]{2,1,0:T(8,128)} %bitcast.58), calls=%async_computation.1 | async-start | bytes 1966080 | tf_op jit(solution)/shard_map/all_to_all | solution.py:98
  135.3 1.1 constant_dynamic-slice_fusion
  136.4 0.1 copy.29
  136.5 0.9 reshape.384
  137.3 13.4 %all-to-all-done.1 = f32[16,24,576]{2,1,0:T(8,128)S(1)} async-done(((f32[16,24,576]{2,1,0:T(8,128)}), f32[16,24,576]{2,1,0:T(8,128)S(1)}, u32[]{:S(2)}, u32[]{:S(2)}) %all-to-all-start.1) | async-done | bytes 884768 | tf_op jit(solution)/shard_map/all_to_all | solution.py:98
  150.7 0.1 reduce_sum.9
  150.8 0.1 reshape.388
  150.9 1.6 convolution_convert_fusion
  152.5 0.1 reshape.389
  152.6 3.0 %collective-permute-start.3 = (bf16[24,576]{1,0:T(8,128)(2,1)S(1)}, bf16[24,576]{1,0:T(8,128)(2,1)S(1)}, u32[]{:S(2)}, u32[]{:S(2)}) collective-permute-start(bf16[24,576]{1,0:T(8,128)(2,1)S(1)} %reshape.389), channel_id=1, source_target_pairs={{0,15},{1,0},{2,1},{3,2},{4,3},{5,4},{6,5},{7,6},{8,7},{9,8},{10,9... | collective-permute-start | bytes 82952 | tf_op jit(solution)/shard_map/ppermute | solution.py:14
  155.6 0.0 collective-permute-start.2
  155.7 1.6 collective-permute-done.3
  157.2 1.7 collective-permute-done.2
  159.0 0.7 fusion.20
  159.6 0.0 collective-permute-start.4
  159.7 3.3 %collective-permute-start.5 = (bf16[80,576]{1,0:T(8,128)(2,1)S(1)}, bf16[80,576]{1,0:T(8,128)(2,1)S(1)}, u32[]{:S(2)}, u32[]{:S(2)}) collective-permute-start(bf16[80,576]{1,0:T(8,128)(2,1)S(1)} %get-tuple-element.11), channel_id=1, source_target_pairs={{0,48},{16,0},{32,16},{48,32},{64,112},{80,64},{96,80},{112,96},{1... | collective-permute-start | bytes 276488 | tf_op jit(solution)/shard_map/ppermute | solution.py:27
  163.0 3.6 %collective-permute-done.4 = bf16[80,576]{1,0:T(8,128)(2,1)S(1)} collective-permute-done((bf16[80,576]{1,0:T(8,128)(2,1)S(1)}, bf16[80,576]{1,0:T(8,128)(2,1)S(1)}, u32[]{:S(2)}, u32[]{:S(2)}) %collective-permute-start.4) | collective-permute-done | bytes 92192 | tf_op jit(solution)/shard_map/ppermute | solution.py:27
  166.6 0.7 compare_and_fusion
  167.3 5.4 %collective-permute-done.6 = bf16[80,576]{1,0:T(8,128)(2,1)S(1)} collective-permute-done((bf16[80,576]{1,0:T(8,128)(2,1)S(1)}, bf16[80,576]{1,0:T(8,128)(2,1)S(1)}, u32[]{:S(2)}, u32[]{:S(2)}) %collective-permute-start.6) | collective-permute-done | bytes 92192 | tf_op jit(solution)/shard_map/ppermute | solution.py:27
  172.7 0.3 collective-permute-start.8
  173.0 1.8 collective-permute-start.7
  174.8 0.7 pad_clamp_fusion
  175.5 0.7 constant_dynamic-update-slice_fusion.6
  176.2 0.7 constant_dynamic-update-slice_fusion.5
  176.8 0.7 constant_dynamic-update-slice_fusion.4
  177.5 6.0 %collective-permute-done.8 = bf16[320,576]{1,0:T(8,128)(2,1)S(1)} collective-permute-done((bf16[320,576]{1,0:T(8,128)(2,1)S(1)}, bf16[320,576]{1,0:T(8,128)(2,1)S(1)}, u32[]{:S(2)}, u32[]{:S(2)}) %collective-permute-start.8) | collective-permute-done | bytes 368672 | tf_op jit(solution)/shard_map/ppermute | solution.py:27
  183.4 1.6 collective-permute-start.10
  185.0 0.0 collective-permute-done.7
  185.0 0.8 collective-permute-start.9
  185.9 0.8 constant_dynamic-update-slice_fusion.3
  186.7 0.8 constant_dynamic-update-slice_fusion.2
  187.4 4.9 %collective-permute-done.9 = bf16[160,576]{1,0:T(8,128)(2,1)S(1)} collective-permute-done((bf16[160,576]{1,0:T(8,128)(2,1)S(1)}, bf16[160,576]{1,0:T(8,128)(2,1)S(1)}, u32[]{:S(2)}, u32[]{:S(2)}) %collective-permute-start.9) | collective-permute-done | bytes 184352 | tf_op jit(solution)/shard_map/ppermute | solution.py:27
  192.3 0.7 constant_dynamic-update-slice_fusion.1
  193.0 0.7 constant_dynamic-update-slice_fusion
  193.7 3.8 %gather_fusion = bf16[512,576]{1,0:T(8,128)(2,1)S(1)} fusion(bf16[1280,576]{1,0:T(8,128)(2,1)} %constant_dynamic-update-slice_fusion, s32[1024]{0:T(1024)S(1)} %pad_clamp_fusion), kind=kCustom, calls=%fused_computation | custom fusion | bytes 1181696 | tf_op jit(solution)/shard_map/jit(_take)/gather | solution.py:124
  197.5 1.1 copy.39
  198.6 1.1 select_select_fusion
  199.7 3.4 %copy.40 = bf16[512,18,32]{2,1,0:T(8,128)(2,1)} copy(bf16[512,18,32]{0,2,1:T(8,128)(2,1)S(1)} %select_select_fusion) | data formatting | bytes 1179648 | tf_op jit(solution)/shard_map/jit(_where)/select_n | solution.py:125
  203.1 7.8 %fusion.2.spread_ref = f32[512,32,128]{2,1,0:T(8,128)} fusion(bf16[512,18,32]{2,1,0:T(8,128)(2,1)} %copy.40, bf16[512,18,128]{2,0,1:T(8,128)(2,1)S(1)} %bitcast.52), kind=kOutput, calls=%fused_computation.5 | convolution fusion | flops 75497472 | bytes 11337728 | tf_op jit(solution)/shard_map/pjk,pjn->pnk/dot_general | solution.py:127
  210.9 14.6 %shard_map.64 = bf16[32,512,128]{2,1,0:T(8,128)(2,1)S(1)} custom-call(s32[512]{0:T(512)S(1)} %bitcast.54, f32[512,32,128]{2,1,0:T(8,128)} %fusion.2.spread_ref), custom_call_target="tpu_custom_call" | custom-call | tf_op jit(solution)/shard_map/pallas_call | solution.py:57
  225.5 0.0 copy-start.1
  225.5 2.0 copy-done.1
  227.5 10.5 %all_to_all.33 = bf16[16,2,65536]{2,1,0:T(2,128)(2,1)} reshape(bf16[32,512,128]{2,1,0:T(8,128)(2,1)} %copy-done.1) | data formatting | bytes 8388608 | tf_op jit(solution)/shard_map/all_to_all | solution.py:130
  238.0 52.1 %all_to_all.40 = bf16[16,2,65536]{2,1,0:T(2,128)(2,1)S(1)} all-to-all(bf16[16,2,65536]{2,1,0:T(2,128)(2,1)} %all_to_all.33), channel_id=1, replica_groups=mesh['band'=16,'slab'=16] {'band'}, dimensions={0} | all-to-all | bytes 8388608 | tf_op jit(solution)/shard_map/all_to_all | solution.py:130
  290.1 2.0 copy.61
  (14 shorter events, 0.1 us)
Async XLA Ops:
  0.0 86.5 %copy-start = (bf16[1,1,512,18,128]{4,2,3,1,0:T(8,128)(2,1)S(1)}, bf16[1,1,512,18,128]{4,2,3,1,0:T(8,128)(2,1)}, u32[]{:S(2)}) copy-start(bf16[1,1,512,18,128]{4,2,3,1,0:T(8,128)(2,1)} %param.7) | copy-start | bytes 7077892
  0.0 7.3 %copy-start.3 = (s32[1,1,512]{2,1,0:T(1,128)S(1)}, s32[1,1,512]{2,1,0:T(1,128)}, u32[]{:S(2)}) copy-start(s32[1,1,512]{2,1,0:T(1,128)} %param.9) | copy-start | bytes 6148
  0.0 70.5 %all-to-all-start = ((bf16[2,16,65536]{2,0,1:T(2,128)(2,1)}), bf16[2,16,65536]{2,0,1:T(2,128)(2,1)}, u32[]{:S(2)}, u32[]{:S(2)}) async-start(bf16[2,16,65536]{2,0,1:T(2,128)(2,1)} %bitcast.57), calls=%async_computation | async-start | bytes 8388608 | tf_op jit(solution)/shard_map/all_to_all | solution.py:71
  70.5 11.4 %copy-start.2 = (s32[1,1,512]{2,1,0:T(1,128)S(1)}, s32[1,1,512]{2,1,0:T(1,128)}, u32[]{:S(2)}) copy-start(s32[1,1,512]{2,1,0:T(1,128)} %param.8) | copy-start | bytes 6148
  111.2 12.8 %collective-permute-start.1 = (f32[384,576]{0,1:T(8,128)}, f32[384,576]{0,1:T(8,128)}, u32[]{:S(2)}, u32[]{:S(2)}) collective-permute-start(f32[384,576]{0,1:T(8,128)} %copy.37), channel_id=1, source_target_pairs={{0,1},{1,2},{2,3},{3,4},{4,5},{5,6},{6,7},{7,8},{8,9},{9,10},{10,1... | collective-permute-start | bytes 2654216 | tf_op jit(solution)/shard_map/ppermute | solution.py:14
  112.4 13.0 %collective-permute-start = (f32[384,576]{0,1:T(8,128)}, f32[384,576]{0,1:T(8,128)}, u32[]{:S(2)}, u32[]{:S(2)}) collective-permute-start(f32[384,576]{0,1:T(8,128)} %copy.35), channel_id=1, source_target_pairs={{0,15},{1,0},{2,1},{3,2},{4,3},{5,4},{6,5},{7,6},{8,7},{9,8},{10,9... | collective-permute-start | bytes 2654216 | tf_op jit(solution)/shard_map/ppermute | solution.py:14
  130.6 20.1 %all-to-all-start.1 = ((f32[16,24,576]{2,1,0:T(8,128)}), f32[16,24,576]{2,1,0:T(8,128)S(1)}, u32[]{:S(2)}, u32[]{:S(2)}) async-start(f32[16,24,576]{2,1,0:T(8,128)} %bitcast.58), calls=%async_computation.1 | async-start | bytes 1966080 | tf_op jit(solution)/shard_map/all_to_all | solution.py:98
  152.6 4.6 %collective-permute-start.3 = (bf16[24,576]{1,0:T(8,128)(2,1)S(1)}, bf16[24,576]{1,0:T(8,128)(2,1)S(1)}, u32[]{:S(2)}, u32[]{:S(2)}) collective-permute-start(bf16[24,576]{1,0:T(8,128)(2,1)S(1)} %reshape.389), channel_id=1, source_target_pairs={{0,15},{1,0},{2,1},{3,2},{4,3},{5,4},{6,5},{7,6},{8,7},{9,8},{10,9... | collective-permute-start | bytes 82952 | tf_op jit(solution)/shard_map/ppermute | solution.py:14
  155.6 3.3 %collective-permute-start.2 = (bf16[24,576]{1,0:T(8,128)(2,1)S(1)}, bf16[24,576]{1,0:T(8,128)(2,1)S(1)}, u32[]{:S(2)}, u32[]{:S(2)}) collective-permute-start(bf16[24,576]{1,0:T(8,128)(2,1)S(1)} %reshape.389), channel_id=1, source_target_pairs={{0,1},{1,2},{2,3},{3,4},{4,5},{5,6},{6,7},{7,8},{8,9},{9,10},{10,1... | collective-permute-start | bytes 82952 | tf_op jit(solution)/shard_map/ppermute | solution.py:14
  159.6 7.0 %collective-permute-start.4 = (bf16[80,576]{1,0:T(8,128)(2,1)S(1)}, bf16[80,576]{1,0:T(8,128)(2,1)S(1)}, u32[]{:S(2)}, u32[]{:S(2)}) collective-permute-start(bf16[80,576]{1,0:T(8,128)(2,1)S(1)} %get-tuple-element.11), channel_id=1, source_target_pairs={{0,16},{16,32},{32,48},{48,0},{64,80},{80,96},{96,112},{112,64},{1... | collective-permute-start | bytes 276488 | tf_op jit(solution)/shard_map/ppermute | solution.py:27
  159.7 7.6 %collective-permute-start.5 = (bf16[80,576]{1,0:T(8,128)(2,1)S(1)}, bf16[80,576]{1,0:T(8,128)(2,1)S(1)}, u32[]{:S(2)}, u32[]{:S(2)}) collective-permute-start(bf16[80,576]{1,0:T(8,128)(2,1)S(1)} %get-tuple-element.11), channel_id=1, source_target_pairs={{0,48},{16,0},{32,16},{48,32},{64,112},{80,64},{96,80},{112,96},{1... | collective-permute-start | bytes 276488 | tf_op jit(solution)/shard_map/ppermute | solution.py:27
  166.6 6.1 %collective-permute-start.6 = (bf16[80,576]{1,0:T(8,128)(2,1)S(1)}, bf16[80,576]{1,0:T(8,128)(2,1)S(1)}, u32[]{:S(2)}, u32[]{:S(2)}) collective-permute-start(bf16[80,576]{1,0:T(8,128)(2,1)S(1)} %collective-permute-done.4), channel_id=1, source_target_pairs={{0,16},{16,32},{32,48},{48,0},{64,80},{80,96},{96,112},{112,64},{1... | collective-permute-start | bytes 276488 | tf_op jit(solution)/shard_map/ppermute | solution.py:27
  172.7 10.7 %collective-permute-start.8 = (bf16[320,576]{1,0:T(8,128)(2,1)S(1)}, bf16[320,576]{1,0:T(8,128)(2,1)S(1)}, u32[]{:S(2)}, u32[]{:S(2)}) collective-permute-start(bf16[320,576]{1,0:T(8,128)(2,1)S(1)} %pad_maximum_fusion), channel_id=1, source_target_pairs={{0,192},{16,208},{32,224},{48,240},{64,0},{80,16},{96,32},{112,48}... | collective-permute-start | bytes 1105928 | tf_op jit(solution)/shard_map/ppermute | solution.py:27
  173.0 12.0 %collective-permute-start.7 = (bf16[320,576]{1,0:T(8,128)(2,1)S(1)}, bf16[320,576]{1,0:T(8,128)(2,1)S(1)}, u32[]{:S(2)}, u32[]{:S(2)}) collective-permute-start(bf16[320,576]{1,0:T(8,128)(2,1)S(1)} %pad_maximum_fusion), channel_id=1, source_target_pairs={{0,64},{16,80},{32,96},{48,112},{64,128},{80,144},{96,160},{112,17... | collective-permute-start | bytes 1105928 | tf_op jit(solution)/shard_map/ppermute | solution.py:27
  183.4 9.6 %collective-permute-start.10 = (bf16[160,576]{1,0:T(8,128)(2,1)S(1)}, bf16[160,576]{1,0:T(8,128)(2,1)S(1)}, u32[]{:S(2)}, u32[]{:S(2)}) collective-permute-start(bf16[160,576]{1,0:T(8,128)(2,1)S(1)} %slice.43), channel_id=1, source_target_pairs={{0,192},{16,208},{32,224},{48,240},{64,0},{80,16},{96,32},{112,48}... | collective-permute-start | bytes 552968 | tf_op jit(solution)/shard_map/ppermute | solution.py:27
  185.0 7.3 %collective-permute-start.9 = (bf16[160,576]{1,0:T(8,128)(2,1)S(1)}, bf16[160,576]{1,0:T(8,128)(2,1)S(1)}, u32[]{:S(2)}, u32[]{:S(2)}) collective-permute-start(bf16[160,576]{1,0:T(8,128)(2,1)S(1)} %slice.42), channel_id=1, source_target_pairs={{0,64},{16,80},{32,96},{48,112},{64,128},{80,144},{96,160},{112,17... | collective-permute-start | bytes 552968 | tf_op jit(solution)/shard_map/ppermute | solution.py:27
  225.5 2.0 copy-start.1

commit v11 on v10

--- a/solution.py
+++ b/solution.py
@@ -121,8 +121,10 @@
     place_y = order[(source // RING - me // RING) % RING]
     place = place_y * RING + place_x
     row_of = place * block_rows + side_of * share + slot_of % share
-    chosen = jnp.take(every, jnp.where(is_live, row_of, 0), axis=0)
-    chosen = jnp.where(is_live[:, None], chosen, jnp.zeros((), jnp.bfloat16))
+    pick = (row_of[:, None] == jnp.arange(every.shape[0])[None, :]) & is_live[:, None]
+    chosen = jnp.einsum(
+        "pr,rc->pc", pick.astype(jnp.bfloat16), every, preferred_element_type=jnp.float32
+    ).astype(jnp.bfloat16)
     chosen = chosen.reshape(pieces, PROJ, band_count)
     spread = jnp.einsum("pjk,pjn->pnk", proj_local, chosen, preferred_element_type=jnp.float32)
     result = scatter_blocks(index_block, spread, block_count)

time: 293 us -> 287 us (0.980)
  local copies, waits for them, and re-layouts: 57.7 us -> 48.1 us
  waiting for transfers between devices: 109 us -> 113 us
    gather x2 -> x0, local copies, waits for them, and re-layouts: 4.84 us -> none  [body(): chosen = jnp.take(every, jnp.where(is_live, row_of, 0), axis=0)]
    unnamed x15, local copies, waits for them, and re-layouts: 8.25 us -> 4.21 us
    ppermute x7, waiting for transfers between devices: 19.8 us -> 23.7 us  [step(): return lax.ppermute(cells, 'band', pairs)]
    reshape x0 -> x1, local copies, waits for them, and re-layouts: none -> 3.44 us  [body(): chosen = chosen.reshape(pieces, PROJ, band_count)]
    select_n x1 -> x0, local copies, waits for them, and re-layouts: 3.44 us -> none  [body(): chosen = jnp.where(is_live[:, None], chosen, jnp.zeros((), jnp.bfloat16))]
  transfers between devices with their start and end apart: 13 -> 13, of which waited for: 9 -> 9; matrix products, arithmetic and copies ran while one was open for 4% -> 2% of each run, Pallas kernels for 0% -> 0%
where the time goes in v11:
time: 287 us; the launch traced here: 285 us
  waiting for transfers between devices  113 us (39%)
  blocking collectives  52 us (18%)
  local copies, waits for them, and re-layouts  48.1 us (17%)
  starting transfers between devices  24.6 us (9%)
  matrix products  22.4 us (8%)
  Pallas kernels  14.6 us (5%)
  other arithmetic  10.5 us (4%)
    all_to_all x1, waiting for transfers between devices, body(): lax.all_to_all(orbitals, 'band', split_axis=1, concat_axis=0, tiled=True)  62.6 us
    all_to_all x1, blocking collectives, body(): lax.all_to_all(result, 'band', split_axis=0, concat_axis=1, tiled=True)  52 us
    ppermute x7, waiting for transfers between devices, step(): return lax.ppermute(cells, 'band', pairs)  23.7 us
    pallas_call x1, Pallas kernels, scatter_blocks(): pl.pallas_call(_scatter_body, out_shape=jax.ShapeDtypeStruct((bands, bloc...  14.6 us
    all_to_all x1, waiting for transfers between devices, body(): lax.all_to_all(own_total.reshape(band_size, share, -1), 'band', split_axi...  13.4 us
    ppermute x4, waiting for transfers between devices, shift(): lax.ppermute(cells, axis, [(i, (i + step) % count) for i in range(count)])  13.1 us
    reshape x1, local copies, waits for them, and re-layouts, body(): blocks = slab_waves.reshape(band_count, -1, BLOCK)  11.4 us
    all_to_all x1, local copies, waits for them, and re-layouts, body(): lax.all_to_all(result, 'band', split_axis=0, concat_axis=1, tiled=True)  10.5 us
  transfers between devices with their start and end apart: 13, of which 9 were waited for; matrix products, arithmetic and copies ran while one was open for 2% of the time, Pallas kernels for 0%

profile of v11, /device:TPU:96, one launch (start us, length us, event | category | flops | bytes accessed | tf_op | source)
XLA Modules:
  0.0 285.3 jit_solution(2935484178497758349)
XLA Ops:
  0.0 0.0 copy-start
  0.0 0.0 copy-start.3
  0.0 7.2 %all-to-all-start = ((bf16[2,16,65536]{2,0,1:T(2,128)(2,1)}), bf16[2,16,65536]{2,0,1:T(2,128)(2,1)}, u32[]{:S(2)}, u32[]{:S(2)}) async-start(bf16[2,16,65536]{2,0,1:T(2,128)(2,1)} %bitcast.41), calls=%async_computation | async-start | bytes 8388608 | tf_op jit(solution)/shard_map/all_to_all | solution.py:71
  7.3 0.0 copy-done.3
  7.3 0.7 fusion.38
  7.9 62.6 %all-to-all-done = bf16[2,16,65536]{2,0,1:T(2,128)(2,1)} async-done(((bf16[2,16,65536]{2,0,1:T(2,128)(2,1)}), bf16[2,16,65536]{2,0,1:T(2,128)(2,1)}, u32[]{:S(2)}, u32[]{:S(2)}) %all-to-all-start) | async-done | bytes 4194336 | tf_op jit(solution)/shard_map/all_to_all | solution.py:71
  70.5 0.0 copy-start.2
  70.5 11.4 %reshape.306 = bf16[32,512,128]{2,1,0:T(8,128)(2,1)} reshape(bf16[16,2,65536]{2,1,0:T(2,128)(2,1)} %bitcast.8) | data formatting | bytes 8388608 | tf_op jit(solution)/shard_map/reshape | solution.py:73
  81.9 0.0 copy-done.2
  81.9 4.6 %convert_bitcast_fusion = bf16[32,512,128]{2,1,0:T(8,128)(2,1)S(1)} fusion(bf16[32,512,128]{2,1,0:T(8,128)(2,1)} %reshape.306, s32[512]{0:T(512)S(1)} %bitcast.37), kind=kOutput, calls=%fused_computation.3 | convolution fusion | flops 2149842944 | bytes 8390656 | tf_op jit(solution)/shard_map/pb,nbk->npk/dot_general | solution.py:82
  86.5 0.0 copy-done
  86.5 7.3 %fusion.5 = f32[512,18,32]{2,1,0:T(8,128)} fusion(bf16[512,18,128]{2,0,1:T(8,128)(2,1)S(1)} %bitcast.35, bf16[32,512,128]{2,1,0:T(8,128)(2,1)S(1)} %convert_bitcast_fusion), kind=kOutput, calls=%fused_computation.7 | convolution fusion | flops 75497472 | bytes 7733248 | tf_op jit(solution)/shard_map/pjk,npk->pjn/dot_general | solution.py:85
  93.8 4.5 %copy.32 = f32[512,18,32]{0,2,1:T(8,128)S(1)} copy(f32[512,18,32]{2,1,0:T(8,128)} %fusion.5) | data formatting | bytes 2359296 | tf_op jit(solution)/shard_map/pjk,npk->pjn/dot_general | solution.py:85
  98.2 1.5 copy.33
  99.7 6.4 %scatter_custom_fusion = f32[1153,576]{1,0:T(8,128)} fusion(s32[512]{0:T(512)S(1)} %bitcast.47, f32[512,576]{1,0:T(8,128)} %copy.33, f32[]{:T(128)} %constant.94.clone.1), kind=kCustom, calls=%fused_computation.11 | custom fusion | flops 294912 | bytes 2657024 | tf_op jit(solution)/shard_map/scatter-add | solution.py:87
  106.1 2.6 fusion.39
  108.7 2.5 copy.36
  111.2 0.0 collective-permute-start.1
  111.2 1.2 copy.34
  112.4 1.7 collective-permute-start
  114.2 9.8 %collective-permute-done.1 = f32[384,576]{0,1:T(8,128)} collective-permute-done((f32[384,576]{0,1:T(8,128)}, f32[384,576]{0,1:T(8,128)}, u32[]{:S(2)}, u32[]{:S(2)}) %collective-permute-start.1) | collective-permute-done | bytes 884768 | tf_op jit(solution)/shard_map/ppermute | solution.py:14
  124.0 1.5 copy.37
  125.5 0.0 collective-permute-done
  125.5 2.5 copy.35
  127.9 2.7 fusion.22
  130.6 4.7 %all-to-all-start.1 = ((f32[16,24,576]{2,1,0:T(8,128)}), f32[16,24,576]{2,1,0:T(8,128)S(1)}, u32[]{:S(2)}, u32[]{:S(2)}) async-start(f32[16,24,576]{2,1,0:T(8,128)} %bitcast.42), calls=%async_computation.1 | async-start | bytes 1966080 | tf_op jit(solution)/shard_map/all_to_all | solution.py:98
  135.3 1.1 constant_dynamic-slice_fusion
  136.4 0.1 copy.28
  136.5 0.9 reshape.305
  137.3 13.4 %all-to-all-done.1 = f32[16,24,576]{2,1,0:T(8,128)S(1)} async-done(((f32[16,24,576]{2,1,0:T(8,128)}), f32[16,24,576]{2,1,0:T(8,128)S(1)}, u32[]{:S(2)}, u32[]{:S(2)}) %all-to-all-start.1) | async-done | bytes 884768 | tf_op jit(solution)/shard_map/all_to_all | solution.py:98
  150.7 0.1 reduce_sum.9
  150.8 0.1 reshape.309
  150.9 1.6 convolution_convert_fusion
  152.5 0.1 reshape.310
  152.6 3.1 %collective-permute-start.3 = (bf16[24,576]{1,0:T(8,128)(2,1)S(1)}, bf16[24,576]{1,0:T(8,128)(2,1)S(1)}, u32[]{:S(2)}, u32[]{:S(2)}) collective-permute-start(bf16[24,576]{1,0:T(8,128)(2,1)S(1)} %reshape.310), channel_id=1, source_target_pairs={{0,15},{1,0},{2,1},{3,2},{4,3},{5,4},{6,5},{7,6},{8,7},{9,8},{10,9... | collective-permute-start | bytes 82952 | tf_op jit(solution)/shard_map/ppermute | solution.py:14
  155.7 0.0 collective-permute-start.2
  155.7 1.6 collective-permute-done.3
  157.3 1.7 collective-permute-done.2
  159.0 0.1 collective-permute-start.4
  159.1 3.3 %collective-permute-start.5 = (bf16[80,576]{1,0:T(8,128)(2,1)S(1)}, bf16[80,576]{1,0:T(8,128)(2,1)S(1)}, u32[]{:S(2)}, u32[]{:S(2)}) collective-permute-start(bf16[80,576]{1,0:T(8,128)(2,1)S(1)} %get-tuple-element.9), channel_id=1, source_target_pairs={{0,48},{16,0},{32,16},{48,32},{64,112},{80,64},{96,80},{112,96},{1... | collective-permute-start | bytes 276488 | tf_op jit(solution)/shard_map/ppermute | solution.py:27
  162.4 3.6 %collective-permute-done.4 = bf16[80,576]{1,0:T(8,128)(2,1)S(1)} collective-permute-done((bf16[80,576]{1,0:T(8,128)(2,1)S(1)}, bf16[80,576]{1,0:T(8,128)(2,1)S(1)}, u32[]{:S(2)}, u32[]{:S(2)}) %collective-permute-start.4) | collective-permute-done | bytes 92192 | tf_op jit(solution)/shard_map/ppermute | solution.py:27
  166.0 0.0 collective-permute-start.6
  166.0 0.0 collective-permute-done.5
  166.1 6.0 %collective-permute-done.6 = bf16[80,576]{1,0:T(8,128)(2,1)S(1)} collective-permute-done((bf16[80,576]{1,0:T(8,128)(2,1)S(1)}, bf16[80,576]{1,0:T(8,128)(2,1)S(1)}, u32[]{:S(2)}, u32[]{:S(2)}) %collective-permute-start.6) | collective-permute-done | bytes 92192 | tf_op jit(solution)/shard_map/ppermute | solution.py:27
  172.1 0.4 collective-permute-start.8
  172.5 1.7 collective-permute-start.7
  174.2 0.7 fusion.32
  175.0 7.8 %collective-permute-done.8 = bf16[320,576]{1,0:T(8,128)(2,1)S(1)} collective-permute-done((bf16[320,576]{1,0:T(8,128)(2,1)S(1)}, bf16[320,576]{1,0:T(8,128)(2,1)S(1)}, u32[]{:S(2)}, u32[]{:S(2)}) %collective-permute-start.8) | collective-permute-done | bytes 368672 | tf_op jit(solution)/shard_map/ppermute | solution.py:27
  182.8 1.6 collective-permute-start.10
  184.4 0.0 collective-permute-done.7
  184.4 0.8 collective-permute-start.9
  185.2 0.1 constant_dynamic-update-slice_fusion.3
  185.3 0.1 constant_dynamic-update-slice_fusion.2
  185.3 6.3 %collective-permute-done.9 = bf16[160,576]{1,0:T(8,128)(2,1)S(1)} collective-permute-done((bf16[160,576]{1,0:T(8,128)(2,1)S(1)}, bf16[160,576]{1,0:T(8,128)(2,1)S(1)}, u32[]{:S(2)}, u32[]{:S(2)}) %collective-permute-start.9) | collective-permute-done | bytes 184352 | tf_op jit(solution)/shard_map/ppermute | solution.py:27
  191.7 0.0 collective-permute-done.10
  191.7 1.2 fusion.15
  193.0 3.4 %copy.38 = bf16[512,18,32]{2,1,0:T(8,128)(2,1)} copy(bf16[512,18,32]{0,2,1:T(8,128)(2,1)S(1)} %bitcast.43) | data formatting | bytes 1179648 | tf_op jit(solution)/shard_map/reshape | solution.py:128
  196.4 7.8 %fusion.2.spread_ref = f32[512,32,128]{2,1,0:T(8,128)} fusion(bf16[512,18,32]{2,1,0:T(8,128)(2,1)} %copy.38, bf16[512,18,128]{2,0,1:T(8,128)(2,1)S(1)} %bitcast.36), kind=kOutput, calls=%fused_computation.4 | convolution fusion | flops 75497472 | bytes 11337728 | tf_op jit(solution)/shard_map/pjk,pjn->pnk/dot_general | solution.py:129
  204.2 14.6 %shard_map.64 = bf16[32,512,128]{2,1,0:T(8,128)(2,1)S(1)} custom-call(s32[512]{0:T(512)S(1)} %bitcast.38, f32[512,32,128]{2,1,0:T(8,128)} %fusion.2.spread_ref), custom_call_target="tpu_custom_call" | custom-call | tf_op jit(solution)/shard_map/pallas_call | solution.py:57
  218.8 0.0 copy-start.1
  218.8 2.0 copy-done.1
  220.8 10.5 %all_to_all.33 = bf16[16,2,65536]{2,1,0:T(2,128)(2,1)} reshape(bf16[32,512,128]{2,1,0:T(8,128)(2,1)} %copy-done.1) | data formatting | bytes 8388608 | tf_op jit(solution)/shard_map/all_to_all | solution.py:132
  231.3 52.0 %all_to_all.40 = bf16[16,2,65536]{2,1,0:T(2,128)(2,1)S(1)} all-to-all(bf16[16,2,65536]{2,1,0:T(2,128)(2,1)} %all_to_all.33), channel_id=1, replica_groups=mesh['band'=16,'slab'=16] {'band'}, dimensions={0} | all-to-all | bytes 8388608 | tf_op jit(solution)/shard_map/all_to_all | solution.py:132
  283.3 2.0 copy.59
  (11 shorter events, 0.2 us)
Async XLA Ops:
  0.0 86.5 %copy-start = (bf16[1,1,512,18,128]{4,2,3,1,0:T(8,128)(2,1)S(1)}, bf16[1,1,512,18,128]{4,2,3,1,0:T(8,128)(2,1)}, u32[]{:S(2)}) copy-start(bf16[1,1,512,18,128]{4,2,3,1,0:T(8,128)(2,1)} %param.7) | copy-start | bytes 7077892
  0.0 7.3 %copy-start.3 = (s32[1,1,512]{2,1,0:T(1,128)S(1)}, s32[1,1,512]{2,1,0:T(1,128)}, u32[]{:S(2)}) copy-start(s32[1,1,512]{2,1,0:T(1,128)} %param.9) | copy-start | bytes 6148
  0.0 70.5 %all-to-all-start = ((bf16[2,16,65536]{2,0,1:T(2,128)(2,1)}), bf16[2,16,65536]{2,0,1:T(2,128)(2,1)}, u32[]{:S(2)}, u32[]{:S(2)}) async-start(bf16[2,16,65536]{2,0,1:T(2,128)(2,1)} %bitcast.41), calls=%async_computation | async-start | bytes 8388608 | tf_op jit(solution)/shard_map/all_to_all | solution.py:71
  70.5 11.4 %copy-start.2 = (s32[1,1,512]{2,1,0:T(1,128)S(1)}, s32[1,1,512]{2,1,0:T(1,128)}, u32[]{:S(2)}) copy-start(s32[1,1,512]{2,1,0:T(1,128)} %param.8) | copy-start | bytes 6148
  111.2 12.8 %collective-permute-start.1 = (f32[384,576]{0,1:T(8,128)}, f32[384,576]{0,1:T(8,128)}, u32[]{:S(2)}, u32[]{:S(2)}) collective-permute-start(f32[384,576]{0,1:T(8,128)} %copy.36), channel_id=1, source_target_pairs={{0,1},{1,2},{2,3},{3,4},{4,5},{5,6},{6,7},{7,8},{8,9},{9,10},{10,1... | collective-permute-start | bytes 2654216 | tf_op jit(solution)/shard_map/ppermute | solution.py:14
  112.4 13.0 %collective-permute-start = (f32[384,576]{0,1:T(8,128)}, f32[384,576]{0,1:T(8,128)}, u32[]{:S(2)}, u32[]{:S(2)}) collective-permute-start(f32[384,576]{0,1:T(8,128)} %copy.34), channel_id=1, source_target_pairs={{0,15},{1,0},{2,1},{3,2},{4,3},{5,4},{6,5},{7,6},{8,7},{9,8},{10,9... | collective-permute-start | bytes 2654216 | tf_op jit(solution)/shard_map/ppermute | solution.py:14
  130.6 20.1 %all-to-all-start.1 = ((f32[16,24,576]{2,1,0:T(8,128)}), f32[16,24,576]{2,1,0:T(8,128)S(1)}, u32[]{:S(2)}, u32[]{:S(2)}) async-start(f32[16,24,576]{2,1,0:T(8,128)} %bitcast.42), calls=%async_computation.1 | async-start | bytes 1966080 | tf_op jit(solution)/shard_map/all_to_all | solution.py:98
  152.6 4.6 %collective-permute-start.3 = (bf16[24,576]{1,0:T(8,128)(2,1)S(1)}, bf16[24,576]{1,0:T(8,128)(2,1)S(1)}, u32[]{:S(2)}, u32[]{:S(2)}) collective-permute-start(bf16[24,576]{1,0:T(8,128)(2,1)S(1)} %reshape.310), channel_id=1, source_target_pairs={{0,15},{1,0},{2,1},{3,2},{4,3},{5,4},{6,5},{7,6},{8,7},{9,8},{10,9... | collective-permute-start | bytes 82952 | tf_op jit(solution)/shard_map/ppermute | solution.py:14
  155.7 3.3 %collective-permute-start.2 = (bf16[24,576]{1,0:T(8,128)(2,1)S(1)}, bf16[24,576]{1,0:T(8,128)(2,1)S(1)}, u32[]{:S(2)}, u32[]{:S(2)}) collective-permute-start(bf16[24,576]{1,0:T(8,128)(2,1)S(1)} %reshape.310), channel_id=1, source_target_pairs={{0,1},{1,2},{2,3},{3,4},{4,5},{5,6},{6,7},{7,8},{8,9},{9,10},{10,1... | collective-permute-start | bytes 82952 | tf_op jit(solution)/shard_map/ppermute | solution.py:14
  159.0 7.0 %collective-permute-start.4 = (bf16[80,576]{1,0:T(8,128)(2,1)S(1)}, bf16[80,576]{1,0:T(8,128)(2,1)S(1)}, u32[]{:S(2)}, u32[]{:S(2)}) collective-permute-start(bf16[80,576]{1,0:T(8,128)(2,1)S(1)} %get-tuple-element.9), channel_id=1, source_target_pairs={{0,16},{16,32},{32,48},{48,0},{64,80},{80,96},{96,112},{112,64},{1... | collective-permute-start | bytes 276488 | tf_op jit(solution)/shard_map/ppermute | solution.py:27
  159.1 6.9 %collective-permute-start.5 = (bf16[80,576]{1,0:T(8,128)(2,1)S(1)}, bf16[80,576]{1,0:T(8,128)(2,1)S(1)}, u32[]{:S(2)}, u32[]{:S(2)}) collective-permute-start(bf16[80,576]{1,0:T(8,128)(2,1)S(1)} %get-tuple-element.9), channel_id=1, source_target_pairs={{0,48},{16,0},{32,16},{48,32},{64,112},{80,64},{96,80},{112,96},{1... | collective-permute-start | bytes 276488 | tf_op jit(solution)/shard_map/ppermute | solution.py:27
  166.0 6.1 %collective-permute-start.6 = (bf16[80,576]{1,0:T(8,128)(2,1)S(1)}, bf16[80,576]{1,0:T(8,128)(2,1)S(1)}, u32[]{:S(2)}, u32[]{:S(2)}) collective-permute-start(bf16[80,576]{1,0:T(8,128)(2,1)S(1)} %collective-permute-done.4), channel_id=1, source_target_pairs={{0,16},{16,32},{32,48},{48,0},{64,80},{80,96},{96,112},{112,64},{1... | collective-permute-start | bytes 276488 | tf_op jit(solution)/shard_map/ppermute | solution.py:27
  172.1 10.7 %collective-permute-start.8 = (bf16[320,576]{1,0:T(8,128)(2,1)S(1)}, bf16[320,576]{1,0:T(8,128)(2,1)S(1)}, u32[]{:S(2)}, u32[]{:S(2)}) collective-permute-start(bf16[320,576]{1,0:T(8,128)(2,1)S(1)} %pad_maximum_fusion), channel_id=1, source_target_pairs={{0,192},{16,208},{32,224},{48,240},{64,0},{80,16},{96,32},{112,48}... | collective-permute-start | bytes 1105928 | tf_op jit(solution)/shard_map/ppermute | solution.py:27
  172.5 11.9 %collective-permute-start.7 = (bf16[320,576]{1,0:T(8,128)(2,1)S(1)}, bf16[320,576]{1,0:T(8,128)(2,1)S(1)}, u32[]{:S(2)}, u32[]{:S(2)}) collective-permute-start(bf16[320,576]{1,0:T(8,128)(2,1)S(1)} %pad_maximum_fusion), channel_id=1, source_target_pairs={{0,64},{16,80},{32,96},{48,112},{64,128},{80,144},{96,160},{112,17... | collective-permute-start | bytes 1105928 | tf_op jit(solution)/shard_map/ppermute | solution.py:27
  182.8 8.9 %collective-permute-start.10 = (bf16[160,576]{1,0:T(8,128)(2,1)S(1)}, bf16[160,576]{1,0:T(8,128)(2,1)S(1)}, u32[]{:S(2)}, u32[]{:S(2)}) collective-permute-start(bf16[160,576]{1,0:T(8,128)(2,1)S(1)} %slice.41), channel_id=1, source_target_pairs={{0,192},{16,208},{32,224},{48,240},{64,0},{80,16},{96,32},{112,48}... | collective-permute-start | bytes 552968 | tf_op jit(solution)/shard_map/ppermute | solution.py:27
  184.4 7.3 %collective-permute-start.9 = (bf16[160,576]{1,0:T(8,128)(2,1)S(1)}, bf16[160,576]{1,0:T(8,128)(2,1)S(1)}, u32[]{:S(2)}, u32[]{:S(2)}) collective-permute-start(bf16[160,576]{1,0:T(8,128)(2,1)S(1)} %slice.40), channel_id=1, source_target_pairs={{0,64},{16,80},{32,96},{48,112},{64,128},{80,144},{96,160},{112,17... | collective-permute-start | bytes 552968 | tf_op jit(solution)/shard_map/ppermute | solution.py:27
  218.8 2.0 copy-start.1

commit v12 on v11

--- a/solution.py
+++ b/solution.py
@@ -84,8 +84,9 @@
     ).astype(jnp.bfloat16)
     projected = jnp.einsum("pjk,npk->pjn", proj_local, picked, preferred_element_type=jnp.float32)
     target = jnp.where(is_live, index_atom, 3 * slot_count)
-    partial_value = jax.ops.segment_sum(
-        projected.reshape(pieces, -1), target, num_segments=3 * slot_count + 1
+    gather_atom = (jnp.arange(3 * slot_count)[:, None] == target[None, :]).astype(jnp.float32)
+    partial_value = jnp.einsum(
+        "ap,pc->ac", gather_atom, projected.reshape(pieces, -1), precision=lax.Precision.HIGHEST
     )
     partial_value = partial_value[: 3 * slot_count].reshape(3, slot_count, -1)
     own_total = (

time: 287 us -> 273 us (0.951)
  local copies, waits for them, and re-layouts: 48.1 us -> 37.7 us
  other arithmetic: 10.5 us -> 0.92 us
  waiting for transfers between devices: 113 us -> 120 us
  starting transfers between devices: 24.6 us -> 21 us
    scatter-add x1 -> x0, other arithmetic: 6.36 us -> none  [body(): jax.ops.segment_sum(projected.reshape(pieces, -1), target, num_segments=3...]
    all_to_all x1, waiting for transfers between devices: 13.4 us -> 17.9 us  [body(): lax.all_to_all(own_total.reshape(band_size, share, -1), 'band', split_axi...]
    ppermute x2 -> x0, local copies, waits for them, and re-layouts: 3.95 us -> none  [shift(): lax.ppermute(cells, axis, [(i, (i + step) % count) for i in range(count)])]
    ppermute x4, starting transfers between devices: 4.81 us -> 1.03 us  [shift(): lax.ppermute(cells, axis, [(i, (i + step) % count) for i in range(count)])]
    slice x2 -> x1, local copies, waits for them, and re-layouts: 3.82 us -> 0.12 us  [body(): partial_value[0]]
  transfers between devices with their start and end apart: 13 -> 13, of which waited for: 9 -> 10; matrix products, arithmetic and copies ran while one was open for 2% -> 1% of each run, Pallas kernels for 0% -> 0%
where the time goes in v12:
time: 273 us; the launch traced here: 272 us
  waiting for transfers between devices  120 us (44%)
  blocking collectives  52.1 us (19%)
  local copies, waits for them, and re-layouts  37.7 us (14%)
  matrix products  25.1 us (9%)
  starting transfers between devices  21 us (8%)
  Pallas kernels  14.6 us (5%)
    all_to_all x1, waiting for transfers between devices, body(): lax.all_to_all(orbitals, 'band', split_axis=1, concat_axis=0, tiled=True)  62.6 us
    all_to_all x1, blocking collectives, body(): lax.all_to_all(result, 'band', split_axis=0, concat_axis=1, tiled=True)  52.1 us
    ppermute x7, waiting for transfers between devices, step(): return lax.ppermute(cells, 'band', pairs)  25 us
    all_to_all x1, waiting for transfers between devices, body(): lax.all_to_all(own_total.reshape(band_size, share, -1), 'band', split_axi...  17.9 us
    ppermute x4, waiting for transfers between devices, shift(): lax.ppermute(cells, axis, [(i, (i + step) % count) for i in range(count)])  14.8 us
    pallas_call x1, Pallas kernels, scatter_blocks(): pl.pallas_call(_scatter_body, out_shape=jax.ShapeDtypeStruct((bands, bloc...  14.6 us
    reshape x1, local copies, waits for them, and re-layouts, body(): blocks = slab_waves.reshape(band_count, -1, BLOCK)  11.4 us
    all_to_all x1, local copies, waits for them, and re-layouts, body(): lax.all_to_all(result, 'band', split_axis=0, concat_axis=1, tiled=True)  10.5 us
  transfers between devices with their start and end apart: 13, of which 10 were waited for; matrix products, arithmetic and copies ran while one was open for 1% of the time, Pallas kernels for 0%

profile of v12, /device:TPU:96, one launch (start us, length us, event | category | flops | bytes accessed | tf_op | source)
XLA Modules:
  0.0 271.9 jit_solution(13624795890947084902)
XLA Ops:
  0.0 0.0 copy-start
  0.0 0.0 copy-start.3
  0.0 7.2 %all-to-all-start = ((bf16[2,16,65536]{2,0,1:T(2,128)(2,1)}), bf16[2,16,65536]{2,0,1:T(2,128)(2,1)}, u32[]{:S(2)}, u32[]{:S(2)}) async-start(bf16[2,16,65536]{2,0,1:T(2,128)(2,1)} %bitcast.40), calls=%async_computation | async-start | bytes 8388608 | tf_op jit(solution)/shard_map/all_to_all | solution.py:71
  7.3 0.0 copy-done.3
  7.3 0.1 fusion.38
  7.3 0.6 fusion.33
  7.9 62.6 %all-to-all-done = bf16[2,16,65536]{2,0,1:T(2,128)(2,1)} async-done(((bf16[2,16,65536]{2,0,1:T(2,128)(2,1)}), bf16[2,16,65536]{2,0,1:T(2,128)(2,1)}, u32[]{:S(2)}, u32[]{:S(2)}) %all-to-all-start) | async-done | bytes 4194336 | tf_op jit(solution)/shard_map/all_to_all | solution.py:71
  70.5 0.0 copy-start.2
  70.5 11.4 %reshape.291 = bf16[32,512,128]{2,1,0:T(8,128)(2,1)} reshape(bf16[16,2,65536]{2,1,0:T(2,128)(2,1)} %bitcast.6) | data formatting | bytes 8388608 | tf_op jit(solution)/shard_map/reshape | solution.py:73
  81.9 0.0 copy-done.2
  81.9 4.6 %fusion.22 = bf16[512,32,128]{2,0,1:T(8,128)(2,1)S(1)} fusion(bf16[32,512,128]{2,1,0:T(8,128)(2,1)} %reshape.291, s32[512]{0:T(512)S(1)} %bitcast.36), kind=kOutput, calls=%fused_computation.19 | convolution fusion | flops 2147745792 | bytes 8390656 | tf_op jit(solution)/shard_map/pb,nbk->npk/dot_general | solution.py:82
  86.5 0.0 copy-done
  86.5 7.3 %fusion.6 = f32[512,18,32]{2,1,0:T(8,128)} fusion(bf16[512,18,128]{2,0,1:T(8,128)(2,1)S(1)} %bitcast.34, bf16[512,32,128]{2,0,1:T(8,128)(2,1)S(1)} %fusion.22), kind=kOutput, calls=%fused_computation.6 | convolution fusion | flops 75497472 | bytes 7733248 | tf_op jit(solution)/shard_map/pjk,npk->pjn/dot_general | solution.py:85
  93.8 4.5 %copy.15 = f32[512,18,32]{0,2,1:T(8,128)S(1)} copy(f32[512,18,32]{2,1,0:T(8,128)} %fusion.6) | data formatting | bytes 2359296 | tf_op jit(solution)/shard_map/pjk,npk->pjn/dot_general | solution.py:85
  98.3 2.6 fusion.14
  100.9 0.1 fusion.40
  101.0 0.0 collective-permute-start
  101.1 0.5 collective-permute-start.1
  101.6 10.1 %collective-permute-done = f32[384,576]{0,1:T(8,128)S(1)} collective-permute-done((f32[384,576]{0,1:T(8,128)S(1)}, f32[384,576]{0,1:T(8,128)S(1)}, u32[]{:S(2)}, u32[]{:S(2)}) %collective-permute-start) | collective-permute-done | bytes 884768 | tf_op jit(solution)/shard_map/ppermute | solution.py:14
  111.6 1.9 collective-permute-done.1
  113.5 0.1 fusion.24
  113.7 1.3 copy.16
  114.9 4.7 %all-to-all-start.1 = ((f32[16,24,576]{2,1,0:T(8,128)}), f32[16,24,576]{2,1,0:T(8,128)S(1)}, u32[]{:S(2)}, u32[]{:S(2)}) async-start(f32[16,24,576]{2,1,0:T(8,128)} %bitcast.11), calls=%async_computation.1 | async-start | bytes 1966080 | tf_op jit(solution)/shard_map/all_to_all | solution.py:99
  119.6 1.1 constant_dynamic-slice_fusion
  120.7 0.1 copy.12
  120.8 0.9 reshape.290
  121.7 17.9 %all-to-all-done.1 = f32[16,24,576]{2,1,0:T(8,128)S(1)} async-done(((f32[16,24,576]{2,1,0:T(8,128)}), f32[16,24,576]{2,1,0:T(8,128)S(1)}, u32[]{:S(2)}, u32[]{:S(2)}) %all-to-all-start.1) | async-done | bytes 884768 | tf_op jit(solution)/shard_map/all_to_all | solution.py:99
  139.5 0.1 reduce_sum.9
  139.6 0.1 reshape.294
  139.7 1.6 convolution_convert_fusion
  141.3 0.1 reshape.295
  141.4 0.0 collective-permute-start.3
  141.5 0.5 collective-permute-start.2
  142.0 1.1 collective-permute-done.3
  143.0 1.8 collective-permute-done.2
  144.8 0.0 copy-start.4
  144.8 0.1 collective-permute-start.4
  144.9 3.2 %collective-permute-start.5 = (bf16[80,576]{1,0:T(8,128)(2,1)S(1)}, bf16[80,576]{1,0:T(8,128)(2,1)S(1)}, u32[]{:S(2)}, u32[]{:S(2)}) collective-permute-start(bf16[80,576]{1,0:T(8,128)(2,1)S(1)} %get-tuple-element.7), channel_id=1, source_target_pairs={{0,48},{16,0},{32,16},{48,32},{64,112},{80,64},{96,80},{112,96},{1... | collective-permute-start | bytes 276488 | tf_op jit(solution)/shard_map/ppermute | solution.py:27
  148.1 3.4 %collective-permute-done.4 = bf16[80,576]{1,0:T(8,128)(2,1)S(1)} collective-permute-done((bf16[80,576]{1,0:T(8,128)(2,1)S(1)}, bf16[80,576]{1,0:T(8,128)(2,1)S(1)}, u32[]{:S(2)}, u32[]{:S(2)}) %collective-permute-start.4) | collective-permute-done | bytes 92192 | tf_op jit(solution)/shard_map/ppermute | solution.py:27
  151.5 0.0 collective-permute-start.6
  151.5 0.0 collective-permute-done.5
  151.5 6.1 %collective-permute-done.6 = bf16[80,576]{1,0:T(8,128)(2,1)S(1)} collective-permute-done((bf16[80,576]{1,0:T(8,128)(2,1)S(1)}, bf16[80,576]{1,0:T(8,128)(2,1)S(1)}, u32[]{:S(2)}, u32[]{:S(2)}) %collective-permute-start.6) | collective-permute-done | bytes 92192 | tf_op jit(solution)/shard_map/ppermute | solution.py:27
  157.7 1.4 collective-permute-start.8
  159.1 0.7 collective-permute-start.7
  159.9 8.6 %collective-permute-done.8 = bf16[320,576]{1,0:T(8,128)(2,1)S(1)} collective-permute-done((bf16[320,576]{1,0:T(8,128)(2,1)S(1)}, bf16[320,576]{1,0:T(8,128)(2,1)S(1)}, u32[]{:S(2)}, u32[]{:S(2)}) %collective-permute-start.8) | collective-permute-done | bytes 368672 | tf_op jit(solution)/shard_map/ppermute | solution.py:27
  168.5 2.6 collective-permute-start.10
  171.1 0.0 collective-permute-done.7
  171.1 0.1 collective-permute-start.9
  171.2 0.1 constant_dynamic-update-slice_fusion.3
  171.2 0.1 constant_dynamic-update-slice_fusion.2
  171.3 6.8 %collective-permute-done.9 = bf16[160,576]{1,0:T(8,128)(2,1)S(1)} collective-permute-done((bf16[160,576]{1,0:T(8,128)(2,1)S(1)}, bf16[160,576]{1,0:T(8,128)(2,1)S(1)}, u32[]{:S(2)}, u32[]{:S(2)}) %collective-permute-start.9) | collective-permute-done | bytes 184352 | tf_op jit(solution)/shard_map/ppermute | solution.py:27
  178.2 0.0 collective-permute-done.10
  178.2 0.0 copy-done.4
  178.2 1.2 fusion.15
  179.4 3.4 %copy.17 = bf16[512,18,32]{2,1,0:T(8,128)(2,1)} copy(bf16[512,18,32]{0,2,1:T(8,128)(2,1)S(1)} %bitcast.41) | data formatting | bytes 1179648 | tf_op jit(solution)/shard_map/reshape | solution.py:129
  182.9 7.8 %fusion.3.spread_ref = f32[512,32,128]{2,1,0:T(8,128)} fusion(bf16[512,18,32]{2,1,0:T(8,128)(2,1)} %copy.17, bf16[512,18,128]{2,0,1:T(8,128)(2,1)S(1)} %bitcast.35), kind=kOutput, calls=%fused_computation.3 | convolution fusion | flops 75497472 | bytes 11337728 | tf_op jit(solution)/shard_map/pjk,pjn->pnk/dot_general | solution.py:130
  190.7 14.6 %shard_map.64 = bf16[32,512,128]{2,1,0:T(8,128)(2,1)S(1)} custom-call(s32[512]{0:T(512)S(1)} %bitcast.37, f32[512,32,128]{2,1,0:T(8,128)} %fusion.3.spread_ref), custom_call_target="tpu_custom_call" | custom-call | tf_op jit(solution)/shard_map/pallas_call | solution.py:57
  205.3 0.0 copy-start.1
  205.3 2.0 copy-done.1
  207.3 10.5 %all_to_all.33 = bf16[16,2,65536]{2,1,0:T(2,128)(2,1)} reshape(bf16[32,512,128]{2,1,0:T(8,128)(2,1)} %copy-done.1) | data formatting | bytes 8388608 | tf_op jit(solution)/shard_map/all_to_all | solution.py:133
  217.8 52.1 %all_to_all.40 = bf16[16,2,65536]{2,1,0:T(2,128)(2,1)S(1)} all-to-all(bf16[16,2,65536]{2,1,0:T(2,128)(2,1)} %all_to_all.33), channel_id=1, replica_groups=mesh['band'=16,'slab'=16] {'band'}, dimensions={0} | all-to-all | bytes 8388608 | tf_op jit(solution)/shard_map/all_to_all | solution.py:133
  269.9 2.0 copy.41
  (10 shorter events, 0.2 us)
Async XLA Ops:
  0.0 86.5 %copy-start = (bf16[1,1,512,18,128]{4,2,3,1,0:T(8,128)(2,1)S(1)}, bf16[1,1,512,18,128]{4,2,3,1,0:T(8,128)(2,1)}, u32[]{:S(2)}) copy-start(bf16[1,1,512,18,128]{4,2,3,1,0:T(8,128)(2,1)} %param.7) | copy-start | bytes 7077892
  0.0 7.3 %copy-start.3 = (s32[1,1,512]{2,1,0:T(1,128)S(1)}, s32[1,1,512]{2,1,0:T(1,128)}, u32[]{:S(2)}) copy-start(s32[1,1,512]{2,1,0:T(1,128)} %param.9) | copy-start | bytes 6148
  0.0 70.5 %all-to-all-start = ((bf16[2,16,65536]{2,0,1:T(2,128)(2,1)}), bf16[2,16,65536]{2,0,1:T(2,128)(2,1)}, u32[]{:S(2)}, u32[]{:S(2)}) async-start(bf16[2,16,65536]{2,0,1:T(2,128)(2,1)} %bitcast.40), calls=%async_computation | async-start | bytes 8388608 | tf_op jit(solution)/shard_map/all_to_all | solution.py:71
  70.5 11.4 %copy-start.2 = (s32[1,1,512]{2,1,0:T(1,128)S(1)}, s32[1,1,512]{2,1,0:T(1,128)}, u32[]{:S(2)}) copy-start(s32[1,1,512]{2,1,0:T(1,128)} %param.8) | copy-start | bytes 6148
  101.0 10.6 %collective-permute-start = (f32[384,576]{0,1:T(8,128)S(1)}, f32[384,576]{0,1:T(8,128)S(1)}, u32[]{:S(2)}, u32[]{:S(2)}) collective-permute-start(f32[384,576]{0,1:T(8,128)S(1)} %get-tuple-element.5), channel_id=1, source_target_pairs={{0,15},{1,0},{2,1},{3,2},{4,3},{5,4},{6,5},{7,6},{8,7},{9,8},{10,9... | collective-permute-start | bytes 2654216 | tf_op jit(solution)/shard_map/ppermute | solution.py:14
  101.1 12.5 %collective-permute-start.1 = (f32[384,576]{0,1:T(8,128)S(1)}, f32[384,576]{0,1:T(8,128)S(1)}, u32[]{:S(2)}, u32[]{:S(2)}) collective-permute-start(f32[384,576]{0,1:T(8,128)S(1)} %get-tuple-element.6), channel_id=1, source_target_pairs={{0,1},{1,2},{2,3},{3,4},{4,5},{5,6},{6,7},{7,8},{8,9},{9,10},{10,1... | collective-permute-start | bytes 2654216 | tf_op jit(solution)/shard_map/ppermute | solution.py:14
  114.9 24.6 %all-to-all-start.1 = ((f32[16,24,576]{2,1,0:T(8,128)}), f32[16,24,576]{2,1,0:T(8,128)S(1)}, u32[]{:S(2)}, u32[]{:S(2)}) async-start(f32[16,24,576]{2,1,0:T(8,128)} %bitcast.11), calls=%async_computation.1 | async-start | bytes 1966080 | tf_op jit(solution)/shard_map/all_to_all | solution.py:99
  141.4 1.6 collective-permute-start.3
  141.5 3.3 %collective-permute-start.2 = (bf16[24,576]{1,0:T(8,128)(2,1)S(1)}, bf16[24,576]{1,0:T(8,128)(2,1)S(1)}, u32[]{:S(2)}, u32[]{:S(2)}) collective-permute-start(bf16[24,576]{1,0:T(8,128)(2,1)S(1)} %reshape.295), channel_id=1, source_target_pairs={{0,1},{1,2},{2,3},{3,4},{4,5},{5,6},{6,7},{7,8},{8,9},{9,10},{10,1... | collective-permute-start | bytes 82952 | tf_op jit(solution)/shard_map/ppermute | solution.py:14
  144.8 33.4 %copy-start.4 = (s32[512]{0:T(512)S(1)}, s32[512]{0:T(512)}, u32[]{:S(2)}) copy-start(s32[512]{0:T(512)} %get-tuple-element.9) | copy-start | bytes 6148
  144.8 6.7 %collective-permute-start.4 = (bf16[80,576]{1,0:T(8,128)(2,1)S(1)}, bf16[80,576]{1,0:T(8,128)(2,1)S(1)}, u32[]{:S(2)}, u32[]{:S(2)}) collective-permute-start(bf16[80,576]{1,0:T(8,128)(2,1)S(1)} %get-tuple-element.7), channel_id=1, source_target_pairs={{0,16},{16,32},{32,48},{48,0},{64,80},{80,96},{96,112},{112,64},{1... | collective-permute-start | bytes 276488 | tf_op jit(solution)/shard_map/ppermute | solution.py:27
  144.9 6.6 %collective-permute-start.5 = (bf16[80,576]{1,0:T(8,128)(2,1)S(1)}, bf16[80,576]{1,0:T(8,128)(2,1)S(1)}, u32[]{:S(2)}, u32[]{:S(2)}) collective-permute-start(bf16[80,576]{1,0:T(8,128)(2,1)S(1)} %get-tuple-element.7), channel_id=1, source_target_pairs={{0,48},{16,0},{32,16},{48,32},{64,112},{80,64},{96,80},{112,96},{1... | collective-permute-start | bytes 276488 | tf_op jit(solution)/shard_map/ppermute | solution.py:27
  151.5 6.2 %collective-permute-start.6 = (bf16[80,576]{1,0:T(8,128)(2,1)S(1)}, bf16[80,576]{1,0:T(8,128)(2,1)S(1)}, u32[]{:S(2)}, u32[]{:S(2)}) collective-permute-start(bf16[80,576]{1,0:T(8,128)(2,1)S(1)} %collective-permute-done.4), channel_id=1, source_target_pairs={{0,16},{16,32},{32,48},{48,0},{64,80},{80,96},{96,112},{112,64},{1... | collective-permute-start | bytes 276488 | tf_op jit(solution)/shard_map/ppermute | solution.py:27
  157.7 10.7 %collective-permute-start.8 = (bf16[320,576]{1,0:T(8,128)(2,1)S(1)}, bf16[320,576]{1,0:T(8,128)(2,1)S(1)}, u32[]{:S(2)}, u32[]{:S(2)}) collective-permute-start(bf16[320,576]{1,0:T(8,128)(2,1)S(1)} %pad_maximum_fusion), channel_id=1, source_target_pairs={{0,192},{16,208},{32,224},{48,240},{64,0},{80,16},{96,32},{112,48}... | collective-permute-start | bytes 1105928 | tf_op jit(solution)/shard_map/ppermute | solution.py:27
  159.1 12.0 %collective-permute-start.7 = (bf16[320,576]{1,0:T(8,128)(2,1)S(1)}, bf16[320,576]{1,0:T(8,128)(2,1)S(1)}, u32[]{:S(2)}, u32[]{:S(2)}) collective-permute-start(bf16[320,576]{1,0:T(8,128)(2,1)S(1)} %pad_maximum_fusion), channel_id=1, source_target_pairs={{0,64},{16,80},{32,96},{48,112},{64,128},{80,144},{96,160},{112,17... | collective-permute-start | bytes 1105928 | tf_op jit(solution)/shard_map/ppermute | solution.py:27
  168.5 9.7 %collective-permute-start.10 = (bf16[160,576]{1,0:T(8,128)(2,1)S(1)}, bf16[160,576]{1,0:T(8,128)(2,1)S(1)}, u32[]{:S(2)}, u32[]{:S(2)}) collective-permute-start(bf16[160,576]{1,0:T(8,128)(2,1)S(1)} %slice.37), channel_id=1, source_target_pairs={{0,192},{16,208},{32,224},{48,240},{64,0},{80,16},{96,32},{112,48}... | collective-permute-start | bytes 552968 | tf_op jit(solution)/shard_map/ppermute | solution.py:27
  171.1 7.0 %collective-permute-start.9 = (bf16[160,576]{1,0:T(8,128)(2,1)S(1)}, bf16[160,576]{1,0:T(8,128)(2,1)S(1)}, u32[]{:S(2)}, u32[]{:S(2)}) collective-permute-start(bf16[160,576]{1,0:T(8,128)(2,1)S(1)} %slice.36), channel_id=1, source_target_pairs={{0,64},{16,80},{32,96},{48,112},{64,128},{80,144},{96,160},{112,17... | collective-permute-start | bytes 552968 | tf_op jit(solution)/shard_map/ppermute | solution.py:27
  205.3 2.0 copy-start.1
